TPU v7x, 512 devices: a whole 4x8x8 slice. The times are simulated.
512 devices in a mesh: chan: 128 (over x, z_hi, y), win: 4 (over z_lo, core).
Axes of the slice: x: 4, y: 8, z: 8 (z_hi: 4, z_lo: 2; z = z_hi * 2 + z_lo), core: 2. Of those that a mesh axis runs over, the one named last changes fastest.
Arguments:
- strain: bfloat16 [6144, 4, 1024], P('chan', 'win'), may hold values from -384 to 384
- seg_ids: int32 [6144], replicated, may hold values from 0 to 511, never falling along the last dimension, each value on 1 to 24 neighbouring positions
- dead: int32 [512], replicated, may hold values 0 or 1
- radius: int32 [6144], P('chan'), may hold values from 1 to 8, as said below
Outputs:
- cross_spectra: bfloat16 [4, 2, 6144, 6144], P('win', None, 'chan')
Inputs may be any that keep to these rules, and one draw needn't show every extreme that they name: `seg_ids`: segment numbers never fall along the fiber; a change of segment between neighbouring channels marks a splice. Every segment has 1 to 24 channels, and one has exactly that many. Some channel has radius 8.
All inputs are finite; a program needn't handle non-finite values.
Results may differ from a plain program's by a relative error of at most 0.0023.
Values may be sent and summed in bfloat16 or wider, within the bound.
No kernel may reach another device: no remote copies, remote signals or barrier semaphores. Data moves between devices by JAX's collectives and lax.ppermute only.
A program may use at most 64 MiB of HBM per device.

v0:
```python
import jax
import jax.numpy as jnp
from jax import lax
from jax.sharding import PartitionSpec as P

SAMPLES = 1024
FREQ_BINS = 128
FIRST_BIN = 8
SMOOTH_BINS = 4
MOST_REACH = 8


FLOOR_POWER = 0.01


def with_halo(x, sides, width):
    for axis, dim in sides:
        devices, length = (lax.axis_size(axis), x.shape[dim])
        up = [(i, (i + 1) % devices) for i in range(devices - 1)]
        down = [(j, i) for i, j in up]
        last = lax.slice_in_dim(x, length - width, length, axis=dim)
        initial = lax.slice_in_dim(x, 0, width, axis=dim)
        before = lax.ppermute(last, axis, up)
        after = lax.ppermute(initial, axis, down)
        x = jnp.concatenate([before, x, after], axis=dim)
    return x


def fourier_table():
    sample_ids = jnp.arange(SAMPLES, dtype=jnp.int32)
    bin_ids = FIRST_BIN + jnp.arange(FREQ_BINS, dtype=jnp.int32)
    phase_ids = sample_ids[:, None] * bin_ids[None, :] % SAMPLES
    angles = 2.0 * jnp.pi / SAMPLES * phase_ids.astype(jnp.float32)
    taper = 0.5 - 0.5 * jnp.cos(2.0 * jnp.pi / SAMPLES * (sample_ids.astype(jnp.float32) + 0.5))
    weights = taper[:, None] / jnp.sqrt(jnp.float32(SAMPLES))
    return jnp.concatenate([weights * jnp.cos(angles), -weights * jnp.sin(angles)], axis=1)


def smoothing_table():
    bin_ids = jnp.arange(FREQ_BINS, dtype=jnp.int32)
    nearby = (jnp.abs(bin_ids[:, None] - bin_ids[None, :]) <= SMOOTH_BINS).astype(jnp.float32)
    return nearby / jnp.sum(nearby, axis=0, keepdims=True)


def swapped_parts(flat, windows):
    parts = flat.reshape(flat.shape[:-1] + (windows, 2, -1))
    turned = jnp.stack([-parts[..., 1, :], parts[..., 0, :]], axis=-2)
    return turned.reshape(flat.shape)


def body(strain, seg_ids, dead, radius):
    local_rows = strain.shape[0]
    device = lax.axis_index("chan")
    seg_padded = jnp.pad(seg_ids, (MOST_REACH, MOST_REACH), constant_values=-1)
    near_segs = lax.dynamic_slice_in_dim(
        seg_padded, device * local_rows, local_rows + 2 * MOST_REACH
    )
    segment_ids = jnp.arange(dead.shape[0], dtype=jnp.int32)
    dead_near = jnp.sum(
        jnp.where(near_segs[:, None] == segment_ids[None, :], dead[None, :], 0), axis=1
    )
    alive_near = jnp.where(near_segs >= 0, 1 - dead_near, 0)
    own_segs = near_segs[MOST_REACH : MOST_REACH + local_rows]
    alive_own = alive_near[MOST_REACH : MOST_REACH + local_rows].astype(jnp.float32)
    columns = jnp.arange(local_rows + 2 * MOST_REACH, dtype=jnp.int32)[None, :]
    offsets = columns - (jnp.arange(local_rows, dtype=jnp.int32)[:, None] + MOST_REACH)
    linked = (
        (jnp.abs(offsets) <= radius[:, None])
        & (near_segs[None, :] == own_segs[:, None])
        & (alive_near[None, :] > 0)
    )
    linked_f = linked.astype(jnp.float32)
    counts = jnp.maximum(jnp.sum(linked_f, axis=1), 1.0)
    fourier = fourier_table()
    extended = with_halo(strain, (("chan", 0),), MOST_REACH)
    neighbor_sums = jnp.einsum(
        "cr,rwt->cwt", linked.astype(jnp.bfloat16), extended, preferred_element_type=jnp.float32
    )
    filtered = alive_own[:, None, None] * (
        strain.astype(jnp.float32) - neighbor_sums / counts[:, None, None]
    )
    spectra = jnp.einsum("cwt,tk->cwk", filtered, fourier, precision=lax.Precision.HIGHEST)
    power_bins = spectra[..., :FREQ_BINS] ** 2 + spectra[..., FREQ_BINS:] ** 2
    smoothed = jnp.einsum(
        "cwk,kj->cwj", power_bins, smoothing_table(), precision=lax.Precision.HIGHEST
    )
    inverse_amp = lax.rsqrt(jnp.maximum(smoothed, FLOOR_POWER))
    whitened = spectra * jnp.concatenate([inverse_amp, inverse_amp], axis=-1)
    whitened = whitened.reshape(local_rows, strain.shape[1], 2, FREQ_BINS)
    banded = lax.all_to_all(whitened, "win", split_axis=3, concat_axis=1, tiled=True)
    windows = banded.shape[1]
    spectra_block = banded.reshape(local_rows, -1)
    inverse_count = 1.0 / (spectra_block.shape[1] // 2)
    piece = lax.all_gather(spectra_block, "chan", axis=0, tiled=True)
    operands = jnp.stack([piece, swapped_parts(piece, windows)], axis=0)
    product = jnp.einsum("ik,pjk->pij", spectra_block, operands, precision=lax.Precision.HIGHEST)
    cross_spectra = (product * inverse_count).astype(jnp.bfloat16)
    return cross_spectra[None]


def solution(mesh):
    return jax.shard_map(
        body,
        mesh=mesh,
        in_specs=(P("chan", "win", None), P(), P(), P("chan")),
        out_specs=P("win", None, "chan", None),
        check_vma=False,
    )
```

profile of v0, /device:TPU:1, one launch (start us, length us, event | category | flops | bytes accessed | tf_op | source)
XLA Modules:
  0.0 223.8 jit_solution(514706371481970638)
XLA Ops:
  6.5 0.7 fusion.45
  7.3 4.0 %collective-permute-start = (bf16[8,1,1024]{2,0,1:T(8,128)(2,1)S(1)}, bf16[8,1,1024]{2,0,1:T(8,128)(2,1)S(1)}, u32[]{:S(2)}, u32[]{:S(2)}) collective-permute-start(bf16[8,1,1024]{2,0,1:T(8,128)(2,1)S(1)} %get-tuple-element.9), channel_id=1, source_target_pairs={{0,4},{4,8},{8,12},{12,16},{16,20},{20,24},{24,28},{28,32},{32,36}... | collective-permute-start | bytes 49160 | tf_op jit(solution)/shard_map/ppermute | solution.py:23
  11.3 1.3 collective-permute-start.1
  12.7 0.8 pad_dynamic-slice_fusion
  13.5 0.9 select_reduce_fusion
  14.4 0.8 broadcast_compare_fusion
  15.3 2.1 cosine_multiply_fusion
  17.3 0.8 convert_reduce_fusion.1
  18.3 1.2 fusion.16
  19.5 0.6 fusion.18
  20.1 0.2 fusion.17
  20.3 0.1 copy.19
  20.5 0.2 reshape.78
  20.7 9.7 %all_to_all.15 = f32[4,1,3072]{2,1,0:T(1,128)S(1)} all-to-all(f32[4,1,3072]{2,1,0:T(1,128)S(1)} %reshape.78), channel_id=1, replica_groups=mesh['chan'=128,'win'=4] {'win'}, dimensions={0} | all-to-all | bytes 98304 | tf_op jit(solution)/shard_map/all_to_all | solution.py:90
  30.4 0.5 broadcast.86
  30.9 0.8 reduce
  31.7 0.3 reshape.79
  32.0 0.7 copy.22
  32.7 147.0 %all-gather.2.cloned.1.call-done = f32[6144,256]{1,0:T(8,128)} async-done(((f32[48,256]{1,0:T(8,128)}), f32[6144,256]{1,0:T(8,128)}) %all-gather.2.cloned.1.call-update) | async-done | bytes 6291472 | tf_op jit(solution)/shard_map/all_gather | solution.py:94
  179.8 6.6 %copy.23 = f32[6144,256]{0,1:T(8,128)} copy(f32[6144,256]{1,0:T(8,128)} %all-gather.2.cloned.1.call-done) | data formatting | bytes 12582912 | tf_op jit(solution)/shard_map/all_gather | solution.py:94
  186.3 3.3 %slice_negate_fusion = (f32[6144,4,1,32]{0,3,2,1:T(8,128)S(1)}, f32[6144,4,1,32]{0,3,2,1:T(8,128)S(1)}) fusion(f32[6144,4,2,32]{0,3,2,1:T(8,128)} %bitcast.35), kind=kLoop, calls=%fused_computation.8 | loop fusion | flops 786432 | bytes 12582912 | tf_op jit(solution)/shard_map/neg | solution.py:47
  189.6 3.1 %pad_maximum_fusion = f32[6144,4,2,32]{0,3,2,1:T(8,128)} fusion(f32[6144,4,1,32]{0,3,2,1:T(8,128)S(1)} %get-tuple-element.8, f32[6144,4,1,32]{0,3,2,1:T(8,128)S(1)} %get-tuple-element.7), kind=kLoop, calls=%fused_computation.7 | loop fusion | flops 1572864 | bytes 12582912 | tf_op jit(solution)/shard_map/stack | solution.py:47
  192.7 6.5 %copy.24 = f32[1,6144,256]{2,1,0:T(8,128)} copy(f32[1,6144,256]{1,2,0:T(8,128)} %bitcast.36) | data formatting | bytes 12582912 | tf_op jit(solution)/shard_map/stack;reshape | solution.py:95
  199.2 17.8 %fusion.10 = bf16[1,2,48,6144]{3,2,1,0:T(8,128)(2,1)} fusion(f32[48,256,1]{0,1,2:T(8,128)S(1)} %bitcast.38, f32[1,6144,256]{2,1,0:T(8,128)} %copy.24, f32[1,6144,256]{2,1,0:T(8,128)} %bitcast.34), kind=kOutput, calls=%fused_computation.6 | convolution fusion | flops 1816264704 | bytes 13811712 | tf_op jit(solution)/shard_map/ik,pjk->pij/dot_general | solution.py:96
  (14 shorter events, 0.3 us)
Async XLA Ops:
  6.5 173.2 %all-gather.2.cloned.1.call-start = ((), (), s32[]{:S(2)}) async-start(), calls=%async_computation.1 | async-start | bytes 6340608 | tf_op jit(solution)/shard_map/all_gather | solution.py:94
  7.3 11.0 %collective-permute-start = (bf16[8,1,1024]{2,0,1:T(8,128)(2,1)S(1)}, bf16[8,1,1024]{2,0,1:T(8,128)(2,1)S(1)}, u32[]{:S(2)}, u32[]{:S(2)}) collective-permute-start(bf16[8,1,1024]{2,0,1:T(8,128)(2,1)S(1)} %get-tuple-element.9), channel_id=1, source_target_pairs={{0,4},{4,8},{8,12},{12,16},{16,20},{20,24},{24,28},{28,32},{32,36}... | collective-permute-start | bytes 49160 | tf_op jit(solution)/shard_map/ppermute | solution.py:23
  11.3 7.0 %collective-permute-start.1 = (bf16[8,1,1024]{2,0,1:T(8,128)(2,1)S(1)}, bf16[8,1,1024]{2,0,1:T(8,128)(2,1)S(1)}, u32[]{:S(2)}, u32[]{:S(2)}) collective-permute-start(bf16[8,1,1024]{2,0,1:T(8,128)(2,1)S(1)} %get-tuple-element.10), channel_id=1, source_target_pairs={{4,0},{8,4},{12,8},{16,12},{20,16},{24,20},{28,24},{32,28},{36,32}... | collective-permute-start | bytes 49160 | tf_op jit(solution)/shard_map/ppermute | solution.py:24
Sparse Core Ops, SparseCore 0:
  32.8 146.8 all-gather.1
where the time goes:
time: 224 us
  waiting for transfers between devices  147 us (66%)
  matrix products  19.8 us (9%)
  local copies, waits for them, and re-layouts  16.5 us (7%)
  between operations  13.5 us (6%)
  other arithmetic  11.9 us (5%)
  blocking collectives  9.71 us (4%)
  starting transfers between devices  5.31 us (2%)
    all_gather x1, waiting for transfers between devices, body(): piece = lax.all_gather(spectra_block, 'chan', axis=0, tiled=True)  147 us
    dot_general x1, matrix products, body(): jnp.einsum('ik,pjk->pij', spectra_block, operands, precision=lax.Precisio...  17.8 us
    all_to_all x1, blocking collectives, body(): lax.all_to_all(whitened, 'win', split_axis=3, concat_axis=1, tiled=True)  9.71 us
    all_gather x1, local copies, waits for them, and re-layouts, body(): piece = lax.all_gather(spectra_block, 'chan', axis=0, tiled=True)  6.56 us
    another operation x1, local copies, waits for them, and re-layouts, body(): operands = jnp.stack([piece, swapped_parts(piece, windows)], axis=0)  6.52 us
  transfers between devices with their start and end apart: 3, of which 1 were waited for; matrix products, arithmetic and copies ran while one was open for 3% of the time, Pallas kernels for 0%

commit v1 on v0

--- a/solution.py
+++ b/solution.py
@@ -1,29 +1,31 @@
+import numpy as np
 import jax
 import jax.numpy as jnp
 from jax import lax
-from jax.sharding import PartitionSpec as P
+from jax.sharding import Mesh, PartitionSpec as P
 
 SAMPLES = 1024
 FREQ_BINS = 128
 FIRST_BIN = 8
 SMOOTH_BINS = 4
 MOST_REACH = 8
+ROW_GROUP = 8
 
 
 FLOOR_POWER = 0.01
 
+CHAN = ("ca", "cb")
 
-def with_halo(x, sides, width):
-    for axis, dim in sides:
-        devices, length = (lax.axis_size(axis), x.shape[dim])
-        up = [(i, (i + 1) % devices) for i in range(devices - 1)]
-        down = [(j, i) for i, j in up]
-        last = lax.slice_in_dim(x, length - width, length, axis=dim)
-        initial = lax.slice_in_dim(x, 0, width, axis=dim)
-        before = lax.ppermute(last, axis, up)
-        after = lax.ppermute(initial, axis, down)
-        x = jnp.concatenate([before, x, after], axis=dim)
-    return x
+
+def with_halo(x, width):
+    devices, length = (lax.axis_size(CHAN), x.shape[0])
+    up = [(i, (i + 1) % devices) for i in range(devices - 1)]
+    down = [(j, i) for i, j in up]
+    last = lax.slice_in_dim(x, length - width, length, axis=0)
+    initial = lax.slice_in_dim(x, 0, width, axis=0)
+    before = lax.ppermute(last, CHAN, up)
+    after = lax.ppermute(initial, CHAN, down)
+    return jnp.concatenate([before, x, after], axis=0)
 
 
 def fourier_table():
@@ -50,7 +52,9 @@
 
 def body(strain, seg_ids, dead, radius):
     local_rows = strain.shape[0]
-    device = lax.axis_index("chan")
+    group_b = lax.axis_size("cb")
+    group_a = lax.axis_size("ca")
+    device = lax.axis_index("ca") * group_b + lax.axis_index("cb")
     seg_padded = jnp.pad(seg_ids, (MOST_REACH, MOST_REACH), constant_values=-1)
     near_segs = lax.dynamic_slice_in_dim(
         seg_padded, device * local_rows, local_rows + 2 * MOST_REACH
@@ -72,7 +76,7 @@
     linked_f = linked.astype(jnp.float32)
     counts = jnp.maximum(jnp.sum(linked_f, axis=1), 1.0)
     fourier = fourier_table()
-    extended = with_halo(strain, (("chan", 0),), MOST_REACH)
+    extended = with_halo(strain, MOST_REACH)
     neighbor_sums = jnp.einsum(
         "cr,rwt->cwt", linked.astype(jnp.bfloat16), extended, preferred_element_type=jnp.float32
     )
@@ -91,18 +95,26 @@
     windows = banded.shape[1]
     spectra_block = banded.reshape(local_rows, -1)
     inverse_count = 1.0 / (spectra_block.shape[1] // 2)
-    piece = lax.all_gather(spectra_block, "chan", axis=0, tiled=True)
-    operands = jnp.stack([piece, swapped_parts(piece, windows)], axis=0)
-    product = jnp.einsum("ik,pjk->pij", spectra_block, operands, precision=lax.Precision.HIGHEST)
-    cross_spectra = (product * inverse_count).astype(jnp.bfloat16)
+    row_set = lax.all_gather(spectra_block, "cb", axis=0, tiled=True)
+    col_set = lax.all_gather(spectra_block, "ca", axis=0, tiled=True)
+    operands = jnp.concatenate([col_set, swapped_parts(col_set, windows)], axis=0)
+    product = jnp.einsum("ik,jk->ij", row_set, operands, precision=lax.Precision.HIGHEST)
+    product = (product * inverse_count).astype(jnp.bfloat16)
+    product = product.reshape(group_b * local_rows, 2, group_a, 1, local_rows)
+    product = product.transpose(1, 0, 2, 3, 4)
+    mine = lax.all_to_all(product, "cb", split_axis=1, concat_axis=3, tiled=True)
+    cross_spectra = mine.reshape(2, local_rows, -1)
     return cross_spectra[None]
 
 
 def solution(mesh):
+    chan_size = mesh.shape["chan"]
+    grid = mesh.devices.reshape(chan_size // ROW_GROUP, ROW_GROUP, mesh.shape["win"])
+    sub_mesh = Mesh(grid, ("ca", "cb", "win"))
     return jax.shard_map(
         body,
-        mesh=mesh,
-        in_specs=(P("chan", "win", None), P(), P(), P("chan")),
-        out_specs=P("win", None, "chan", None),
+        mesh=sub_mesh,
+        in_specs=(P(CHAN, "win", None), P(), P(), P(CHAN)),
+        out_specs=P("win", None, CHAN, None),
         check_vma=False,
     )

time: 224 us -> 164 us (0.73)
  the two profiles are of different devices: /device:TPU:1 before, /device:TPU:8 now
where the time goes in v1:
time: 164 us; the launch traced here: 163 us
  blocking collectives  111 us (68%)
  local copies, waits for them, and re-layouts  32.6 us (20%)
  starting transfers between devices  9.01 us (5%)
  other arithmetic  5.66 us (3%)
  matrix products  4.09 us (2%)
    all_gather x1, blocking collectives, body(): col_set = lax.all_gather(spectra_block, 'ca', axis=0, tiled=True)  52.2 us
    all_to_all x1, blocking collectives, body(): lax.all_to_all(product, 'cb', split_axis=1, concat_axis=3, tiled=True)  26.7 us
    all_gather x1, blocking collectives, body(): row_set = lax.all_gather(spectra_block, 'cb', axis=0, tiled=True)  26 us
    unnamed x4, local copies, waits for them, and re-layouts  10.7 us
    another operation x1, local copies, waits for them, and re-layouts, body(): return cross_spectra[None]  7.33 us
    all_to_all x1, blocking collectives, body(): lax.all_to_all(whitened, 'win', split_axis=3, concat_axis=1, tiled=True)  6.39 us
    ppermute x1, starting transfers between devices, with_halo(): after = lax.ppermute(initial, CHAN, down)  5.54 us
    all_to_all x1, local copies, waits for them, and re-layouts, body(): lax.all_to_all(product, 'cb', split_axis=1, concat_axis=3, tiled=True)  5.31 us
  transfers between devices with their start and end apart: 2, of which 0 were waited for; matrix products, arithmetic and copies ran while one was open for 3% of the time, Pallas kernels for 0%

profile of v1, /device:TPU:8, one launch (start us, length us, event | category | flops | bytes accessed | tf_op | source)
XLA Modules:
  0.0 162.9 jit_solution(6324231459040430103)
XLA Ops:
  0.0 0.7 fusion.36
  0.7 3.5 %collective-permute-start = (bf16[8,1,1024]{2,0,1:T(8,128)(2,1)S(1)}, bf16[8,1,1024]{2,0,1:T(8,128)(2,1)S(1)}, u32[]{:S(2)}, u32[]{:S(2)}) collective-permute-start(bf16[8,1,1024]{2,0,1:T(8,128)(2,1)S(1)} %get-tuple-element.9), channel_id=1, source_target_pairs={{0,4},{4,8},{8,12},{12,16},{16,20},{20,24},{24,28},{28,32},{32,36}... | collective-permute-start | bytes 49160 | tf_op jit(solution)/shard_map/ppermute | solution.py:26
  4.2 5.5 %collective-permute-start.1 = (bf16[8,1,1024]{2,0,1:T(8,128)(2,1)S(1)}, bf16[8,1,1024]{2,0,1:T(8,128)(2,1)S(1)}, u32[]{:S(2)}, u32[]{:S(2)}) collective-permute-start(bf16[8,1,1024]{2,0,1:T(8,128)(2,1)S(1)} %get-tuple-element.10), channel_id=1, source_target_pairs={{4,0},{8,4},{12,8},{16,12},{20,16},{24,20},{28,24},{32,28},{36,32}... | collective-permute-start | bytes 49160 | tf_op jit(solution)/shard_map/ppermute | solution.py:27
  9.8 0.8 pad_dynamic-slice_fusion
  10.7 0.9 select_reduce_fusion
  11.6 0.8 broadcast_compare_fusion
  12.4 2.1 %cosine_multiply_fusion = (f32[1024,128]{1,0:T(8,128)S(1)}, f32[1024,128]{1,0:T(8,128)S(1)}) fusion(s32[128]{0:T(128)S(1)} %iota_add_fusion, f32[1024]{0:T(1024)S(1)} %get-tuple-element.15, f32[1024]{0:T(1024)S(1)} %get-tuple-element.16), kind=kLoop, calls=%fused_computation.24 | loop fusion | flops 2097152 | bytes 1057280 | tf_op jit(solution)/shard_map/mul | solution.py:38
  14.5 0.8 convert_reduce_fusion.1
  15.4 1.2 fusion.7
  16.7 0.6 fusion.9
  17.9 6.4 %all_to_all.30 = f32[4,1,3072]{2,1,0:T(1,128)S(1)} all-to-all(f32[4,1,3072]{2,1,0:T(1,128)S(1)} %reshape.86), channel_id=1, replica_groups=mesh['ca'=16,'cb'=8,'win'=4] {'win'}, dimensions={0} | all-to-all | bytes 98304 | tf_op jit(solution)/shard_map/all_to_all | solution.py:94
  24.3 0.5 broadcast.84
  24.8 0.8 reduce
  25.9 26.0 %all_gather.6 = f32[384,256]{1,0:T(8,128)S(1)} all-gather(f32[48,256]{1,0:T(8,128)S(1)} %copy.23), channel_id=1, replica_groups=mesh['ca'=16,'cb'=8,'win'=4] {'cb'}, dimensions={0}, use_global_device_ids=true | all-gather | bytes 442368 | tf_op jit(solution)/shard_map/all_gather | solution.py:98
  51.9 52.2 %all_gather.7 = f32[768,256]{1,0:T(8,128)S(1)} all-gather(f32[48,256]{1,0:T(8,128)S(1)} %copy.23), channel_id=1, replica_groups=mesh['ca'=16,'cb'=8,'win'=4] {'ca'}, dimensions={0}, use_global_device_ids=true | all-gather | bytes 835584 | tf_op jit(solution)/shard_map/all_gather | solution.py:99
  104.2 0.3 copy.26
  104.6 2.1 %fusion = bf16[384,1536]{1,0:T(8,128)(2,1)S(1)} fusion(f32[384,256]{1,0:T(8,128)S(1)} %all_gather.6, f32[768,256]{0,1:T(8,128)S(1)} %bitcast.43, f32[768,256]{0,1:T(8,128)S(1)} %copy.26), kind=kOutput, calls=%fused_computation.1 | convolution fusion | flops 1813512192 | bytes 3145728 | tf_op jit(solution)/shard_map/ik,jk->ij/dot_general | solution.py:101
  106.6 1.4 copy.27
  108.1 5.3 %copy.28 = bf16[2,384,16,1,48]{4,2,0,3,1:T(8,128)(2,1)S(1)} copy(bf16[2,384,16,1,48]{1,4,2,0,3:T(8,128)(2,1)} %bitcast.42) | data formatting | bytes 2359296 | tf_op jit(solution)/shard_map/transpose | solution.py:104
  113.4 6.0 %reshape.88 = bf16[8,2,36864]{2,1,0:T(2,128)(2,1)} reshape(bf16[384,1,2,16,48]{4,3,2,1,0:T(8,128)(2,1)S(1)} %bitcast.40) | data formatting | bytes 2359296
  119.4 26.7 %all_to_all.31 = bf16[8,2,36864]{2,1,0:T(2,128)(2,1)} all-to-all(bf16[8,2,36864]{2,1,0:T(2,128)(2,1)} %reshape.88), channel_id=1, replica_groups=mesh['ca'=16,'cb'=8,'win'=4] {'cb'}, dimensions={0} | all-to-all | bytes 2359296 | tf_op jit(solution)/shard_map/all_to_all | solution.py:105
  146.1 4.2 %reshape.89 = bf16[384,1,2,16,48]{4,3,2,1,0:T(8,128)(2,1)S(1)} reshape(bf16[8,2,36864]{2,1,0:T(2,128)(2,1)} %all_to_all.31) | data formatting | bytes 2359296
  150.3 5.3 %copy.29 = bf16[2,48,16,8,1,48]{5,3,2,1,0,4:T(8,128)(2,1)} copy(bf16[2,48,16,8,1,48]{5,2,0,1,3,4:T(8,128)(2,1)S(1)} %bitcast.39) | data formatting | bytes 2359296 | tf_op jit(solution)/shard_map/all_to_all | solution.py:105
  155.6 7.3 %broadcast_in_dim_reshape.3 = bf16[1,2,48,6144]{3,2,1,0:T(8,128)(2,1)} reshape(bf16[2,48,16,8,1,48]{5,3,2,1,0,4:T(8,128)(2,1)} %copy.29) | data formatting | bytes 2359296 | tf_op jit(solution)/shard_map/broadcast_in_dim;reshape | solution.py:107
  (19 shorter events, 1.3 us)
Async XLA Ops:
  0.7 14.7 %collective-permute-start = (bf16[8,1,1024]{2,0,1:T(8,128)(2,1)S(1)}, bf16[8,1,1024]{2,0,1:T(8,128)(2,1)S(1)}, u32[]{:S(2)}, u32[]{:S(2)}) collective-permute-start(bf16[8,1,1024]{2,0,1:T(8,128)(2,1)S(1)} %get-tuple-element.9), channel_id=1, source_target_pairs={{0,4},{4,8},{8,12},{12,16},{16,20},{20,24},{24,28},{28,32},{32,36}... | collective-permute-start | bytes 49160 | tf_op jit(solution)/shard_map/ppermute | solution.py:26
  4.2 11.2 %collective-permute-start.1 = (bf16[8,1,1024]{2,0,1:T(8,128)(2,1)S(1)}, bf16[8,1,1024]{2,0,1:T(8,128)(2,1)S(1)}, u32[]{:S(2)}, u32[]{:S(2)}) collective-permute-start(bf16[8,1,1024]{2,0,1:T(8,128)(2,1)S(1)} %get-tuple-element.10), channel_id=1, source_target_pairs={{4,0},{8,4},{12,8},{16,12},{20,16},{24,20},{28,24},{32,28},{36,32}... | collective-permute-start | bytes 49160 | tf_op jit(solution)/shard_map/ppermute | solution.py:27

commit v2 on v1

--- a/solution.py
+++ b/solution.py
@@ -26,6 +26,19 @@
     before = lax.ppermute(last, CHAN, up)
     after = lax.ppermute(initial, CHAN, down)
     return jnp.concatenate([before, x, after], axis=0)
+
+
+def gather_blocks(block, axis):
+    size = lax.axis_size(axis)
+    me = lax.axis_index(axis)
+    pieces = [block]
+    for shift in range(1, size):
+        pairs = [(src, (src - shift) % size) for src in range(size)]
+        pieces.append(lax.ppermute(block, axis, pairs))
+    rel = jnp.concatenate(pieces + pieces, axis=0)
+    rows = block.shape[0]
+    start = ((size - me) % size) * rows
+    return lax.dynamic_slice_in_dim(rel, start, size * rows, axis=0)
 
 
 def fourier_table():
@@ -95,15 +108,15 @@
     windows = banded.shape[1]
     spectra_block = banded.reshape(local_rows, -1)
     inverse_count = 1.0 / (spectra_block.shape[1] // 2)
-    row_set = lax.all_gather(spectra_block, "cb", axis=0, tiled=True)
-    col_set = lax.all_gather(spectra_block, "ca", axis=0, tiled=True)
+    row_set = gather_blocks(spectra_block, "cb")
+    col_set = gather_blocks(spectra_block, "ca")
     operands = jnp.concatenate([col_set, swapped_parts(col_set, windows)], axis=0)
     product = jnp.einsum("ik,jk->ij", row_set, operands, precision=lax.Precision.HIGHEST)
     product = (product * inverse_count).astype(jnp.bfloat16)
-    product = product.reshape(group_b * local_rows, 2, group_a, 1, local_rows)
-    product = product.transpose(1, 0, 2, 3, 4)
-    mine = lax.all_to_all(product, "cb", split_axis=1, concat_axis=3, tiled=True)
-    cross_spectra = mine.reshape(2, local_rows, -1)
+    product = product.reshape(group_b * local_rows, 2, group_a, local_rows)
+    mine = lax.all_to_all(product, "cb", split_axis=0, concat_axis=0, tiled=True)
+    mine = mine.reshape(group_b, local_rows, 2, group_a, local_rows)
+    cross_spectra = mine.transpose(2, 1, 3, 0, 4).reshape(2, local_rows, -1)
     return cross_spectra[None]
 
 

time: 164 us -> 208 us (1.27)
  starting transfers between devices: 9.01 us -> 110 us
  blocking collectives: 111 us -> 39.4 us
  local copies, waits for them, and re-layouts: 32.6 us -> 40.6 us
  waiting for transfers between devices: 0.01 us -> 4.7 us
    ppermute x0 -> x22, starting transfers between devices: none -> 101 us  [gather_blocks(): pieces.append(lax.ppermute(block, axis, pairs))]
    all_gather x2 -> x0, blocking collectives: 78.2 us -> none  [the longest x1 52.2 us: body(): col_set = lax.all_gather(spectra_block, 'ca', axis=0, tiled=True)]
    concatenate x0 -> x2, local copies, waits for them, and re-layouts: none -> 7.39 us  [gather_blocks(): rel = jnp.concatenate(pieces + pieces, axis=0)]
    all_to_all x1, blocking collectives: 26.7 us -> 33 us  [body(): lax.all_to_all(product, 'cb', split_axis=0, concat_axis=0, tiled=True)]
    all_to_all x1 -> x0, local copies, waits for them, and re-layouts: 5.31 us -> none  [body(): lax.all_to_all(product, 'cb', split_axis=1, concat_axis=3, tiled=True)]
    reshape x1, local copies, waits for them, and re-layouts: 0.07 us -> 5.3 us  [body(): product = product.reshape(group_b * local_rows, 2, group_a, local_rows)]
    ppermute x0 -> x22, waiting for transfers between devices: none -> 4.7 us  [gather_blocks(): pieces.append(lax.ppermute(block, axis, pairs))]
    unnamed x4 -> x6, local copies, waits for them, and re-layouts: 10.7 us -> 11.3 us
  transfers between devices with their start and end apart: 2 -> 24, of which waited for: 0 -> 2; matrix products, arithmetic and copies ran while one was open for 3% -> 5% of each run, Pallas kernels for 0% -> 0%
where the time goes in v2:
time: 208 us; the launch traced here: 207 us
  starting transfers between devices  110 us (53%)
  local copies, waits for them, and re-layouts  40.6 us (20%)
  blocking collectives  39.4 us (19%)
  other arithmetic  5.66 us (3%)
  matrix products  5.27 us (3%)
  waiting for transfers between devices  4.7 us (2%)
    ppermute x22, starting transfers between devices, gather_blocks(): pieces.append(lax.ppermute(block, axis, pairs))  101 us
    all_to_all x1, blocking collectives, body(): lax.all_to_all(product, 'cb', split_axis=0, concat_axis=0, tiled=True)  33 us
    unnamed x6, local copies, waits for them, and re-layouts  11.3 us
    concatenate x2, local copies, waits for them, and re-layouts, gather_blocks(): rel = jnp.concatenate(pieces + pieces, axis=0)  7.39 us
    another operation x1, local copies, waits for them, and re-layouts, body(): return cross_spectra[None]  7.33 us
    all_to_all x1, blocking collectives, body(): lax.all_to_all(whitened, 'win', split_axis=3, concat_axis=1, tiled=True)  6.39 us
    ppermute x1, starting transfers between devices, with_halo(): after = lax.ppermute(initial, CHAN, down)  5.54 us
    reshape x1, local copies, waits for them, and re-layouts, body(): product = product.reshape(group_b * local_rows, 2, group_a, local_rows)  5.3 us
  transfers between devices with their start and end apart: 24, of which 2 were waited for; matrix products, arithmetic and copies ran while one was open for 5% of the time, Pallas kernels for 0%

profile of v2, /device:TPU:8, one launch (start us, length us, event | category | flops | bytes accessed | tf_op | source)
XLA Modules:
  0.0 206.7 jit_solution(10289871390235772952)
XLA Ops:
  4.2 5.5 %collective-permute-start.1 = (bf16[8,1,1024]{2,0,1:T(8,128)(2,1)S(1)}, bf16[8,1,1024]{2,0,1:T(8,128)(2,1)S(1)}, u32[]{:S(2)}, u32[]{:S(2)}) collective-permute-start(bf16[8,1,1024]{2,0,1:T(8,128)(2,1)S(1)} %get-tuple-element.10), channel_id=1, source_target_pairs={{4,0},{8,4},{12,8},{16,12},{20,16},{24,20},{28,24},{32,28},{36,32}... | collective-permute-start | bytes 49160 | tf_op jit(solution)/shard_map/ppermute | solution.py:27
  17.9 6.4 %all_to_all.20 = f32[4,1,3072]{2,1,0:T(1,128)S(1)} all-to-all(f32[4,1,3072]{2,1,0:T(1,128)S(1)} %reshape.89), channel_id=1, replica_groups=mesh['ca'=16,'cb'=8,'win'=4] {'win'}, dimensions={0} | all-to-all | bytes 98304 | tf_op jit(solution)/shard_map/all_to_all | solution.py:107
  25.9 4.0 %collective-permute-start.23 = (f32[48,256]{0,1:T(8,128)S(1)}, f32[48,256]{0,1:T(8,128)S(1)}, u32[]{:S(2)}, u32[]{:S(2)}) collective-permute-start(f32[48,256]{0,1:T(8,128)S(1)} %bitcast.35), channel_id=1, source_target_pairs={{0,32},{32,64},{64,96},{96,128},{128,160},{160,192},{192,224},{224... | collective-permute-start | bytes 147464 | tf_op jit(solution)/shard_map/ppermute | solution.py:37
  29.9 8.2 %collective-permute-start.22 = (f32[48,256]{0,1:T(8,128)S(1)}, f32[48,256]{0,1:T(8,128)S(1)}, u32[]{:S(2)}, u32[]{:S(2)}) collective-permute-start(f32[48,256]{0,1:T(8,128)S(1)} %bitcast.36), channel_id=1, source_target_pairs={{0,64},{32,96},{64,128},{96,160},{128,192},{160,224},{192,256},{22... | collective-permute-start | bytes 147464 | tf_op jit(solution)/shard_map/ppermute | solution.py:37
  38.1 4.6 %collective-permute-start.21 = (f32[48,256]{0,1:T(8,128)S(1)}, f32[48,256]{0,1:T(8,128)S(1)}, u32[]{:S(2)}, u32[]{:S(2)}) collective-permute-start(f32[48,256]{0,1:T(8,128)S(1)} %bitcast.37), channel_id=1, source_target_pairs={{0,96},{32,128},{64,160},{96,192},{128,224},{160,256},{192,288},{2... | collective-permute-start | bytes 147464 | tf_op jit(solution)/shard_map/ppermute | solution.py:37
  46.1 3.7 %collective-permute-start.19 = (f32[48,256]{0,1:T(8,128)S(1)}, f32[48,256]{0,1:T(8,128)S(1)}, u32[]{:S(2)}, u32[]{:S(2)}) collective-permute-start(f32[48,256]{0,1:T(8,128)S(1)} %bitcast.39), channel_id=1, source_target_pairs={{0,160},{32,192},{64,224},{96,256},{128,288},{160,320},{192,352},{... | collective-permute-start | bytes 147464 | tf_op jit(solution)/shard_map/ppermute | solution.py:37
  52.9 7.3 %collective-permute-start.17 = (f32[48,256]{0,1:T(8,128)S(1)}, f32[48,256]{0,1:T(8,128)S(1)}, u32[]{:S(2)}, u32[]{:S(2)}) collective-permute-start(f32[48,256]{0,1:T(8,128)S(1)} %bitcast.41), channel_id=1, source_target_pairs={{0,224},{32,256},{64,288},{96,320},{128,352},{160,384},{192,416},{... | collective-permute-start | bytes 147464 | tf_op jit(solution)/shard_map/ppermute | solution.py:37
  60.2 3.6 %collective-permute-start.16 = (f32[48,256]{0,1:T(8,128)S(1)}, f32[48,256]{0,1:T(8,128)S(1)}, u32[]{:S(2)}, u32[]{:S(2)}) collective-permute-start(f32[48,256]{0,1:T(8,128)S(1)} %bitcast.42), channel_id=1, source_target_pairs={{0,256},{32,288},{64,320},{96,352},{128,384},{160,416},{192,448},{... | collective-permute-start | bytes 147464 | tf_op jit(solution)/shard_map/ppermute | solution.py:37
  67.0 8.1 %collective-permute-start.14 = (f32[48,256]{0,1:T(8,128)S(1)}, f32[48,256]{0,1:T(8,128)S(1)}, u32[]{:S(2)}, u32[]{:S(2)}) collective-permute-start(f32[48,256]{0,1:T(8,128)S(1)} %bitcast.44), channel_id=1, source_target_pairs={{0,320},{32,352},{64,384},{96,416},{128,448},{160,480},{192,0},{22... | collective-permute-start | bytes 147464 | tf_op jit(solution)/shard_map/ppermute | solution.py:37
  75.1 6.7 %collective-permute-start.13 = (f32[48,256]{0,1:T(8,128)S(1)}, f32[48,256]{0,1:T(8,128)S(1)}, u32[]{:S(2)}, u32[]{:S(2)}) collective-permute-start(f32[48,256]{0,1:T(8,128)S(1)} %bitcast.45), channel_id=1, source_target_pairs={{0,352},{32,384},{64,416},{96,448},{128,480},{160,0},{192,32},{224... | collective-permute-start | bytes 147464 | tf_op jit(solution)/shard_map/ppermute | solution.py:37
  81.8 4.0 %collective-permute-start.12 = (f32[48,256]{0,1:T(8,128)S(1)}, f32[48,256]{0,1:T(8,128)S(1)}, u32[]{:S(2)}, u32[]{:S(2)}) collective-permute-start(f32[48,256]{0,1:T(8,128)S(1)} %bitcast.46), channel_id=1, source_target_pairs={{0,384},{32,416},{64,448},{96,480},{128,0},{160,32},{192,64},{224,... | collective-permute-start | bytes 147464 | tf_op jit(solution)/shard_map/ppermute | solution.py:37
  87.8 3.7 %collective-permute-start.10 = (f32[48,256]{0,1:T(8,128)S(1)}, f32[48,256]{0,1:T(8,128)S(1)}, u32[]{:S(2)}, u32[]{:S(2)}) collective-permute-start(f32[48,256]{0,1:T(8,128)S(1)} %bitcast.48), channel_id=1, source_target_pairs={{0,448},{32,480},{64,0},{96,32},{128,64},{160,96},{192,128},{224,1... | collective-permute-start | bytes 147464 | tf_op jit(solution)/shard_map/ppermute | solution.py:37
  91.5 5.5 %collective-permute-start.9 = (f32[48,256]{0,1:T(8,128)S(1)}, f32[48,256]{0,1:T(8,128)S(1)}, u32[]{:S(2)}, u32[]{:S(2)}) collective-permute-start(f32[48,256]{0,1:T(8,128)S(1)} %bitcast.49), channel_id=1, source_target_pairs={{0,480},{32,0},{64,32},{96,64},{128,96},{160,128},{192,160},{224,1... | collective-permute-start | bytes 147464 | tf_op jit(solution)/shard_map/ppermute | solution.py:37
  100.5 6.9 %collective-permute-start.7 = (f32[48,256]{0,1:T(8,128)S(1)}, f32[48,256]{0,1:T(8,128)}, u32[]{:S(2)}, u32[]{:S(2)}) collective-permute-start(f32[48,256]{0,1:T(8,128)S(1)} %bitcast.51), channel_id=1, source_target_pairs={{0,8},{4,12},{8,16},{12,20},{16,24},{20,28},{24,0},{28,4},{1,9},{5... | collective-permute-start | bytes 147464 | tf_op jit(solution)/shard_map/ppermute | solution.py:37
  110.2 5.9 %collective-permute-start.5 = (f32[48,256]{0,1:T(8,128)S(1)}, f32[48,256]{0,1:T(8,128)}, u32[]{:S(2)}, u32[]{:S(2)}) collective-permute-start(f32[48,256]{0,1:T(8,128)S(1)} %bitcast.53), channel_id=1, source_target_pairs={{0,16},{4,20},{8,24},{12,28},{16,0},{20,4},{24,8},{28,12},{1,17},{... | collective-permute-start | bytes 147464 | tf_op jit(solution)/shard_map/ppermute | solution.py:37
  116.8 6.9 %collective-permute-start.4 = (f32[48,256]{0,1:T(8,128)S(1)}, f32[48,256]{0,1:T(8,128)}, u32[]{:S(2)}, u32[]{:S(2)}) collective-permute-start(f32[48,256]{0,1:T(8,128)S(1)} %bitcast.54), channel_id=1, source_target_pairs={{0,20},{4,24},{8,28},{12,0},{16,4},{20,8},{24,12},{28,16},{1,21},{... | collective-permute-start | bytes 147464 | tf_op jit(solution)/shard_map/ppermute | solution.py:37
  123.7 4.7 %concatenate.23 = f32[1536,256]{0,1:T(8,128)S(1)} concatenate(f32[48,256]{0,1:T(8,128)S(1)} %bitcast.55, f32[48,256]{0,1:T(8,128)} %copy-done, f32[48,256]{0,1:T(8,128)S(1)} %collective-permute-done.10, f32[48,256]{0,1:T(8,128)S(1)} %collective-permute-done.11, f32[48,256]{0,1:T(8,128)S(1)} %collective-permute-done.12, f32[48,256]{0,1:T(8,128)S(1)} %collective-permute-done.13, ...), dimensions={0} | concatenate | bytes 3145728 | tf_op jit(solution)/shard_map/concatenate | solution.py:38
  133.5 4.2 %collective-permute-done.3 = f32[48,256]{0,1:T(8,128)S(1)} collective-permute-done((f32[48,256]{0,1:T(8,128)S(1)}, f32[48,256]{0,1:T(8,128)S(1)}, u32[]{:S(2)}, u32[]{:S(2)}) %collective-permute-start.3) | collective-permute-done | bytes 49184 | tf_op jit(solution)/shard_map/ppermute | solution.py:37
  145.5 5.3 %copy.20 = bf16[384,2,16,48]{3,2,1,0:T(8,128)(2,1)S(1)} copy(bf16[384,2,16,48]{0,3,2,1:T(8,128)(2,1)} %bitcast.34) | data formatting | bytes 2359296 | tf_op jit(solution)/shard_map/reshape | solution.py:116
  150.8 6.0 %reshape.91 = bf16[8,2,36864]{2,1,0:T(2,128)(2,1)} reshape(bf16[384,2,16,48]{3,2,1,0:T(8,128)(2,1)S(1)} %copy.20) | data formatting | bytes 2359296
  156.8 33.0 %all_to_all.21 = bf16[8,2,36864]{2,1,0:T(2,128)(2,1)} all-to-all(bf16[8,2,36864]{2,1,0:T(2,128)(2,1)} %reshape.91), channel_id=1, replica_groups=mesh['ca'=16,'cb'=8,'win'=4] {'cb'}, dimensions={0} | all-to-all | bytes 2359296 | tf_op jit(solution)/shard_map/all_to_all | solution.py:117
  189.9 4.2 %reshape.92 = bf16[384,2,16,48]{3,2,1,0:T(8,128)(2,1)S(1)} reshape(bf16[8,2,36864]{2,1,0:T(2,128)(2,1)} %all_to_all.21) | data formatting | bytes 2359296
  194.0 5.3 %copy.21 = bf16[2,48,16,8,48]{4,3,2,1,0:T(8,128)(2,1)} copy(bf16[2,48,16,8,48]{4,2,0,1,3:T(8,128)(2,1)S(1)} %bitcast.32) | data formatting | bytes 2359296 | tf_op jit(solution)/shard_map/transpose | solution.py:119
  199.3 7.3 %broadcast_in_dim_reshape.3 = bf16[1,2,48,6144]{3,2,1,0:T(8,128)(2,1)} reshape(bf16[2,48,16,8,48]{4,3,2,1,0:T(8,128)(2,1)} %copy.21) | data formatting | bytes 2359296 | tf_op jit(solution)/shard_map/broadcast_in_dim;reshape | solution.py:120
  (64 shorter events, 44.9 us)
Async XLA Ops:
  0.7 14.7 %collective-permute-start = (bf16[8,1,1024]{2,0,1:T(8,128)(2,1)S(1)}, bf16[8,1,1024]{2,0,1:T(8,128)(2,1)S(1)}, u32[]{:S(2)}, u32[]{:S(2)}) collective-permute-start(bf16[8,1,1024]{2,0,1:T(8,128)(2,1)S(1)} %get-tuple-element.9), channel_id=1, source_target_pairs={{0,4},{4,8},{8,12},{12,16},{16,20},{20,24},{24,28},{28,32},{32,36}... | collective-permute-start | bytes 49160 | tf_op jit(solution)/shard_map/ppermute | solution.py:26
  4.2 11.2 %collective-permute-start.1 = (bf16[8,1,1024]{2,0,1:T(8,128)(2,1)S(1)}, bf16[8,1,1024]{2,0,1:T(8,128)(2,1)S(1)}, u32[]{:S(2)}, u32[]{:S(2)}) collective-permute-start(bf16[8,1,1024]{2,0,1:T(8,128)(2,1)S(1)} %get-tuple-element.10), channel_id=1, source_target_pairs={{4,0},{8,4},{12,8},{16,12},{20,16},{24,20},{28,24},{32,28},{36,32}... | collective-permute-start | bytes 49160 | tf_op jit(solution)/shard_map/ppermute | solution.py:27
  25.9 23.9 %collective-permute-start.23 = (f32[48,256]{0,1:T(8,128)S(1)}, f32[48,256]{0,1:T(8,128)S(1)}, u32[]{:S(2)}, u32[]{:S(2)}) collective-permute-start(f32[48,256]{0,1:T(8,128)S(1)} %bitcast.35), channel_id=1, source_target_pairs={{0,32},{32,64},{64,96},{96,128},{128,160},{160,192},{192,224},{224... | collective-permute-start | bytes 147464 | tf_op jit(solution)/shard_map/ppermute | solution.py:37
  29.9 23.0 %collective-permute-start.22 = (f32[48,256]{0,1:T(8,128)S(1)}, f32[48,256]{0,1:T(8,128)S(1)}, u32[]{:S(2)}, u32[]{:S(2)}) collective-permute-start(f32[48,256]{0,1:T(8,128)S(1)} %bitcast.36), channel_id=1, source_target_pairs={{0,64},{32,96},{64,128},{96,160},{128,192},{160,224},{192,256},{22... | collective-permute-start | bytes 147464 | tf_op jit(solution)/shard_map/ppermute | solution.py:37
  38.1 22.1 %collective-permute-start.21 = (f32[48,256]{0,1:T(8,128)S(1)}, f32[48,256]{0,1:T(8,128)S(1)}, u32[]{:S(2)}, u32[]{:S(2)}) collective-permute-start(f32[48,256]{0,1:T(8,128)S(1)} %bitcast.37), channel_id=1, source_target_pairs={{0,96},{32,128},{64,160},{96,192},{128,224},{160,256},{192,288},{2... | collective-permute-start | bytes 147464 | tf_op jit(solution)/shard_map/ppermute | solution.py:37
  42.7 21.2 %collective-permute-start.20 = (f32[48,256]{0,1:T(8,128)S(1)}, f32[48,256]{0,1:T(8,128)S(1)}, u32[]{:S(2)}, u32[]{:S(2)}) collective-permute-start(f32[48,256]{0,1:T(8,128)S(1)} %bitcast.38), channel_id=1, source_target_pairs={{0,128},{32,160},{64,192},{96,224},{128,256},{160,288},{192,320},{... | collective-permute-start | bytes 147464 | tf_op jit(solution)/shard_map/ppermute | solution.py:37
  46.1 20.9 %collective-permute-start.19 = (f32[48,256]{0,1:T(8,128)S(1)}, f32[48,256]{0,1:T(8,128)S(1)}, u32[]{:S(2)}, u32[]{:S(2)}) collective-permute-start(f32[48,256]{0,1:T(8,128)S(1)} %bitcast.39), channel_id=1, source_target_pairs={{0,160},{32,192},{64,224},{96,256},{128,288},{160,320},{192,352},{... | collective-permute-start | bytes 147464 | tf_op jit(solution)/shard_map/ppermute | solution.py:37
  49.8 25.3 %collective-permute-start.18 = (f32[48,256]{0,1:T(8,128)S(1)}, f32[48,256]{0,1:T(8,128)S(1)}, u32[]{:S(2)}, u32[]{:S(2)}) collective-permute-start(f32[48,256]{0,1:T(8,128)S(1)} %bitcast.40), channel_id=1, source_target_pairs={{0,192},{32,224},{64,256},{96,288},{128,320},{160,352},{192,384},{... | collective-permute-start | bytes 147464 | tf_op jit(solution)/shard_map/ppermute | solution.py:37
  52.9 28.9 %collective-permute-start.17 = (f32[48,256]{0,1:T(8,128)S(1)}, f32[48,256]{0,1:T(8,128)S(1)}, u32[]{:S(2)}, u32[]{:S(2)}) collective-permute-start(f32[48,256]{0,1:T(8,128)S(1)} %bitcast.41), channel_id=1, source_target_pairs={{0,224},{32,256},{64,288},{96,320},{128,352},{160,384},{192,416},{... | collective-permute-start | bytes 147464 | tf_op jit(solution)/shard_map/ppermute | solution.py:37
  60.2 25.6 %collective-permute-start.16 = (f32[48,256]{0,1:T(8,128)S(1)}, f32[48,256]{0,1:T(8,128)S(1)}, u32[]{:S(2)}, u32[]{:S(2)}) collective-permute-start(f32[48,256]{0,1:T(8,128)S(1)} %bitcast.42), channel_id=1, source_target_pairs={{0,256},{32,288},{64,320},{96,352},{128,384},{160,416},{192,448},{... | collective-permute-start | bytes 147464 | tf_op jit(solution)/shard_map/ppermute | solution.py:37
  63.9 23.9 %collective-permute-start.15 = (f32[48,256]{0,1:T(8,128)S(1)}, f32[48,256]{0,1:T(8,128)S(1)}, u32[]{:S(2)}, u32[]{:S(2)}) collective-permute-start(f32[48,256]{0,1:T(8,128)S(1)} %bitcast.43), channel_id=1, source_target_pairs={{0,288},{32,320},{64,352},{96,384},{128,416},{160,448},{192,480},{... | collective-permute-start | bytes 147464 | tf_op jit(solution)/shard_map/ppermute | solution.py:37
  67.0 24.5 %collective-permute-start.14 = (f32[48,256]{0,1:T(8,128)S(1)}, f32[48,256]{0,1:T(8,128)S(1)}, u32[]{:S(2)}, u32[]{:S(2)}) collective-permute-start(f32[48,256]{0,1:T(8,128)S(1)} %bitcast.44), channel_id=1, source_target_pairs={{0,320},{32,352},{64,384},{96,416},{128,448},{160,480},{192,0},{22... | collective-permute-start | bytes 147464 | tf_op jit(solution)/shard_map/ppermute | solution.py:37
  75.1 21.9 %collective-permute-start.13 = (f32[48,256]{0,1:T(8,128)S(1)}, f32[48,256]{0,1:T(8,128)S(1)}, u32[]{:S(2)}, u32[]{:S(2)}) collective-permute-start(f32[48,256]{0,1:T(8,128)S(1)} %bitcast.45), channel_id=1, source_target_pairs={{0,352},{32,384},{64,416},{96,448},{128,480},{160,0},{192,32},{224... | collective-permute-start | bytes 147464 | tf_op jit(solution)/shard_map/ppermute | solution.py:37
  81.8 18.7 %collective-permute-start.12 = (f32[48,256]{0,1:T(8,128)S(1)}, f32[48,256]{0,1:T(8,128)S(1)}, u32[]{:S(2)}, u32[]{:S(2)}) collective-permute-start(f32[48,256]{0,1:T(8,128)S(1)} %bitcast.46), channel_id=1, source_target_pairs={{0,384},{32,416},{64,448},{96,480},{128,0},{160,32},{192,64},{224,... | collective-permute-start | bytes 147464 | tf_op jit(solution)/shard_map/ppermute | solution.py:37
  85.8 21.6 %collective-permute-start.11 = (f32[48,256]{0,1:T(8,128)S(1)}, f32[48,256]{0,1:T(8,128)S(1)}, u32[]{:S(2)}, u32[]{:S(2)}) collective-permute-start(f32[48,256]{0,1:T(8,128)S(1)} %bitcast.47), channel_id=1, source_target_pairs={{0,416},{32,448},{64,480},{96,0},{128,32},{160,64},{192,96},{224,1... | collective-permute-start | bytes 147464 | tf_op jit(solution)/shard_map/ppermute | solution.py:37
  87.8 22.4 %collective-permute-start.10 = (f32[48,256]{0,1:T(8,128)S(1)}, f32[48,256]{0,1:T(8,128)S(1)}, u32[]{:S(2)}, u32[]{:S(2)}) collective-permute-start(f32[48,256]{0,1:T(8,128)S(1)} %bitcast.48), channel_id=1, source_target_pairs={{0,448},{32,480},{64,0},{96,32},{128,64},{160,96},{192,128},{224,1... | collective-permute-start | bytes 147464 | tf_op jit(solution)/shard_map/ppermute | solution.py:37
  91.5 24.7 %collective-permute-start.9 = (f32[48,256]{0,1:T(8,128)S(1)}, f32[48,256]{0,1:T(8,128)S(1)}, u32[]{:S(2)}, u32[]{:S(2)}) collective-permute-start(f32[48,256]{0,1:T(8,128)S(1)} %bitcast.49), channel_id=1, source_target_pairs={{0,480},{32,0},{64,32},{96,64},{128,96},{160,128},{192,160},{224,1... | collective-permute-start | bytes 147464 | tf_op jit(solution)/shard_map/ppermute | solution.py:37
  97.0 31.8 %collective-permute-start.8 = (f32[48,256]{0,1:T(8,128)S(1)}, f32[48,256]{0,1:T(8,128)}, u32[]{:S(2)}, u32[]{:S(2)}) collective-permute-start(f32[48,256]{0,1:T(8,128)S(1)} %bitcast.50), channel_id=1, source_target_pairs={{0,4},{4,8},{8,12},{12,16},{16,20},{20,24},{24,28},{28,0},{1,5},{5... | collective-permute-start | bytes 147464 | tf_op jit(solution)/shard_map/ppermute | solution.py:37
  100.5 30.2 %collective-permute-start.7 = (f32[48,256]{0,1:T(8,128)S(1)}, f32[48,256]{0,1:T(8,128)}, u32[]{:S(2)}, u32[]{:S(2)}) collective-permute-start(f32[48,256]{0,1:T(8,128)S(1)} %bitcast.51), channel_id=1, source_target_pairs={{0,8},{4,12},{8,16},{12,20},{16,24},{20,28},{24,0},{28,4},{1,9},{5... | collective-permute-start | bytes 147464 | tf_op jit(solution)/shard_map/ppermute | solution.py:37
  107.4 26.0 %collective-permute-start.6 = (f32[48,256]{0,1:T(8,128)S(1)}, f32[48,256]{0,1:T(8,128)}, u32[]{:S(2)}, u32[]{:S(2)}) collective-permute-start(f32[48,256]{0,1:T(8,128)S(1)} %bitcast.52), channel_id=1, source_target_pairs={{0,12},{4,16},{8,20},{12,24},{16,28},{20,0},{24,4},{28,8},{1,13},{... | collective-permute-start | bytes 147464 | tf_op jit(solution)/shard_map/ppermute | solution.py:37
  110.2 23.3 %collective-permute-start.5 = (f32[48,256]{0,1:T(8,128)S(1)}, f32[48,256]{0,1:T(8,128)}, u32[]{:S(2)}, u32[]{:S(2)}) collective-permute-start(f32[48,256]{0,1:T(8,128)S(1)} %bitcast.53), channel_id=1, source_target_pairs={{0,16},{4,20},{8,24},{12,28},{16,0},{20,4},{24,8},{28,12},{1,17},{... | collective-permute-start | bytes 147464 | tf_op jit(solution)/shard_map/ppermute | solution.py:37
  116.8 16.7 %collective-permute-start.4 = (f32[48,256]{0,1:T(8,128)S(1)}, f32[48,256]{0,1:T(8,128)}, u32[]{:S(2)}, u32[]{:S(2)}) collective-permute-start(f32[48,256]{0,1:T(8,128)S(1)} %bitcast.54), channel_id=1, source_target_pairs={{0,20},{4,24},{8,28},{12,0},{16,4},{20,8},{24,12},{28,16},{1,21},{... | collective-permute-start | bytes 147464 | tf_op jit(solution)/shard_map/ppermute | solution.py:37
  128.8 8.9 %collective-permute-start.3 = (f32[48,256]{0,1:T(8,128)S(1)}, f32[48,256]{0,1:T(8,128)S(1)}, u32[]{:S(2)}, u32[]{:S(2)}) collective-permute-start(f32[48,256]{0,1:T(8,128)S(1)} %bitcast.57), channel_id=1, source_target_pairs={{0,24},{4,28},{8,0},{12,4},{16,8},{20,12},{24,16},{28,20},{1,25},{... | collective-permute-start | bytes 147464 | tf_op jit(solution)/shard_map/ppermute | solution.py:37
  130.8 7.4 %collective-permute-start.2 = (f32[48,256]{0,1:T(8,128)S(1)}, f32[48,256]{0,1:T(8,128)S(1)}, u32[]{:S(2)}, u32[]{:S(2)}) collective-permute-start(f32[48,256]{0,1:T(8,128)S(1)} %bitcast.58), channel_id=1, source_target_pairs={{0,28},{4,0},{8,4},{12,8},{16,12},{20,16},{24,20},{28,24},{1,29},{... | collective-permute-start | bytes 147464 | tf_op jit(solution)/shard_map/ppermute | solution.py:37
  (1 other events, 0.7 us)

commit v3 on v1

--- a/solution.py
+++ b/solution.py
@@ -10,6 +10,8 @@
 SMOOTH_BINS = 4
 MOST_REACH = 8
 ROW_GROUP = 8
+COL_PAD = 128
+ROW_PAD = 64
 
 
 FLOOR_POWER = 0.01
@@ -27,6 +29,12 @@
     after = lax.ppermute(initial, CHAN, down)
     return jnp.concatenate([before, x, after], axis=0)
 
+
+def gather_blocks(block, axis, padded_rows):
+    rows = block.shape[0]
+    wide = jnp.pad(block, ((0, padded_rows - rows), (0, 0)))
+    every = lax.all_gather(wide, axis, axis=0, tiled=False)
+    return every[:, :rows].reshape(-1, block.shape[1])
 
 def fourier_table():
     sample_ids = jnp.arange(SAMPLES, dtype=jnp.int32)
@@ -95,15 +103,15 @@
     windows = banded.shape[1]
     spectra_block = banded.reshape(local_rows, -1)
     inverse_count = 1.0 / (spectra_block.shape[1] // 2)
-    row_set = lax.all_gather(spectra_block, "cb", axis=0, tiled=True)
-    col_set = lax.all_gather(spectra_block, "ca", axis=0, tiled=True)
+    col_set = gather_blocks(spectra_block, "cb", COL_PAD)
+    row_set = gather_blocks(spectra_block, "ca", ROW_PAD)
     operands = jnp.concatenate([col_set, swapped_parts(col_set, windows)], axis=0)
     product = jnp.einsum("ik,jk->ij", row_set, operands, precision=lax.Precision.HIGHEST)
     product = (product * inverse_count).astype(jnp.bfloat16)
-    product = product.reshape(group_b * local_rows, 2, group_a, 1, local_rows)
-    product = product.transpose(1, 0, 2, 3, 4)
-    mine = lax.all_to_all(product, "cb", split_axis=1, concat_axis=3, tiled=True)
-    cross_spectra = mine.reshape(2, local_rows, -1)
+    product = product.reshape(group_a, local_rows, operands.shape[0])
+    mine = lax.all_to_all(product, "ca", split_axis=0, concat_axis=0, tiled=True)
+    mine = mine.reshape(group_a, local_rows, 2, col_set.shape[0])
+    cross_spectra = mine.transpose(2, 1, 0, 3).reshape(2, local_rows, -1)
     return cross_spectra[None]
 
 

time: 164 us -> 187 us (1.14)
  the two profiles are of different devices: /device:TPU:8 before, /device:TPU:1 now
where the time goes in v3:
time: 187 us
  waiting for transfers between devices  104 us (56%)
  blocking collectives  46.3 us (25%)
  between operations  13.6 us (7%)
  local copies, waits for them, and re-layouts  9.92 us (5%)
  starting transfers between devices  5.36 us (3%)
  other arithmetic  4.94 us (3%)
  matrix products  3.13 us (2%)
    all_gather x2, waiting for transfers between devices, gather_blocks(): every = lax.all_gather(wide, axis, axis=0, tiled=False)  104 us
    all_to_all x1, blocking collectives, body(): lax.all_to_all(product, 'ca', split_axis=0, concat_axis=0, tiled=True)  36.6 us
    all_to_all x1, blocking collectives, body(): lax.all_to_all(whitened, 'win', split_axis=3, concat_axis=1, tiled=True)  9.71 us
    ppermute x1, starting transfers between devices, with_halo(): before = lax.ppermute(last, CHAN, up)  4.02 us
  transfers between devices with their start and end apart: 4, of which 2 were waited for; matrix products, arithmetic and copies ran while one was open for 4% of the time, Pallas kernels for 0%

profile of v3, /device:TPU:1, one launch (start us, length us, event | category | flops | bytes accessed | tf_op | source)
XLA Modules:
  0.0 187.0 jit_solution(14439219022090187181)
XLA Ops:
  6.5 0.8 fusion.35
  7.3 4.0 %collective-permute-start = (bf16[8,1,1024]{2,0,1:T(8,128)(2,1)S(1)}, bf16[8,1,1024]{2,0,1:T(8,128)(2,1)S(1)}, u32[]{:S(2)}, u32[]{:S(2)}) collective-permute-start(bf16[8,1,1024]{2,0,1:T(8,128)(2,1)S(1)} %get-tuple-element.9), channel_id=1, source_target_pairs={{0,4},{4,8},{8,12},{12,16},{16,20},{20,24},{24,28},{28,32},{32,36}... | collective-permute-start | bytes 49160 | tf_op jit(solution)/shard_map/ppermute | solution.py:28
  11.4 1.3 collective-permute-start.1
  12.7 0.8 pad_dynamic-slice_fusion
  13.6 0.9 select_reduce_fusion
  14.4 0.8 broadcast_compare_fusion
  15.3 2.1 %cosine_multiply_fusion = (f32[1024,128]{1,0:T(8,128)S(1)}, f32[1024,128]{1,0:T(8,128)S(1)}) fusion(s32[128]{0:T(128)S(1)} %iota_add_fusion, f32[1024]{0:T(1024)S(1)} %get-tuple-element.15, f32[1024]{0:T(1024)S(1)} %get-tuple-element.16), kind=kLoop, calls=%fused_computation.23 | loop fusion | flops 2097152 | bytes 1057280 | tf_op jit(solution)/shard_map/mul | solution.py:46
  17.9 0.6 fusion.5
  19.1 9.7 %all_to_all.20 = f32[4,1,3072]{2,1,0:T(1,128)S(1)} all-to-all(f32[4,1,3072]{2,1,0:T(1,128)S(1)} %reshape.95), channel_id=1, replica_groups=mesh['ca'=16,'cb'=8,'win'=4] {'win'}, dimensions={0} | all-to-all | bytes 98304 | tf_op jit(solution)/shard_map/all_to_all | solution.py:102
  28.8 0.5 broadcast.88
  29.4 0.8 reduce
  30.4 0.7 pad.14
  31.2 0.6 pad.13.clone
  31.9 41.5 %all-gather.7.cloned.1.call-done = f32[1024,256]{0,1:T(8,128)} async-done(((f32[128,256]{0,1:T(8,128)}), f32[1024,256]{0,1:T(8,128)}) %all-gather.7.cloned.1.call-update) | async-done | bytes 1048592 | tf_op jit(solution)/shard_map/all_gather | solution.py:36
  73.4 1.6 copy.32
  75.0 0.4 copy.29
  75.5 0.3 reshape_reshape.3
  76.0 62.1 %all-gather.5.cloned.1.call-done = f32[1024,256]{1,0:T(8,128)} async-done(((f32[64,256]{1,0:T(8,128)}), f32[1024,256]{1,0:T(8,128)}) %all-gather.5.cloned.1.call-update) | async-done | bytes 1048592 | tf_op jit(solution)/shard_map/all_gather | solution.py:36
  138.2 1.2 slice.42
  139.3 2.1 %multiply_convert_fusion = bf16[768,768]{1,0:T(8,128)(2,1)S(1)} fusion(f32[768,256]{1,0:T(8,128)S(1)} %bitcast.41, f32[384,256]{1,0:T(8,128)S(1)} %copy.30, f32[384,256]{1,0:T(8,128)S(1)} %bitcast.40), kind=kOutput, calls=%fused_computation | convolution fusion | flops 1813315584 | bytes 2752512 | tf_op jit(solution)/shard_map/ik,jk->ij/dot_general | solution.py:109
  141.5 36.6 %all_to_all.21 = bf16[16,48,768]{2,1,0:T(8,128)(2,1)S(1)} all-to-all(bf16[16,48,768]{2,1,0:T(8,128)(2,1)S(1)} %bitcast.39), channel_id=1, replica_groups=mesh['ca'=16,'cb'=8,'win'=4] {'ca'}, dimensions={0} | all-to-all | bytes 2359296 | tf_op jit(solution)/shard_map/all_to_all | solution.py:112
  178.1 0.3 reshape.92
  178.4 0.4 copy.35
  178.8 1.4 broadcast_in_dim_reshape.3
  (31 shorter events, 1.9 us)
Async XLA Ops:
  6.5 11.1 %copy-start = (bf16[48,1,1024]{2,0,1:T(8,128)(2,1)S(1)}, bf16[48,1,1024]{2,0,1:T(8,128)(2,1)}, u32[]{:S(2)}) copy-start(bf16[48,1,1024]{2,0,1:T(8,128)(2,1)} %param.4) | copy-start | bytes 294916
  6.5 10.9 %copy-start.1 = (s32[48]{0:T(128)S(1)}, s32[48]{0:T(128)}, u32[]{:S(2)}) copy-start(s32[48]{0:T(128)} %param.7) | copy-start | bytes 580
  6.5 66.9 %all-gather.7.cloned.1.call-start = ((), (), s32[]{:S(2)}) async-start(), calls=%async_computation.3 | async-start | bytes 1179648 | tf_op jit(solution)/shard_map/all_gather | solution.py:36
  7.3 10.3 %collective-permute-start = (bf16[8,1,1024]{2,0,1:T(8,128)(2,1)S(1)}, bf16[8,1,1024]{2,0,1:T(8,128)(2,1)S(1)}, u32[]{:S(2)}, u32[]{:S(2)}) collective-permute-start(bf16[8,1,1024]{2,0,1:T(8,128)(2,1)S(1)} %get-tuple-element.9), channel_id=1, source_target_pairs={{0,4},{4,8},{8,12},{12,16},{16,20},{20,24},{24,28},{28,32},{32,36}... | collective-permute-start | bytes 49160 | tf_op jit(solution)/shard_map/ppermute | solution.py:28
  11.4 6.3 %collective-permute-start.1 = (bf16[8,1,1024]{2,0,1:T(8,128)(2,1)S(1)}, bf16[8,1,1024]{2,0,1:T(8,128)(2,1)S(1)}, u32[]{:S(2)}, u32[]{:S(2)}) collective-permute-start(bf16[8,1,1024]{2,0,1:T(8,128)(2,1)S(1)} %get-tuple-element.10), channel_id=1, source_target_pairs={{4,0},{8,4},{12,8},{16,12},{20,16},{24,20},{28,24},{32,28},{36,32}... | collective-permute-start | bytes 49160 | tf_op jit(solution)/shard_map/ppermute | solution.py:29
  31.1 107.0 %all-gather.5.cloned.1.call-start = ((), (), s32[]{:S(2)}) async-start(), calls=%async_computation.2 | async-start | bytes 1114112 | tf_op jit(solution)/shard_map/all_gather | solution.py:36
Sparse Core Ops, SparseCore 0:
  31.2 42.1 all-gather.6
  76.5 61.6 all-gather.4

commit v4 on v3

--- a/solution.py
+++ b/solution.py
@@ -10,8 +10,6 @@
 SMOOTH_BINS = 4
 MOST_REACH = 8
 ROW_GROUP = 8
-COL_PAD = 128
-ROW_PAD = 64
 
 
 FLOOR_POWER = 0.01
@@ -30,11 +28,11 @@
     return jnp.concatenate([before, x, after], axis=0)
 
 
-def gather_blocks(block, axis, padded_rows):
-    rows = block.shape[0]
-    wide = jnp.pad(block, ((0, padded_rows - rows), (0, 0)))
-    every = lax.all_gather(wide, axis, axis=0, tiled=False)
-    return every[:, :rows].reshape(-1, block.shape[1])
+def gather_blocks(block, axis):
+    size = lax.axis_size(axis)
+    copies = jnp.broadcast_to(block[None], (size,) + block.shape)
+    every = lax.all_to_all(copies, axis, split_axis=0, concat_axis=0, tiled=True)
+    return every.reshape(-1, block.shape[1])
 
 def fourier_table():
     sample_ids = jnp.arange(SAMPLES, dtype=jnp.int32)
@@ -103,8 +101,8 @@
     windows = banded.shape[1]
     spectra_block = banded.reshape(local_rows, -1)
     inverse_count = 1.0 / (spectra_block.shape[1] // 2)
-    col_set = gather_blocks(spectra_block, "cb", COL_PAD)
-    row_set = gather_blocks(spectra_block, "ca", ROW_PAD)
+    col_set = gather_blocks(spectra_block, "cb")
+    row_set = gather_blocks(spectra_block, "ca")
     operands = jnp.concatenate([col_set, swapped_parts(col_set, windows)], axis=0)
     product = jnp.einsum("ik,jk->ij", row_set, operands, precision=lax.Precision.HIGHEST)
     product = (product * inverse_count).astype(jnp.bfloat16)

time: 187 us -> 116 us (0.62); the launches traced: 187 us -> 114 us
  waiting for transfers between devices: 104 us -> 20.3 us
  blocking collectives: 46.3 us -> 61.6 us
  between operations: 13.6 us -> 0.23 us
  starting transfers between devices: 5.36 us -> 17 us
  local copies, waits for them, and re-layouts: 9.92 us -> 6.84 us
    all_gather x2 -> x0, waiting for transfers between devices: 104 us -> none  [gather_blocks(): every = lax.all_gather(wide, axis, axis=0, tiled=False)]
    all_to_all x0 -> x1, waiting for transfers between devices: none -> 20.3 us  [gather_blocks(): lax.all_to_all(copies, axis, split_axis=0, concat_axis=0, tiled=True)]
    all_to_all x0 -> x1, blocking collectives: none -> 20.2 us  [gather_blocks(): lax.all_to_all(copies, axis, split_axis=0, concat_axis=0, tiled=True)]
    all_to_all x0 -> x1, starting transfers between devices: none -> 11.7 us  [gather_blocks(): lax.all_to_all(copies, axis, split_axis=0, concat_axis=0, tiled=True)]
    all_to_all x1, blocking collectives: 36.6 us -> 31.7 us  [body(): lax.all_to_all(product, 'ca', split_axis=0, concat_axis=0, tiled=True)]
  transfers between devices with their start and end apart: 4 -> 3, of which waited for: 2 -> 1; matrix products, arithmetic and copies ran while one was open for 4% -> 5% of each run, Pallas kernels for 0% -> 0%
where the time goes in v4:
time: 116 us; the launch traced here: 114 us
  blocking collectives  61.6 us (53%)
  waiting for transfers between devices  20.3 us (18%)
  starting transfers between devices  17 us (15%)
  local copies, waits for them, and re-layouts  6.84 us (6%)
  other arithmetic  4.94 us (4%)
  matrix products  3.13 us (3%)
    all_to_all x1, blocking collectives, body(): lax.all_to_all(product, 'ca', split_axis=0, concat_axis=0, tiled=True)  31.7 us
    all_to_all x1, waiting for transfers between devices, gather_blocks(): lax.all_to_all(copies, axis, split_axis=0, concat_axis=0, tiled=True)  20.3 us
    all_to_all x1, blocking collectives, gather_blocks(): lax.all_to_all(copies, axis, split_axis=0, concat_axis=0, tiled=True)  20.2 us
    all_to_all x1, starting transfers between devices, gather_blocks(): lax.all_to_all(copies, axis, split_axis=0, concat_axis=0, tiled=True)  11.7 us
    all_to_all x1, blocking collectives, body(): lax.all_to_all(whitened, 'win', split_axis=3, concat_axis=1, tiled=True)  9.71 us
    ppermute x1, starting transfers between devices, with_halo(): before = lax.ppermute(last, CHAN, up)  4.02 us
  transfers between devices with their start and end apart: 3, of which 1 were waited for; matrix products, arithmetic and copies ran while one was open for 5% of the time, Pallas kernels for 0%

profile of v4, /device:TPU:1, one launch (start us, length us, event | category | flops | bytes accessed | tf_op | source)
XLA Modules:
  0.0 114.0 jit_solution(7182180770216843133)
XLA Ops:
  0.0 0.8 fusion.35
  0.8 4.0 %collective-permute-start = (bf16[8,1,1024]{2,0,1:T(8,128)(2,1)S(1)}, bf16[8,1,1024]{2,0,1:T(8,128)(2,1)S(1)}, u32[]{:S(2)}, u32[]{:S(2)}) collective-permute-start(bf16[8,1,1024]{2,0,1:T(8,128)(2,1)S(1)} %get-tuple-element.9), channel_id=1, source_target_pairs={{0,4},{4,8},{8,12},{12,16},{16,20},{20,24},{24,28},{28,32},{32,36}... | collective-permute-start | bytes 49160 | tf_op jit(solution)/shard_map/ppermute | solution.py:26
  4.8 1.3 %collective-permute-start.1 = (bf16[8,1,1024]{2,0,1:T(8,128)(2,1)S(1)}, bf16[8,1,1024]{2,0,1:T(8,128)(2,1)S(1)}, u32[]{:S(2)}, u32[]{:S(2)}) collective-permute-start(bf16[8,1,1024]{2,0,1:T(8,128)(2,1)S(1)} %get-tuple-element.10), channel_id=1, source_target_pairs={{4,0},{8,4},{12,8},{16,12},{20,16},{24,20},{28,24},{32,28},{36,32}... | collective-permute-start | bytes 49160 | tf_op jit(solution)/shard_map/ppermute | solution.py:27
  6.2 0.8 pad_dynamic-slice_fusion
  7.0 0.9 select_reduce_fusion
  7.9 0.8 broadcast_compare_fusion
  8.8 2.1 %cosine_multiply_fusion = (f32[1024,128]{1,0:T(8,128)S(1)}, f32[1024,128]{1,0:T(8,128)S(1)}) fusion(s32[128]{0:T(128)S(1)} %iota_add_fusion, f32[1024]{0:T(1024)S(1)} %get-tuple-element.15, f32[1024]{0:T(1024)S(1)} %get-tuple-element.16), kind=kLoop, calls=%fused_computation.23 | loop fusion | flops 2097152 | bytes 1057280 | tf_op jit(solution)/shard_map/mul | solution.py:44
  11.4 0.6 fusion.5
  12.4 0.2 reshape.90
  12.6 9.7 %all_to_all.30 = f32[4,1,3072]{2,1,0:T(1,128)S(1)} all-to-all(f32[4,1,3072]{2,1,0:T(1,128)S(1)} %reshape.90), channel_id=1, replica_groups=mesh['ca'=16,'cb'=8,'win'=4] {'win'}, dimensions={0} | all-to-all | bytes 98304 | tf_op jit(solution)/shard_map/all_to_all | solution.py:100
  22.3 0.5 broadcast.84
  22.8 0.8 reduce
  23.6 0.3 reshape.91
  24.0 20.2 %all_to_all.31 = f32[8,48,256]{2,1,0:T(8,128)S(1)} all-to-all(f32[8,48,256]{2,1,0:T(8,128)S(1)} %broadcast_in_dim.24), channel_id=1, replica_groups=mesh['ca'=16,'cb'=8,'win'=4] {'cb'}, dimensions={0} | all-to-all | bytes 786432 | tf_op jit(solution)/shard_map/all_to_all | solution.py:34
  44.3 1.0 broadcast_in_dim.23
  45.2 11.7 %all-to-all-start.1 = ((f32[16,48,256]{2,1,0:T(8,128)}), f32[16,48,256]{2,1,0:T(8,128)S(1)}, u32[]{:S(2)}, u32[]{:S(2)}) async-start(f32[16,48,256]{2,1,0:T(8,128)} %broadcast_in_dim.23), calls=%async_computation.1 | async-start | bytes 1572864 | tf_op jit(solution)/shard_map/all_to_all | solution.py:34
  56.9 0.4 copy.30
  57.3 0.3 reshape_reshape.3
  57.9 20.3 %all-to-all-done.1 = f32[16,48,256]{2,1,0:T(8,128)S(1)} async-done(((f32[16,48,256]{2,1,0:T(8,128)}), f32[16,48,256]{2,1,0:T(8,128)S(1)}, u32[]{:S(2)}, u32[]{:S(2)}) %all-to-all-start.1) | async-done | bytes 786464 | tf_op jit(solution)/shard_map/all_to_all | solution.py:34
  78.2 2.1 %multiply_convert_fusion = bf16[768,768]{1,0:T(8,128)(2,1)S(1)} fusion(f32[768,256]{1,0:T(8,128)S(1)} %bitcast.39, f32[384,256]{1,0:T(8,128)S(1)} %copy.31, f32[384,256]{1,0:T(8,128)S(1)} %bitcast.38), kind=kOutput, calls=%fused_computation | convolution fusion | flops 1813315584 | bytes 2752512 | tf_op jit(solution)/shard_map/ik,jk->ij/dot_general | solution.py:107
  80.3 31.7 %all_to_all.32 = bf16[16,48,768]{2,1,0:T(8,128)(2,1)S(1)} all-to-all(bf16[16,48,768]{2,1,0:T(8,128)(2,1)S(1)} %bitcast.37), channel_id=1, replica_groups=mesh['ca'=16,'cb'=8,'win'=4] {'ca'}, dimensions={0} | all-to-all | bytes 2359296 | tf_op jit(solution)/shard_map/all_to_all | solution.py:110
  111.9 0.3 reshape.89
  112.2 0.4 copy.34
  112.6 1.4 %broadcast_in_dim_reshape.2 = bf16[1,2,48,6144]{3,2,1,0:T(8,128)(2,1)} reshape(bf16[2,48,16,384]{3,2,1,0:T(8,128)(2,1)S(1)} %bitcast.36) | data formatting | bytes 2359296 | tf_op jit(solution)/shard_map/broadcast_in_dim;reshape | solution.py:113
  (25 shorter events, 1.4 us)
Async XLA Ops:
  0.0 11.1 %copy-start = (bf16[48,1,1024]{2,0,1:T(8,128)(2,1)S(1)}, bf16[48,1,1024]{2,0,1:T(8,128)(2,1)}, u32[]{:S(2)}) copy-start(bf16[48,1,1024]{2,0,1:T(8,128)(2,1)} %param.4) | copy-start | bytes 294916
  0.0 10.9 %copy-start.1 = (s32[48]{0:T(128)S(1)}, s32[48]{0:T(128)}, u32[]{:S(2)}) copy-start(s32[48]{0:T(128)} %param.7) | copy-start | bytes 580
  0.8 10.3 %collective-permute-start = (bf16[8,1,1024]{2,0,1:T(8,128)(2,1)S(1)}, bf16[8,1,1024]{2,0,1:T(8,128)(2,1)S(1)}, u32[]{:S(2)}, u32[]{:S(2)}) collective-permute-start(bf16[8,1,1024]{2,0,1:T(8,128)(2,1)S(1)} %get-tuple-element.9), channel_id=1, source_target_pairs={{0,4},{4,8},{8,12},{12,16},{16,20},{20,24},{24,28},{28,32},{32,36}... | collective-permute-start | bytes 49160 | tf_op jit(solution)/shard_map/ppermute | solution.py:26
  4.8 6.3 %collective-permute-start.1 = (bf16[8,1,1024]{2,0,1:T(8,128)(2,1)S(1)}, bf16[8,1,1024]{2,0,1:T(8,128)(2,1)S(1)}, u32[]{:S(2)}, u32[]{:S(2)}) collective-permute-start(bf16[8,1,1024]{2,0,1:T(8,128)(2,1)S(1)} %get-tuple-element.10), channel_id=1, source_target_pairs={{4,0},{8,4},{12,8},{16,12},{20,16},{24,20},{28,24},{32,28},{36,32}... | collective-permute-start | bytes 49160 | tf_op jit(solution)/shard_map/ppermute | solution.py:27
  45.2 32.9 %all-to-all-start.1 = ((f32[16,48,256]{2,1,0:T(8,128)}), f32[16,48,256]{2,1,0:T(8,128)S(1)}, u32[]{:S(2)}, u32[]{:S(2)}) async-start(f32[16,48,256]{2,1,0:T(8,128)} %broadcast_in_dim.23), calls=%async_computation.1 | async-start | bytes 1572864 | tf_op jit(solution)/shard_map/all_to_all | solution.py:34

commit v5 on v4

--- a/solution.py
+++ b/solution.py
@@ -101,14 +101,17 @@
     windows = banded.shape[1]
     spectra_block = banded.reshape(local_rows, -1)
     inverse_count = 1.0 / (spectra_block.shape[1] // 2)
-    col_set = gather_blocks(spectra_block, "cb")
-    row_set = gather_blocks(spectra_block, "ca")
+    chan_size = group_a * group_b
+    pairs = [((dst % group_b) * group_a + dst // group_b, dst) for dst in range(chan_size)]
+    placed = lax.ppermute(spectra_block, CHAN, pairs)
+    row_set = gather_blocks(spectra_block, "cb")
+    col_set = gather_blocks(placed, "ca")
     operands = jnp.concatenate([col_set, swapped_parts(col_set, windows)], axis=0)
     product = jnp.einsum("ik,jk->ij", row_set, operands, precision=lax.Precision.HIGHEST)
     product = (product * inverse_count).astype(jnp.bfloat16)
-    product = product.reshape(group_a, local_rows, operands.shape[0])
-    mine = lax.all_to_all(product, "ca", split_axis=0, concat_axis=0, tiled=True)
-    mine = mine.reshape(group_a, local_rows, 2, col_set.shape[0])
+    product = product.reshape(group_b, local_rows, operands.shape[0])
+    mine = lax.all_to_all(product, "cb", split_axis=0, concat_axis=0, tiled=True)
+    mine = mine.reshape(group_b, local_rows, 2, col_set.shape[0])
     cross_spectra = mine.transpose(2, 1, 0, 3).reshape(2, local_rows, -1)
     return cross_spectra[None]
 

time: 116 us -> 150 us (1.29)
  the two profiles are of different devices: /device:TPU:1 before, /device:TPU:132 now
where the time goes in v5:
time: 150 us
  starting transfers between devices  50.6 us (34%)
  blocking collectives  41.8 us (28%)
  waiting for transfers between devices  35.7 us (24%)
  local copies, waits for them, and re-layouts  10.3 us (7%)
  other arithmetic  6.78 us (5%)
  matrix products  4.13 us (3%)
    all_to_all x2, starting transfers between devices, gather_blocks(): lax.all_to_all(copies, axis, split_axis=0, concat_axis=0, tiled=True)  37.7 us
    all_to_all x1, blocking collectives, body(): lax.all_to_all(product, 'cb', split_axis=0, concat_axis=0, tiled=True)  34.3 us
    all_to_all x2, waiting for transfers between devices, gather_blocks(): lax.all_to_all(copies, axis, split_axis=0, concat_axis=0, tiled=True)  30.5 us
    all_to_all x1, blocking collectives, body(): lax.all_to_all(whitened, 'win', split_axis=3, concat_axis=1, tiled=True)  7.48 us
    ppermute x1, starting transfers between devices, with_halo(): after = lax.ppermute(initial, CHAN, down)  5.37 us
    ppermute x1, waiting for transfers between devices, body(): placed = lax.ppermute(spectra_block, CHAN, pairs)  5.26 us
    ppermute x1, starting transfers between devices, body(): placed = lax.ppermute(spectra_block, CHAN, pairs)  4.12 us
    ppermute x1, starting transfers between devices, with_halo(): before = lax.ppermute(last, CHAN, up)  3.47 us
  transfers between devices with their start and end apart: 5, of which 3 were waited for; matrix products, arithmetic and copies ran while one was open for 7% of the time, Pallas kernels for 0%

profile of v5, /device:TPU:132, one launch (start us, length us, event | category | flops | bytes accessed | tf_op | source)
XLA Modules:
  0.0 149.6 jit_solution(9891957391374980356)
XLA Ops:
  0.7 3.5 %collective-permute-start = (bf16[8,1,1024]{2,0,1:T(8,128)(2,1)S(1)}, bf16[8,1,1024]{2,0,1:T(8,128)(2,1)S(1)}, u32[]{:S(2)}, u32[]{:S(2)}) collective-permute-start(bf16[8,1,1024]{2,0,1:T(8,128)(2,1)S(1)} %get-tuple-element.9), channel_id=1, source_target_pairs={{0,4},{4,8},{8,12},{12,16},{16,20},{20,24},{24,28},{28,32},{32,36}... | collective-permute-start | bytes 49160 | tf_op jit(solution)/shard_map/ppermute | solution.py:26
  4.2 5.4 %collective-permute-start.1 = (bf16[8,1,1024]{2,0,1:T(8,128)(2,1)S(1)}, bf16[8,1,1024]{2,0,1:T(8,128)(2,1)S(1)}, u32[]{:S(2)}, u32[]{:S(2)}) collective-permute-start(bf16[8,1,1024]{2,0,1:T(8,128)(2,1)S(1)} %get-tuple-element.10), channel_id=1, source_target_pairs={{4,0},{8,4},{12,8},{16,12},{20,16},{24,20},{28,24},{32,28},{36,32}... | collective-permute-start | bytes 49160 | tf_op jit(solution)/shard_map/ppermute | solution.py:27
  9.7 0.8 pad_dynamic-slice_fusion
  10.5 0.9 select_reduce_fusion
  11.4 0.8 broadcast_compare_fusion
  12.3 2.1 %cosine_multiply_fusion = (f32[1024,128]{1,0:T(8,128)S(1)}, f32[1024,128]{1,0:T(8,128)S(1)}) fusion(s32[128]{0:T(128)S(1)} %iota_add_fusion, f32[1024]{0:T(1024)S(1)} %get-tuple-element.15, f32[1024]{0:T(1024)S(1)} %get-tuple-element.16), kind=kLoop, calls=%fused_computation.25 | loop fusion | flops 2097152 | bytes 1057280 | tf_op jit(solution)/shard_map/mul | solution.py:44
  14.4 0.8 convert_reduce_fusion.1
  15.3 1.2 fusion.7
  17.7 7.5 %all_to_all.30 = f32[4,1,3072]{2,1,0:T(1,128)S(1)} all-to-all(f32[4,1,3072]{2,1,0:T(1,128)S(1)} %reshape.93), channel_id=1, replica_groups=mesh['ca'=16,'cb'=8,'win'=4] {'win'}, dimensions={0} | all-to-all | bytes 98304 | tf_op jit(solution)/shard_map/all_to_all | solution.py:100
  25.7 0.8 reduce
  26.8 4.1 %collective-permute-start.2 = (f32[48,256]{0,1:T(8,128)S(1)}, f32[48,256]{0,1:T(8,128)S(1)}, u32[]{:S(2)}, u32[]{:S(2)}) collective-permute-start(f32[48,256]{0,1:T(8,128)S(1)} %bitcast.41), channel_id=1, source_target_pairs={{0,0},{64,4},{128,8},{192,12},{256,16},{320,20},{384,24},{448,28},... | collective-permute-start | bytes 147464 | tf_op jit(solution)/shard_map/ppermute | solution.py:106
  30.9 5.3 %collective-permute-done.2 = f32[48,256]{0,1:T(8,128)S(1)} collective-permute-done((f32[48,256]{0,1:T(8,128)S(1)}, f32[48,256]{0,1:T(8,128)S(1)}, u32[]{:S(2)}, u32[]{:S(2)}) %collective-permute-start.2) | collective-permute-done | bytes 49184 | tf_op jit(solution)/shard_map/ppermute | solution.py:106
  36.2 1.0 broadcast_in_dim.24
  37.2 33.2 %all-to-all-start.2 = ((f32[16,48,256]{2,1,0:T(8,128)}), f32[16,48,256]{2,1,0:T(8,128)S(1)}, u32[]{:S(2)}, u32[]{:S(2)}) async-start(f32[16,48,256]{2,1,0:T(8,128)} %broadcast_in_dim.24), calls=%async_computation.2 | async-start | bytes 1572864 | tf_op jit(solution)/shard_map/all_to_all | solution.py:34
  70.4 20.2 %all-to-all-done.2 = f32[16,48,256]{2,1,0:T(8,128)S(1)} async-done(((f32[16,48,256]{2,1,0:T(8,128)}), f32[16,48,256]{2,1,0:T(8,128)S(1)}, u32[]{:S(2)}, u32[]{:S(2)}) %all-to-all-start.2) | async-done | bytes 786464 | tf_op jit(solution)/shard_map/all_to_all | solution.py:34
  90.6 0.8 broadcast_in_dim.23
  91.4 4.5 %all-to-all-start.1 = ((f32[8,48,256]{2,1,0:T(8,128)}), f32[8,48,256]{2,1,0:T(8,128)S(1)}, u32[]{:S(2)}, u32[]{:S(2)}) async-start(f32[8,48,256]{2,1,0:T(8,128)} %broadcast_in_dim.23), calls=%async_computation.1 | async-start | bytes 786432 | tf_op jit(solution)/shard_map/all_to_all | solution.py:34
  95.9 1.3 copy.30
  97.2 1.8 %reshape_reshape.3 = f32[768,4,2,32]{0,3,2,1:T(8,128)} reshape(f32[16,48,256]{1,0,2:T(8,128)S(1)} %copy.30) | data formatting | bytes 1572864 | tf_op jit(solution)/shard_map/reshape;reshape | solution.py:54
  99.0 1.2 slice_negate_fusion
  100.5 10.3 %all-to-all-done.1 = f32[8,48,256]{2,1,0:T(8,128)S(1)} async-done(((f32[8,48,256]{2,1,0:T(8,128)}), f32[8,48,256]{2,1,0:T(8,128)S(1)}, u32[]{:S(2)}, u32[]{:S(2)}) %all-to-all-start.1) | async-done | bytes 393248 | tf_op jit(solution)/shard_map/all_to_all | solution.py:34
  110.8 2.1 %fusion = bf16[384,1536]{1,0:T(8,128)(2,1)S(1)} fusion(f32[384,256]{1,0:T(8,128)S(1)} %bitcast.40, f32[768,256]{1,0:T(8,128)S(1)} %copy.31, f32[768,256]{1,0:T(8,128)S(1)} %bitcast.36), kind=kOutput, calls=%fused_computation.1 | convolution fusion | flops 1813512192 | bytes 3145728 | tf_op jit(solution)/shard_map/ik,jk->ij/dot_general | solution.py:110
  112.9 34.3 %all_to_all.31 = bf16[8,48,1536]{2,1,0:T(8,128)(2,1)S(1)} all-to-all(bf16[8,48,1536]{2,1,0:T(8,128)(2,1)S(1)} %bitcast.37), channel_id=1, replica_groups=mesh['ca'=16,'cb'=8,'win'=4] {'cb'}, dimensions={0} | all-to-all | bytes 2359296 | tf_op jit(solution)/shard_map/all_to_all | solution.py:113
  148.2 1.4 broadcast_in_dim_reshape.4
  (25 shorter events, 4.3 us)
Async XLA Ops:
  0.7 14.5 %collective-permute-start = (bf16[8,1,1024]{2,0,1:T(8,128)(2,1)S(1)}, bf16[8,1,1024]{2,0,1:T(8,128)(2,1)S(1)}, u32[]{:S(2)}, u32[]{:S(2)}) collective-permute-start(bf16[8,1,1024]{2,0,1:T(8,128)(2,1)S(1)} %get-tuple-element.9), channel_id=1, source_target_pairs={{0,4},{4,8},{8,12},{12,16},{16,20},{20,24},{24,28},{28,32},{32,36}... | collective-permute-start | bytes 49160 | tf_op jit(solution)/shard_map/ppermute | solution.py:26
  4.2 11.1 %collective-permute-start.1 = (bf16[8,1,1024]{2,0,1:T(8,128)(2,1)S(1)}, bf16[8,1,1024]{2,0,1:T(8,128)(2,1)S(1)}, u32[]{:S(2)}, u32[]{:S(2)}) collective-permute-start(bf16[8,1,1024]{2,0,1:T(8,128)(2,1)S(1)} %get-tuple-element.10), channel_id=1, source_target_pairs={{4,0},{8,4},{12,8},{16,12},{20,16},{24,20},{28,24},{32,28},{36,32}... | collective-permute-start | bytes 49160 | tf_op jit(solution)/shard_map/ppermute | solution.py:27
  26.8 9.4 %collective-permute-start.2 = (f32[48,256]{0,1:T(8,128)S(1)}, f32[48,256]{0,1:T(8,128)S(1)}, u32[]{:S(2)}, u32[]{:S(2)}) collective-permute-start(f32[48,256]{0,1:T(8,128)S(1)} %bitcast.41), channel_id=1, source_target_pairs={{0,0},{64,4},{128,8},{192,12},{256,16},{320,20},{384,24},{448,28},... | collective-permute-start | bytes 147464 | tf_op jit(solution)/shard_map/ppermute | solution.py:106
  37.2 53.5 %all-to-all-start.2 = ((f32[16,48,256]{2,1,0:T(8,128)}), f32[16,48,256]{2,1,0:T(8,128)S(1)}, u32[]{:S(2)}, u32[]{:S(2)}) async-start(f32[16,48,256]{2,1,0:T(8,128)} %broadcast_in_dim.24), calls=%async_computation.2 | async-start | bytes 1572864 | tf_op jit(solution)/shard_map/all_to_all | solution.py:34
  91.4 19.4 %all-to-all-start.1 = ((f32[8,48,256]{2,1,0:T(8,128)}), f32[8,48,256]{2,1,0:T(8,128)S(1)}, u32[]{:S(2)}, u32[]{:S(2)}) async-start(f32[8,48,256]{2,1,0:T(8,128)} %broadcast_in_dim.23), calls=%async_computation.1 | async-start | bytes 786432 | tf_op jit(solution)/shard_map/all_to_all | solution.py:34

commit v6 on v4

--- a/solution.py
+++ b/solution.py
@@ -10,11 +10,12 @@
 SMOOTH_BINS = 4
 MOST_REACH = 8
 ROW_GROUP = 8
+Z_GROUP = 4
 
 
 FLOOR_POWER = 0.01
 
-CHAN = ("ca", "cb")
+CHAN = ("cx", "cz", "cb")
 
 
 def with_halo(x, width):
@@ -59,8 +60,9 @@
 def body(strain, seg_ids, dead, radius):
     local_rows = strain.shape[0]
     group_b = lax.axis_size("cb")
-    group_a = lax.axis_size("ca")
-    device = lax.axis_index("ca") * group_b + lax.axis_index("cb")
+    group_x = lax.axis_size("cx")
+    group_z = lax.axis_size("cz")
+    device = (lax.axis_index("cx") * group_z + lax.axis_index("cz")) * group_b + lax.axis_index("cb")
     seg_padded = jnp.pad(seg_ids, (MOST_REACH, MOST_REACH), constant_values=-1)
     near_segs = lax.dynamic_slice_in_dim(
         seg_padded, device * local_rows, local_rows + 2 * MOST_REACH
@@ -102,21 +104,24 @@
     spectra_block = banded.reshape(local_rows, -1)
     inverse_count = 1.0 / (spectra_block.shape[1] // 2)
     col_set = gather_blocks(spectra_block, "cb")
-    row_set = gather_blocks(spectra_block, "ca")
+    row_set = gather_blocks(gather_blocks(spectra_block, "cz"), "cx")
     operands = jnp.concatenate([col_set, swapped_parts(col_set, windows)], axis=0)
     product = jnp.einsum("ik,jk->ij", row_set, operands, precision=lax.Precision.HIGHEST)
     product = (product * inverse_count).astype(jnp.bfloat16)
-    product = product.reshape(group_a, local_rows, operands.shape[0])
-    mine = lax.all_to_all(product, "ca", split_axis=0, concat_axis=0, tiled=True)
-    mine = mine.reshape(group_a, local_rows, 2, col_set.shape[0])
-    cross_spectra = mine.transpose(2, 1, 0, 3).reshape(2, local_rows, -1)
+    product = product.reshape(group_x, group_z, local_rows, operands.shape[0])
+    stage = lax.all_to_all(product, "cx", split_axis=0, concat_axis=0, tiled=True)
+    stage = stage.transpose(1, 0, 2, 3)
+    mine = lax.all_to_all(stage, "cz", split_axis=0, concat_axis=0, tiled=True)
+    mine = mine.reshape(group_z, group_x, local_rows, 2, col_set.shape[0])
+    cross_spectra = mine.transpose(3, 2, 1, 0, 4).reshape(2, local_rows, -1)
     return cross_spectra[None]
 
 
 def solution(mesh):
     chan_size = mesh.shape["chan"]
-    grid = mesh.devices.reshape(chan_size // ROW_GROUP, ROW_GROUP, mesh.shape["win"])
-    sub_mesh = Mesh(grid, ("ca", "cb", "win"))
+    outer = chan_size // ROW_GROUP
+    grid = mesh.devices.reshape(outer // Z_GROUP, Z_GROUP, ROW_GROUP, mesh.shape["win"])
+    sub_mesh = Mesh(grid, ("cx", "cz", "cb", "win"))
     return jax.shard_map(
         body,
         mesh=sub_mesh,

time: 116 us -> 130 us (1.12)
  blocking collectives: 61.6 us -> 94.9 us
  waiting for transfers between devices: 20.3 us -> 7.36 us
  starting transfers between devices: 17 us -> 9.3 us
    all_to_all x1 -> x2, blocking collectives: 31.7 us -> 50.2 us  [the longest x1 37.3 us: body(): mine = lax.all_to_all(stage, 'cz', split_axis=0, concat_axis=0, tiled=True)]
    all_to_all x1 -> x2, blocking collectives: 20.2 us -> 35 us  [gather_blocks(): lax.all_to_all(copies, axis, split_axis=0, concat_axis=0, tiled=True)]
    all_to_all x1, waiting for transfers between devices: 20.3 us -> 7.35 us  [gather_blocks(): lax.all_to_all(copies, axis, split_axis=0, concat_axis=0, tiled=True)]
    all_to_all x1, starting transfers between devices: 11.7 us -> 3.99 us  [gather_blocks(): lax.all_to_all(copies, axis, split_axis=0, concat_axis=0, tiled=True)]
where the time goes in v6:
time: 130 us; the launch traced here: 128 us
  blocking collectives  94.9 us (73%)
  starting transfers between devices  9.3 us (7%)
  local copies, waits for them, and re-layouts  7.73 us (6%)
  waiting for transfers between devices  7.36 us (6%)
  other arithmetic  4.94 us (4%)
  matrix products  3.12 us (2%)
    all_to_all x1, blocking collectives, body(): mine = lax.all_to_all(stage, 'cz', split_axis=0, concat_axis=0, tiled=True)  37.3 us
    all_to_all x2, blocking collectives, gather_blocks(): lax.all_to_all(copies, axis, split_axis=0, concat_axis=0, tiled=True)  35 us
    all_to_all x1, blocking collectives, body(): lax.all_to_all(product, 'cx', split_axis=0, concat_axis=0, tiled=True)  12.9 us
    all_to_all x1, blocking collectives, body(): lax.all_to_all(whitened, 'win', split_axis=3, concat_axis=1, tiled=True)  9.71 us
    all_to_all x1, waiting for transfers between devices, gather_blocks(): lax.all_to_all(copies, axis, split_axis=0, concat_axis=0, tiled=True)  7.35 us
    ppermute x1, starting transfers between devices, with_halo(): before = lax.ppermute(last, CHAN, up)  4.02 us
    all_to_all x1, starting transfers between devices, gather_blocks(): lax.all_to_all(copies, axis, split_axis=0, concat_axis=0, tiled=True)  3.99 us
  transfers between devices with their start and end apart: 3, of which 1 were waited for; matrix products, arithmetic and copies ran while one was open for 5% of the time, Pallas kernels for 0%

profile of v6, /device:TPU:1, one launch (start us, length us, event | category | flops | bytes accessed | tf_op | source)
XLA Modules:
  0.0 127.6 jit_solution(13217469633632056954)
XLA Ops:
  0.0 0.8 fusion.35
  0.8 4.0 %collective-permute-start = (bf16[8,1,1024]{2,0,1:T(8,128)(2,1)S(1)}, bf16[8,1,1024]{2,0,1:T(8,128)(2,1)S(1)}, u32[]{:S(2)}, u32[]{:S(2)}) collective-permute-start(bf16[8,1,1024]{2,0,1:T(8,128)(2,1)S(1)} %get-tuple-element.9), channel_id=1, source_target_pairs={{0,4},{4,8},{8,12},{12,16},{16,20},{20,24},{24,28},{28,32},{32,36}... | collective-permute-start | bytes 49160 | tf_op jit(solution)/shard_map/ppermute | solution.py:27
  4.8 1.3 %collective-permute-start.1 = (bf16[8,1,1024]{2,0,1:T(8,128)(2,1)S(1)}, bf16[8,1,1024]{2,0,1:T(8,128)(2,1)S(1)}, u32[]{:S(2)}, u32[]{:S(2)}) collective-permute-start(bf16[8,1,1024]{2,0,1:T(8,128)(2,1)S(1)} %get-tuple-element.10), channel_id=1, source_target_pairs={{4,0},{8,4},{12,8},{16,12},{20,16},{24,20},{28,24},{32,28},{36,32}... | collective-permute-start | bytes 49160 | tf_op jit(solution)/shard_map/ppermute | solution.py:28
  6.2 0.8 pad_dynamic-slice_fusion
  7.0 0.9 select_reduce_fusion
  7.9 0.8 broadcast_compare_fusion
  8.8 2.1 %cosine_multiply_fusion = (f32[1024,128]{1,0:T(8,128)S(1)}, f32[1024,128]{1,0:T(8,128)S(1)}) fusion(s32[128]{0:T(128)S(1)} %iota_add_fusion, f32[1024]{0:T(1024)S(1)} %get-tuple-element.15, f32[1024]{0:T(1024)S(1)} %get-tuple-element.16), kind=kLoop, calls=%fused_computation.22 | loop fusion | flops 2097152 | bytes 1057280 | tf_op jit(solution)/shard_map/mul | solution.py:45
  11.4 0.6 fusion.5
  12.6 9.7 %all_to_all.40 = f32[4,1,3072]{2,1,0:T(1,128)S(1)} all-to-all(f32[4,1,3072]{2,1,0:T(1,128)S(1)} %reshape.91), channel_id=1, replica_groups=mesh['cx'=4,'cz'=4,'cb'=8,'win'=4] {'win'}, dimensions={0} | all-to-all | bytes 98304 | tf_op jit(solution)/shard_map/all_to_all | solution.py:102
  22.3 0.5 broadcast.84
  22.8 0.8 reduce
  24.0 20.2 %all_to_all.41 = f32[4,48,256]{2,1,0:T(8,128)S(1)} all-to-all(f32[4,48,256]{2,1,0:T(8,128)S(1)} %broadcast_in_dim.27), channel_id=1, replica_groups=mesh['cx'=4,'cz'=4,'cb'=8,'win'=4] {'cz'}, dimensions={0} | all-to-all | bytes 393216 | tf_op jit(solution)/shard_map/all_to_all | solution.py:35
  44.2 14.8 %all_to_all.42 = f32[8,48,256]{2,1,0:T(8,128)S(1)} all-to-all(f32[8,48,256]{2,1,0:T(8,128)S(1)} %broadcast_in_dim.30), channel_id=1, replica_groups=mesh['cx'=4,'cz'=4,'cb'=8,'win'=4] {'cb'}, dimensions={0} | all-to-all | bytes 786432 | tf_op jit(solution)/shard_map/all_to_all | solution.py:35
  59.0 0.9 broadcast_in_dim.29
  60.0 4.0 %all-to-all-start.2 = ((f32[4,192,256]{2,1,0:T(8,128)}), f32[4,192,256]{2,1,0:T(8,128)S(1)}, u32[]{:S(2)}, u32[]{:S(2)}) async-start(f32[4,192,256]{2,1,0:T(8,128)} %broadcast_in_dim.29), calls=%async_computation.2 | async-start | bytes 1572864 | tf_op jit(solution)/shard_map/all_to_all | solution.py:35
  63.9 0.4 copy.40
  64.4 0.3 reshape_reshape.3
  64.9 7.4 %all-to-all-done.2 = f32[4,192,256]{2,1,0:T(8,128)S(1)} async-done(((f32[4,192,256]{2,1,0:T(8,128)}), f32[4,192,256]{2,1,0:T(8,128)S(1)}, u32[]{:S(2)}, u32[]{:S(2)}) %all-to-all-start.2) | async-done | bytes 786464 | tf_op jit(solution)/shard_map/all_to_all | solution.py:35
  72.3 2.1 %multiply_convert_fusion = bf16[768,768]{1,0:T(8,128)(2,1)S(1)} fusion(f32[768,256]{1,0:T(8,128)S(1)} %bitcast.40, f32[384,256]{1,0:T(8,128)S(1)} %copy.41, f32[384,256]{1,0:T(8,128)S(1)} %bitcast.39), kind=kOutput, calls=%fused_computation | convolution fusion | flops 1813315584 | bytes 2752512 | tf_op jit(solution)/shard_map/ik,jk->ij/dot_general | solution.py:109
  74.4 12.9 %all_to_all.43 = bf16[4,4,48,768]{3,2,1,0:T(8,128)(2,1)S(1)} all-to-all(bf16[4,4,48,768]{3,2,1,0:T(8,128)(2,1)S(1)} %bitcast.38), channel_id=1, replica_groups=mesh['cx'=4,'cz'=4,'cb'=8,'win'=4] {'cx'}, dimensions={0} | all-to-all | bytes 2359296 | tf_op jit(solution)/shard_map/all_to_all | solution.py:112
  87.4 37.3 %all_to_all.44 = bf16[4,4,48,768]{3,2,1,0:T(8,128)(2,1)S(1)} all-to-all(bf16[4,4,48,768]{3,2,1,0:T(8,128)(2,1)S(1)} %copy.42), channel_id=1, replica_groups=mesh['cx'=4,'cz'=4,'cb'=8,'win'=4] {'cz'}, dimensions={0} | all-to-all | bytes 2359296 | tf_op jit(solution)/shard_map/all_to_all | solution.py:114
  124.7 0.3 reshape.90
  125.0 0.9 copy.43
  125.9 1.7 %broadcast_in_dim_reshape.2 = bf16[1,2,48,6144]{3,2,1,0:T(8,128)(2,1)} reshape(bf16[2,48,4,4,384]{4,3,2,1,0:T(4,128)(2,1)S(1)} %copy.43) | data formatting | bytes 2359296 | tf_op jit(solution)/shard_map/broadcast_in_dim;reshape | solution.py:117
  (29 shorter events, 1.9 us)
Async XLA Ops:
  0.0 11.1 %copy-start = (bf16[48,1,1024]{2,0,1:T(8,128)(2,1)S(1)}, bf16[48,1,1024]{2,0,1:T(8,128)(2,1)}, u32[]{:S(2)}) copy-start(bf16[48,1,1024]{2,0,1:T(8,128)(2,1)} %param.4) | copy-start | bytes 294916
  0.0 10.9 %copy-start.1 = (s32[48]{0:T(128)S(1)}, s32[48]{0:T(128)}, u32[]{:S(2)}) copy-start(s32[48]{0:T(128)} %param.7) | copy-start | bytes 580
  0.8 10.3 %collective-permute-start = (bf16[8,1,1024]{2,0,1:T(8,128)(2,1)S(1)}, bf16[8,1,1024]{2,0,1:T(8,128)(2,1)S(1)}, u32[]{:S(2)}, u32[]{:S(2)}) collective-permute-start(bf16[8,1,1024]{2,0,1:T(8,128)(2,1)S(1)} %get-tuple-element.9), channel_id=1, source_target_pairs={{0,4},{4,8},{8,12},{12,16},{16,20},{20,24},{24,28},{28,32},{32,36}... | collective-permute-start | bytes 49160 | tf_op jit(solution)/shard_map/ppermute | solution.py:27
  4.8 6.3 %collective-permute-start.1 = (bf16[8,1,1024]{2,0,1:T(8,128)(2,1)S(1)}, bf16[8,1,1024]{2,0,1:T(8,128)(2,1)S(1)}, u32[]{:S(2)}, u32[]{:S(2)}) collective-permute-start(bf16[8,1,1024]{2,0,1:T(8,128)(2,1)S(1)} %get-tuple-element.10), channel_id=1, source_target_pairs={{4,0},{8,4},{12,8},{16,12},{20,16},{24,20},{28,24},{32,28},{36,32}... | collective-permute-start | bytes 49160 | tf_op jit(solution)/shard_map/ppermute | solution.py:28
  60.0 12.3 %all-to-all-start.2 = ((f32[4,192,256]{2,1,0:T(8,128)}), f32[4,192,256]{2,1,0:T(8,128)S(1)}, u32[]{:S(2)}, u32[]{:S(2)}) async-start(f32[4,192,256]{2,1,0:T(8,128)} %broadcast_in_dim.29), calls=%async_computation.2 | async-start | bytes 1572864 | tf_op jit(solution)/shard_map/all_to_all | solution.py:35

commit v7 on v4

--- a/solution.py
+++ b/solution.py
@@ -10,6 +10,7 @@
 SMOOTH_BINS = 4
 MOST_REACH = 8
 ROW_GROUP = 8
+COL_PAD = 128
 
 
 FLOOR_POWER = 0.01
@@ -33,6 +34,12 @@
     copies = jnp.broadcast_to(block[None], (size,) + block.shape)
     every = lax.all_to_all(copies, axis, split_axis=0, concat_axis=0, tiled=True)
     return every.reshape(-1, block.shape[1])
+
+def gather_offloaded(block, axis, padded_rows):
+    rows = block.shape[0]
+    wide = jnp.pad(block, ((0, padded_rows - rows), (0, 0)))
+    every = lax.all_gather(wide, axis, axis=0, tiled=False)
+    return every[:, :rows].reshape(-1, block.shape[1])
 
 def fourier_table():
     sample_ids = jnp.arange(SAMPLES, dtype=jnp.int32)
@@ -101,7 +108,7 @@
     windows = banded.shape[1]
     spectra_block = banded.reshape(local_rows, -1)
     inverse_count = 1.0 / (spectra_block.shape[1] // 2)
-    col_set = gather_blocks(spectra_block, "cb")
+    col_set = gather_offloaded(spectra_block, "cb", COL_PAD)
     row_set = gather_blocks(spectra_block, "ca")
     operands = jnp.concatenate([col_set, swapped_parts(col_set, windows)], axis=0)
     product = jnp.einsum("ik,jk->ij", row_set, operands, precision=lax.Precision.HIGHEST)

time: 116 us -> 129 us (1.11)
  the two profiles are of different devices: /device:TPU:1 before, /device:TPU:8 now
where the time goes in v7:
time: 129 us
  blocking collectives  44.9 us (35%)
  waiting for transfers between devices  34.1 us (26%)
  starting transfers between devices  18.9 us (15%)
  between operations  13.6 us (11%)
  local copies, waits for them, and re-layouts  9.06 us (7%)
  other arithmetic  4.95 us (4%)
  matrix products  3.13 us (2%)
    all_to_all x1, blocking collectives, body(): lax.all_to_all(product, 'ca', split_axis=0, concat_axis=0, tiled=True)  38.5 us
    all_gather x1, waiting for transfers between devices, gather_offloaded(): every = lax.all_gather(wide, axis, axis=0, tiled=False)  34 us
    all_to_all x1, starting transfers between devices, gather_blocks(): lax.all_to_all(copies, axis, split_axis=0, concat_axis=0, tiled=True)  9.85 us
    all_to_all x1, blocking collectives, body(): lax.all_to_all(whitened, 'win', split_axis=3, concat_axis=1, tiled=True)  6.39 us
    ppermute x1, starting transfers between devices, with_halo(): after = lax.ppermute(initial, CHAN, down)  5.54 us
    ppermute x1, starting transfers between devices, with_halo(): before = lax.ppermute(last, CHAN, up)  3.47 us
  transfers between devices with their start and end apart: 4, of which 1 were waited for; matrix products, arithmetic and copies ran while one was open for 7% of the time, Pallas kernels for 0%

profile of v7, /device:TPU:8, one launch (start us, length us, event | category | flops | bytes accessed | tf_op | source)
XLA Modules:
  0.0 128.6 jit_solution(7720254808124559819)
XLA Ops:
  6.5 0.8 fusion.35
  7.3 3.5 %collective-permute-start = (bf16[8,1,1024]{2,0,1:T(8,128)(2,1)S(1)}, bf16[8,1,1024]{2,0,1:T(8,128)(2,1)S(1)}, u32[]{:S(2)}, u32[]{:S(2)}) collective-permute-start(bf16[8,1,1024]{2,0,1:T(8,128)(2,1)S(1)} %get-tuple-element.9), channel_id=1, source_target_pairs={{0,4},{4,8},{8,12},{12,16},{16,20},{20,24},{24,28},{28,32},{32,36}... | collective-permute-start | bytes 49160 | tf_op jit(solution)/shard_map/ppermute | solution.py:27
  10.8 5.5 %collective-permute-start.1 = (bf16[8,1,1024]{2,0,1:T(8,128)(2,1)S(1)}, bf16[8,1,1024]{2,0,1:T(8,128)(2,1)S(1)}, u32[]{:S(2)}, u32[]{:S(2)}) collective-permute-start(bf16[8,1,1024]{2,0,1:T(8,128)(2,1)S(1)} %get-tuple-element.10), channel_id=1, source_target_pairs={{4,0},{8,4},{12,8},{16,12},{20,16},{24,20},{28,24},{32,28},{36,32}... | collective-permute-start | bytes 49160 | tf_op jit(solution)/shard_map/ppermute | solution.py:28
  16.4 0.8 pad_dynamic-slice_fusion
  17.3 0.9 select_reduce_fusion
  18.2 0.8 broadcast_compare_fusion
  19.0 2.1 %cosine_multiply_fusion = (f32[1024,128]{1,0:T(8,128)S(1)}, f32[1024,128]{1,0:T(8,128)S(1)}) fusion(s32[128]{0:T(128)S(1)} %iota_add_fusion, f32[1024]{0:T(1024)S(1)} %get-tuple-element.15, f32[1024]{0:T(1024)S(1)} %get-tuple-element.16), kind=kLoop, calls=%fused_computation.23 | loop fusion | flops 2097152 | bytes 1057280 | tf_op jit(solution)/shard_map/mul | solution.py:51
  21.6 0.6 fusion.5
  22.9 6.4 %all_to_all.25 = f32[4,1,3072]{2,1,0:T(1,128)S(1)} all-to-all(f32[4,1,3072]{2,1,0:T(1,128)S(1)} %reshape.93), channel_id=1, replica_groups=mesh['ca'=16,'cb'=8,'win'=4] {'win'}, dimensions={0} | all-to-all | bytes 98304 | tf_op jit(solution)/shard_map/all_to_all | solution.py:107
  29.2 0.5 broadcast.86
  29.8 0.8 reduce
  30.5 0.3 reshape.94
  30.8 0.7 pad.9
  31.6 1.0 broadcast_in_dim.21
  32.6 9.9 %all-to-all-start.1 = ((f32[16,48,256]{2,1,0:T(8,128)}), f32[16,48,256]{2,1,0:T(8,128)S(1)}, u32[]{:S(2)}, u32[]{:S(2)}) async-start(f32[16,48,256]{2,1,0:T(8,128)} %broadcast_in_dim.21), calls=%async_computation.1 | async-start | bytes 1572864 | tf_op jit(solution)/shard_map/all_to_all | solution.py:35
  42.4 34.0 %all-gather.3.cloned.1.call-done = f32[1024,256]{0,1:T(8,128)} async-done(((f32[128,256]{0,1:T(8,128)}), f32[1024,256]{0,1:T(8,128)}) %all-gather.3.cloned.1.call-update) | async-done | bytes 1048592 | tf_op jit(solution)/shard_map/all_gather | solution.py:41
  76.5 1.6 %copy.33 = f32[1024,256]{1,0:T(8,128)S(1)} copy(f32[1024,256]{0,1:T(8,128)} %all-gather.3.cloned.1.call-done) | data formatting | bytes 2097152 | tf_op jit(solution)/shard_map/all_gather | solution.py:41
  78.0 0.4 copy.30
  78.5 0.3 reshape_reshape.3
  79.0 2.1 %multiply_convert_fusion = bf16[768,768]{1,0:T(8,128)(2,1)S(1)} fusion(f32[768,256]{1,0:T(8,128)S(1)} %bitcast.40, f32[384,256]{1,0:T(8,128)S(1)} %copy.31, f32[384,256]{1,0:T(8,128)S(1)} %bitcast.39), kind=kOutput, calls=%fused_computation | convolution fusion | flops 1813315584 | bytes 2752512 | tf_op jit(solution)/shard_map/ik,jk->ij/dot_general | solution.py:114
  81.2 38.5 %all_to_all.26 = bf16[16,48,768]{2,1,0:T(8,128)(2,1)S(1)} all-to-all(bf16[16,48,768]{2,1,0:T(8,128)(2,1)S(1)} %bitcast.38), channel_id=1, replica_groups=mesh['ca'=16,'cb'=8,'win'=4] {'ca'}, dimensions={0} | all-to-all | bytes 2359296 | tf_op jit(solution)/shard_map/all_to_all | solution.py:117
  119.6 0.3 reshape.91
  119.9 0.4 copy.35
  120.3 1.4 %broadcast_in_dim_reshape.4 = bf16[1,2,48,6144]{3,2,1,0:T(8,128)(2,1)} reshape(bf16[2,48,16,384]{3,2,1,0:T(8,128)(2,1)S(1)} %bitcast.37) | data formatting | bytes 2359296 | tf_op jit(solution)/shard_map/broadcast_in_dim;reshape | solution.py:120
  (29 shorter events, 1.6 us)
Async XLA Ops:
  6.5 14.9 %copy-start = (bf16[48,1,1024]{2,0,1:T(8,128)(2,1)S(1)}, bf16[48,1,1024]{2,0,1:T(8,128)(2,1)}, u32[]{:S(2)}) copy-start(bf16[48,1,1024]{2,0,1:T(8,128)(2,1)} %param.4) | copy-start | bytes 294916
  6.5 14.6 %copy-start.1 = (s32[48]{0:T(128)S(1)}, s32[48]{0:T(128)}, u32[]{:S(2)}) copy-start(s32[48]{0:T(128)} %param.7) | copy-start | bytes 580
  6.5 69.9 %all-gather.3.cloned.1.call-start = ((), (), s32[]{:S(2)}) async-start(), calls=%async_computation.3 | async-start | bytes 1179648 | tf_op jit(solution)/shard_map/all_gather | solution.py:41
  7.3 14.0 %collective-permute-start = (bf16[8,1,1024]{2,0,1:T(8,128)(2,1)S(1)}, bf16[8,1,1024]{2,0,1:T(8,128)(2,1)S(1)}, u32[]{:S(2)}, u32[]{:S(2)}) collective-permute-start(bf16[8,1,1024]{2,0,1:T(8,128)(2,1)S(1)} %get-tuple-element.9), channel_id=1, source_target_pairs={{0,4},{4,8},{8,12},{12,16},{16,20},{20,24},{24,28},{28,32},{32,36}... | collective-permute-start | bytes 49160 | tf_op jit(solution)/shard_map/ppermute | solution.py:27
  10.8 10.6 %collective-permute-start.1 = (bf16[8,1,1024]{2,0,1:T(8,128)(2,1)S(1)}, bf16[8,1,1024]{2,0,1:T(8,128)(2,1)S(1)}, u32[]{:S(2)}, u32[]{:S(2)}) collective-permute-start(bf16[8,1,1024]{2,0,1:T(8,128)(2,1)S(1)} %get-tuple-element.10), channel_id=1, source_target_pairs={{4,0},{8,4},{12,8},{16,12},{20,16},{24,20},{28,24},{32,28},{36,32}... | collective-permute-start | bytes 49160 | tf_op jit(solution)/shard_map/ppermute | solution.py:28
  32.6 46.5 %all-to-all-start.1 = ((f32[16,48,256]{2,1,0:T(8,128)}), f32[16,48,256]{2,1,0:T(8,128)S(1)}, u32[]{:S(2)}, u32[]{:S(2)}) async-start(f32[16,48,256]{2,1,0:T(8,128)} %broadcast_in_dim.21), calls=%async_computation.1 | async-start | bytes 1572864 | tf_op jit(solution)/shard_map/all_to_all | solution.py:35
Sparse Core Ops, SparseCore 0:
  31.6 44.7 all-gather.2

commit v8 on v6

--- a/solution.py
+++ b/solution.py
@@ -103,17 +103,15 @@
     windows = banded.shape[1]
     spectra_block = banded.reshape(local_rows, -1)
     inverse_count = 1.0 / (spectra_block.shape[1] // 2)
-    col_set = gather_blocks(spectra_block, "cb")
-    row_set = gather_blocks(gather_blocks(spectra_block, "cz"), "cx")
+    col_set = gather_blocks(gather_blocks(spectra_block, "cb"), "cz")
+    row_set = gather_blocks(spectra_block, "cx")
     operands = jnp.concatenate([col_set, swapped_parts(col_set, windows)], axis=0)
     product = jnp.einsum("ik,jk->ij", row_set, operands, precision=lax.Precision.HIGHEST)
     product = (product * inverse_count).astype(jnp.bfloat16)
-    product = product.reshape(group_x, group_z, local_rows, operands.shape[0])
-    stage = lax.all_to_all(product, "cx", split_axis=0, concat_axis=0, tiled=True)
-    stage = stage.transpose(1, 0, 2, 3)
-    mine = lax.all_to_all(stage, "cz", split_axis=0, concat_axis=0, tiled=True)
-    mine = mine.reshape(group_z, group_x, local_rows, 2, col_set.shape[0])
-    cross_spectra = mine.transpose(3, 2, 1, 0, 4).reshape(2, local_rows, -1)
+    product = product.reshape(group_x, local_rows, operands.shape[0])
+    mine = lax.all_to_all(product, "cx", split_axis=0, concat_axis=0, tiled=True)
+    mine = mine.reshape(group_x, local_rows, 2, col_set.shape[0])
+    cross_spectra = mine.transpose(2, 1, 0, 3).reshape(2, local_rows, -1)
     return cross_spectra[None]
 
 

time: 130 us -> 127 us (0.977)
  waiting for transfers between devices: 7.36 us -> 0.62 us
  local copies, waits for them, and re-layouts: 7.73 us -> 11.6 us
  blocking collectives: 94.9 us -> 92.7 us
    all_to_all x1 -> x0, blocking collectives: 37.3 us -> none  [body(): mine = lax.all_to_all(stage, 'cz', split_axis=0, concat_axis=0, tiled=True)]
    all_to_all x2, blocking collectives: 35 us -> 66.2 us  [gather_blocks(): lax.all_to_all(copies, axis, split_axis=0, concat_axis=0, tiled=True)]
    all_to_all x1, waiting for transfers between devices: 7.35 us -> 0.62 us  [gather_blocks(): lax.all_to_all(copies, axis, split_axis=0, concat_axis=0, tiled=True)]
    all_to_all x1, blocking collectives: 12.9 us -> 16.9 us  [body(): lax.all_to_all(product, 'cx', split_axis=0, concat_axis=0, tiled=True)]
    all_to_all x1, local copies, waits for them, and re-layouts: 0.41 us -> 2.17 us  [gather_blocks(): lax.all_to_all(copies, axis, split_axis=0, concat_axis=0, tiled=True)]
    another operation x1, local copies, waits for them, and re-layouts: 0.31 us -> 1.92 us  [swapped_parts(): parts = flat.reshape(flat.shape[:-1] + (windows, 2, -1))]
    reshape x2 -> x3, local copies, waits for them, and re-layouts: 0.45 us -> 1.99 us  [the longest x2 1.8 us: body(): mine = mine.reshape(group_x, local_rows, 2, col_set.shape[0])]
  transfers between devices with their start and end apart: 3 -> 3, of which waited for: 1 -> 1; matrix products, arithmetic and copies ran while one was open for 5% -> 8% of each run, Pallas kernels for 0% -> 0%
where the time goes in v8:
time: 127 us; the launch traced here: 124 us
  blocking collectives  92.7 us (73%)
  local copies, waits for them, and re-layouts  11.6 us (9%)
  starting transfers between devices  9.3 us (7%)
  other arithmetic  5.78 us (5%)
  matrix products  4.17 us (3%)
    all_to_all x2, blocking collectives, gather_blocks(): lax.all_to_all(copies, axis, split_axis=0, concat_axis=0, tiled=True)  66.2 us
    all_to_all x1, blocking collectives, body(): lax.all_to_all(product, 'cx', split_axis=0, concat_axis=0, tiled=True)  16.9 us
    all_to_all x1, blocking collectives, body(): lax.all_to_all(whitened, 'win', split_axis=3, concat_axis=1, tiled=True)  9.71 us
    ppermute x1, starting transfers between devices, with_halo(): before = lax.ppermute(last, CHAN, up)  4.02 us
    all_to_all x1, starting transfers between devices, gather_blocks(): lax.all_to_all(copies, axis, split_axis=0, concat_axis=0, tiled=True)  3.99 us
  transfers between devices with their start and end apart: 3, of which 1 were waited for; matrix products, arithmetic and copies ran while one was open for 8% of the time, Pallas kernels for 0%

profile of v8, /device:TPU:1, one launch (start us, length us, event | category | flops | bytes accessed | tf_op | source)
XLA Modules:
  0.0 124.4 jit_solution(195530096125330023)
XLA Ops:
  0.0 0.7 fusion.36
  0.7 4.0 %collective-permute-start = (bf16[8,1,1024]{2,0,1:T(8,128)(2,1)S(1)}, bf16[8,1,1024]{2,0,1:T(8,128)(2,1)S(1)}, u32[]{:S(2)}, u32[]{:S(2)}) collective-permute-start(bf16[8,1,1024]{2,0,1:T(8,128)(2,1)S(1)} %get-tuple-element.9), channel_id=1, source_target_pairs={{0,4},{4,8},{8,12},{12,16},{16,20},{20,24},{24,28},{28,32},{32,36}... | collective-permute-start | bytes 49160 | tf_op jit(solution)/shard_map/ppermute | solution.py:27
  4.8 1.3 %collective-permute-start.1 = (bf16[8,1,1024]{2,0,1:T(8,128)(2,1)S(1)}, bf16[8,1,1024]{2,0,1:T(8,128)(2,1)S(1)}, u32[]{:S(2)}, u32[]{:S(2)}) collective-permute-start(bf16[8,1,1024]{2,0,1:T(8,128)(2,1)S(1)} %get-tuple-element.10), channel_id=1, source_target_pairs={{4,0},{8,4},{12,8},{16,12},{20,16},{24,20},{28,24},{32,28},{36,32}... | collective-permute-start | bytes 49160 | tf_op jit(solution)/shard_map/ppermute | solution.py:28
  6.1 0.8 pad_dynamic-slice_fusion
  7.0 0.9 select_reduce_fusion
  7.9 0.8 broadcast_compare_fusion
  8.7 2.1 %cosine_multiply_fusion = (f32[1024,128]{1,0:T(8,128)S(1)}, f32[1024,128]{1,0:T(8,128)S(1)}) fusion(s32[128]{0:T(128)S(1)} %iota_add_fusion, f32[1024]{0:T(1024)S(1)} %get-tuple-element.15, f32[1024]{0:T(1024)S(1)} %get-tuple-element.16), kind=kLoop, calls=%fused_computation.26 | loop fusion | flops 2097152 | bytes 1057280 | tf_op jit(solution)/shard_map/mul | solution.py:45
  10.8 0.8 convert_reduce_fusion.1
  11.7 1.2 fusion.7
  12.9 0.6 fusion.9
  14.2 9.7 %all_to_all.35 = f32[4,1,3072]{2,1,0:T(1,128)S(1)} all-to-all(f32[4,1,3072]{2,1,0:T(1,128)S(1)} %reshape.91), channel_id=1, replica_groups=mesh['cx'=4,'cz'=4,'cb'=8,'win'=4] {'win'}, dimensions={0} | all-to-all | bytes 98304 | tf_op jit(solution)/shard_map/all_to_all | solution.py:102
  24.4 0.8 reduce
  25.6 20.2 %all_to_all.36 = f32[8,48,256]{2,1,0:T(8,128)S(1)} all-to-all(f32[8,48,256]{2,1,0:T(8,128)S(1)} %broadcast_in_dim.28), channel_id=1, replica_groups=mesh['cx'=4,'cz'=4,'cb'=8,'win'=4] {'cb'}, dimensions={0} | all-to-all | bytes 786432 | tf_op jit(solution)/shard_map/all_to_all | solution.py:35
  46.1 45.9 %all_to_all.37 = f32[4,384,256]{1,2,0:T(8,128)S(1)} all-to-all(f32[4,384,256]{1,2,0:T(8,128)S(1)} %broadcast_in_dim.30), channel_id=1, replica_groups=mesh['cx'=4,'cz'=4,'cb'=8,'win'=4] {'cz'}, dimensions={0} | all-to-all | bytes 3145728 | tf_op jit(solution)/shard_map/all_to_all | solution.py:35
  92.0 0.7 broadcast_in_dim.27
  92.7 4.0 %all-to-all-start.1 = ((f32[4,48,256]{2,1,0:T(8,128)}), f32[4,48,256]{2,1,0:T(8,128)S(1)}, u32[]{:S(2)}, u32[]{:S(2)}) async-start(f32[4,48,256]{2,1,0:T(8,128)} %broadcast_in_dim.27), calls=%async_computation.1 | async-start | bytes 393216 | tf_op jit(solution)/shard_map/all_to_all | solution.py:35
  96.7 2.2 %copy.31 = f32[4,384,256]{1,0,2:T(4,128)} copy(f32[4,384,256]{1,2,0:T(8,128)S(1)} %all_to_all.37) | data formatting | bytes 3145728 | tf_op jit(solution)/shard_map/all_to_all | solution.py:35
  98.9 1.9 %reshape_reshape.3 = f32[1536,4,2,32]{0,3,2,1:T(8,128)S(1)} reshape(f32[4,384,256]{1,0,2:T(4,128)} %copy.31) | data formatting | bytes 3145728 | tf_op jit(solution)/shard_map/reshape;reshape | solution.py:55
  101.2 0.6 all-to-all-done.1
  101.9 2.2 %fusion = bf16[192,3072]{1,0:T(8,128)(2,1)S(1)} fusion(f32[192,256]{1,0:T(8,128)S(1)} %bitcast.42, f32[1536,256]{0,1:T(8,128)S(1)} %bitcast.38, f32[1536,256]{0,1:T(8,128)S(1)} %bitcast.37), kind=kOutput, calls=%fused_computation.1 | convolution fusion | flops 1813905408 | bytes 4521984 | tf_op jit(solution)/shard_map/ik,jk->ij/dot_general | solution.py:109
  104.0 16.9 %all_to_all.38 = bf16[4,48,3072]{2,1,0:T(8,128)(2,1)S(1)} all-to-all(bf16[4,48,3072]{2,1,0:T(8,128)(2,1)S(1)} %bitcast.40), channel_id=1, replica_groups=mesh['cx'=4,'cz'=4,'cb'=8,'win'=4] {'cx'}, dimensions={0} | all-to-all | bytes 2359296 | tf_op jit(solution)/shard_map/all_to_all | solution.py:112
  120.9 0.9 reshape.90
  121.8 0.9 copy.36
  122.7 1.7 %broadcast_in_dim_reshape.2 = bf16[1,2,48,6144]{3,2,1,0:T(8,128)(2,1)} reshape(bf16[2,48,4,1536]{3,2,1,0:T(4,128)(2,1)S(1)} %bitcast.39) | data formatting | bytes 2359296 | tf_op jit(solution)/shard_map/broadcast_in_dim;reshape | solution.py:115
  (24 shorter events, 2.4 us)
Async XLA Ops:
  0.7 11.0 %collective-permute-start = (bf16[8,1,1024]{2,0,1:T(8,128)(2,1)S(1)}, bf16[8,1,1024]{2,0,1:T(8,128)(2,1)S(1)}, u32[]{:S(2)}, u32[]{:S(2)}) collective-permute-start(bf16[8,1,1024]{2,0,1:T(8,128)(2,1)S(1)} %get-tuple-element.9), channel_id=1, source_target_pairs={{0,4},{4,8},{8,12},{12,16},{16,20},{20,24},{24,28},{28,32},{32,36}... | collective-permute-start | bytes 49160 | tf_op jit(solution)/shard_map/ppermute | solution.py:27
  4.8 7.0 %collective-permute-start.1 = (bf16[8,1,1024]{2,0,1:T(8,128)(2,1)S(1)}, bf16[8,1,1024]{2,0,1:T(8,128)(2,1)S(1)}, u32[]{:S(2)}, u32[]{:S(2)}) collective-permute-start(bf16[8,1,1024]{2,0,1:T(8,128)(2,1)S(1)} %get-tuple-element.10), channel_id=1, source_target_pairs={{4,0},{8,4},{12,8},{16,12},{20,16},{24,20},{28,24},{32,28},{36,32}... | collective-permute-start | bytes 49160 | tf_op jit(solution)/shard_map/ppermute | solution.py:28
  92.7 9.2 %all-to-all-start.1 = ((f32[4,48,256]{2,1,0:T(8,128)}), f32[4,48,256]{2,1,0:T(8,128)S(1)}, u32[]{:S(2)}, u32[]{:S(2)}) async-start(f32[4,48,256]{2,1,0:T(8,128)} %broadcast_in_dim.27), calls=%async_computation.1 | async-start | bytes 393216 | tf_op jit(solution)/shard_map/all_to_all | solution.py:35

commit v9 on v8

--- a/solution.py
+++ b/solution.py
@@ -103,7 +103,9 @@
     windows = banded.shape[1]
     spectra_block = banded.reshape(local_rows, -1)
     inverse_count = 1.0 / (spectra_block.shape[1] // 2)
-    col_set = gather_blocks(gather_blocks(spectra_block, "cb"), "cz")
+    col_set = gather_blocks(gather_blocks(spectra_block, "cz"), "cb")
+    col_set = col_set.reshape(group_b, group_z, local_rows, -1).transpose(1, 0, 2, 3)
+    col_set = col_set.reshape(group_z * group_b * local_rows, -1)
     row_set = gather_blocks(spectra_block, "cx")
     operands = jnp.concatenate([col_set, swapped_parts(col_set, windows)], axis=0)
     product = jnp.einsum("ik,jk->ij", row_set, operands, precision=lax.Precision.HIGHEST)

time: 127 us -> 130 us (1.024)
  the two profiles are of different devices: /device:TPU:1 before, /device:TPU:128 now
where the time goes in v9:
time: 130 us
  blocking collectives  85.9 us (66%)
  local copies, waits for them, and re-layouts  18 us (14%)
  starting transfers between devices  13.1 us (10%)
  other arithmetic  7 us (5%)
  matrix products  5.32 us (4%)
    all_to_all x2, blocking collectives, gather_blocks(): lax.all_to_all(copies, axis, split_axis=0, concat_axis=0, tiled=True)  59.9 us
    all_to_all x1, blocking collectives, body(): lax.all_to_all(product, 'cx', split_axis=0, concat_axis=0, tiled=True)  18.5 us
    all_to_all x1, blocking collectives, body(): lax.all_to_all(whitened, 'win', split_axis=3, concat_axis=1, tiled=True)  7.48 us
    ppermute x1, starting transfers between devices, with_halo(): after = lax.ppermute(initial, CHAN, down)  5.37 us
    transpose x2, local copies, waits for them, and re-layouts, body(): col_set.reshape(group_b, group_z, local_rows, -1).transpose(1, 0, 2, 3)  4.54 us
    another operation x1, local copies, waits for them, and re-layouts, swapped_parts(): parts = flat.reshape(flat.shape[:-1] + (windows, 2, -1))  4.45 us
    all_to_all x1, starting transfers between devices, gather_blocks(): lax.all_to_all(copies, axis, split_axis=0, concat_axis=0, tiled=True)  4.27 us
    ppermute x1, starting transfers between devices, with_halo(): before = lax.ppermute(last, CHAN, up)  3.47 us
  transfers between devices with their start and end apart: 3, of which 0 were waited for; matrix products, arithmetic and copies ran while one was open for 14% of the time, Pallas kernels for 0%

profile of v9, /device:TPU:128, one launch (start us, length us, event | category | flops | bytes accessed | tf_op | source)
XLA Modules:
  0.0 129.6 jit_solution(4213053963397436416)
XLA Ops:
  0.0 0.7 fusion.36
  0.7 3.5 %collective-permute-start = (bf16[8,1,1024]{2,0,1:T(8,128)(2,1)S(1)}, bf16[8,1,1024]{2,0,1:T(8,128)(2,1)S(1)}, u32[]{:S(2)}, u32[]{:S(2)}) collective-permute-start(bf16[8,1,1024]{2,0,1:T(8,128)(2,1)S(1)} %get-tuple-element.9), channel_id=1, source_target_pairs={{0,4},{4,8},{8,12},{12,16},{16,20},{20,24},{24,28},{28,32},{32,36}... | collective-permute-start | bytes 49160 | tf_op jit(solution)/shard_map/ppermute | solution.py:27
  4.2 5.4 %collective-permute-start.1 = (bf16[8,1,1024]{2,0,1:T(8,128)(2,1)S(1)}, bf16[8,1,1024]{2,0,1:T(8,128)(2,1)S(1)}, u32[]{:S(2)}, u32[]{:S(2)}) collective-permute-start(bf16[8,1,1024]{2,0,1:T(8,128)(2,1)S(1)} %get-tuple-element.10), channel_id=1, source_target_pairs={{4,0},{8,4},{12,8},{16,12},{20,16},{24,20},{28,24},{32,28},{36,32}... | collective-permute-start | bytes 49160 | tf_op jit(solution)/shard_map/ppermute | solution.py:28
  9.7 0.8 pad_dynamic-slice_fusion
  10.5 0.9 select_reduce_fusion
  11.4 0.8 broadcast_compare_fusion
  12.3 2.1 %cosine_multiply_fusion = (f32[1024,128]{1,0:T(8,128)S(1)}, f32[1024,128]{1,0:T(8,128)S(1)}) fusion(s32[128]{0:T(128)S(1)} %iota_add_fusion, f32[1024]{0:T(1024)S(1)} %get-tuple-element.15, f32[1024]{0:T(1024)S(1)} %get-tuple-element.16), kind=kLoop, calls=%fused_computation.26 | loop fusion | flops 2097152 | bytes 1057280 | tf_op jit(solution)/shard_map/mul | solution.py:45
  14.4 0.8 convert_reduce_fusion.1
  15.3 1.2 fusion.7
  17.7 7.5 %all_to_all.35 = f32[4,1,3072]{2,1,0:T(1,128)S(1)} all-to-all(f32[4,1,3072]{2,1,0:T(1,128)S(1)} %reshape.91), channel_id=1, replica_groups=mesh['cx'=4,'cz'=4,'cb'=8,'win'=4] {'win'}, dimensions={0} | all-to-all | bytes 98304 | tf_op jit(solution)/shard_map/all_to_all | solution.py:102
  25.7 0.8 reduce
  26.8 0.7 broadcast_in_dim.25
  27.5 16.3 %all_to_all.36 = f32[4,48,256]{2,1,0:T(8,128)S(1)} all-to-all(f32[4,48,256]{2,1,0:T(8,128)} %broadcast_in_dim.25), channel_id=1, replica_groups=mesh['cx'=4,'cz'=4,'cb'=8,'win'=4] {'cz'}, dimensions={0} | all-to-all | bytes 393216 | tf_op jit(solution)/shard_map/all_to_all | solution.py:35
  44.0 43.6 %all_to_all.37 = f32[8,192,256]{2,1,0:T(8,128)S(1)} all-to-all(f32[8,192,256]{2,1,0:T(8,128)S(1)} %broadcast_in_dim.27), channel_id=1, replica_groups=mesh['cx'=4,'cz'=4,'cb'=8,'win'=4] {'cb'}, dimensions={0} | all-to-all | bytes 3145728 | tf_op jit(solution)/shard_map/all_to_all | solution.py:35
  87.6 4.3 %all-to-all-start.1 = ((f32[4,48,256]{2,1,0:T(8,128)}), f32[4,48,256]{2,1,0:T(8,128)S(1)}, u32[]{:S(2)}, u32[]{:S(2)}) async-start(f32[4,48,256]{2,1,0:T(8,128)} %broadcast_in_dim.25), calls=%async_computation.1 | async-start | bytes 393216 | tf_op jit(solution)/shard_map/all_to_all | solution.py:35
  92.0 4.4 %copy.32 = f32[4,8,48,256]{2,1,0,3:T(8,128)} copy(f32[4,8,48,256]{3,2,0,1:T(8,128)S(1)} %bitcast.41) | data formatting | bytes 3145728 | tf_op jit(solution)/shard_map/transpose | solution.py:107
  96.4 4.4 %reshape_reshape.7 = f32[1536,4,2,32]{0,3,2,1:T(8,128)S(1)} reshape(f32[4,8,48,256]{2,1,0,3:T(8,128)} %copy.32) | data formatting | bytes 3145728 | tf_op jit(solution)/shard_map/reshape;reshape | solution.py:55
  101.0 1.3 %pad_maximum_fusion = f32[1536,4,2,32]{0,3,2,1:T(8,128)} fusion(f32[1536,4,1,32]{0,3,2,1:T(8,128)S(1)} %get-tuple-element.8, f32[1536,4,1,32]{0,3,2,1:T(8,128)S(1)} %get-tuple-element.7), kind=kLoop, calls=%fused_computation.5 | loop fusion | flops 393216 | bytes 3145728 | tf_op jit(solution)/shard_map/stack | solution.py:56
  102.4 1.9 %copy.33 = f32[1536,256]{1,0:T(8,128)S(1)} copy(f32[1536,256]{0,1:T(8,128)} %bitcast.43) | data formatting | bytes 3145728 | tf_op jit(solution)/shard_map/reshape | solution.py:57
  104.3 3.3 %fusion = bf16[192,3072]{1,0:T(8,128)(2,1)S(1)} fusion(f32[192,256]{1,0:T(8,128)S(1)} %bitcast.46, f32[1536,256]{1,0:T(8,128)S(1)} %copy.33, f32[1536,256]{1,0:T(8,128)S(1)} %bitcast.42), kind=kOutput, calls=%fused_computation.1 | convolution fusion | flops 1813905408 | bytes 4521984 | tf_op jit(solution)/shard_map/ik,jk->ij/dot_general | solution.py:111
  107.6 18.5 %all_to_all.38 = bf16[4,48,3072]{2,1,0:T(8,128)(2,1)S(1)} all-to-all(bf16[4,48,3072]{2,1,0:T(8,128)(2,1)S(1)} %bitcast.45), channel_id=1, replica_groups=mesh['cx'=4,'cz'=4,'cb'=8,'win'=4] {'cx'}, dimensions={0} | all-to-all | bytes 2359296 | tf_op jit(solution)/shard_map/all_to_all | solution.py:114
  126.1 0.9 reshape.90
  127.0 0.9 copy.36
  127.9 1.7 %broadcast_in_dim_reshape.2 = bf16[1,2,48,6144]{3,2,1,0:T(8,128)(2,1)} reshape(bf16[2,48,4,1536]{3,2,1,0:T(4,128)(2,1)S(1)} %bitcast.44) | data formatting | bytes 2359296 | tf_op jit(solution)/shard_map/broadcast_in_dim;reshape | solution.py:117
  (23 shorter events, 2.7 us)
Async XLA Ops:
  0.7 14.5 %collective-permute-start = (bf16[8,1,1024]{2,0,1:T(8,128)(2,1)S(1)}, bf16[8,1,1024]{2,0,1:T(8,128)(2,1)S(1)}, u32[]{:S(2)}, u32[]{:S(2)}) collective-permute-start(bf16[8,1,1024]{2,0,1:T(8,128)(2,1)S(1)} %get-tuple-element.9), channel_id=1, source_target_pairs={{0,4},{4,8},{8,12},{12,16},{16,20},{20,24},{24,28},{28,32},{32,36}... | collective-permute-start | bytes 49160 | tf_op jit(solution)/shard_map/ppermute | solution.py:27
  4.2 11.1 %collective-permute-start.1 = (bf16[8,1,1024]{2,0,1:T(8,128)(2,1)S(1)}, bf16[8,1,1024]{2,0,1:T(8,128)(2,1)S(1)}, u32[]{:S(2)}, u32[]{:S(2)}) collective-permute-start(bf16[8,1,1024]{2,0,1:T(8,128)(2,1)S(1)} %get-tuple-element.10), channel_id=1, source_target_pairs={{4,0},{8,4},{12,8},{16,12},{20,16},{24,20},{28,24},{32,28},{36,32}... | collective-permute-start | bytes 49160 | tf_op jit(solution)/shard_map/ppermute | solution.py:28
  87.6 16.6 %all-to-all-start.1 = ((f32[4,48,256]{2,1,0:T(8,128)}), f32[4,48,256]{2,1,0:T(8,128)S(1)}, u32[]{:S(2)}, u32[]{:S(2)}) async-start(f32[4,48,256]{2,1,0:T(8,128)} %broadcast_in_dim.25), calls=%async_computation.1 | async-start | bytes 393216 | tf_op jit(solution)/shard_map/all_to_all | solution.py:35

commit v10 on v8

--- a/solution.py
+++ b/solution.py
@@ -36,13 +36,13 @@
     return every.reshape(-1, block.shape[1])
 
 def fourier_table():
-    sample_ids = jnp.arange(SAMPLES, dtype=jnp.int32)
-    bin_ids = FIRST_BIN + jnp.arange(FREQ_BINS, dtype=jnp.int32)
-    phase_ids = sample_ids[:, None] * bin_ids[None, :] % SAMPLES
-    angles = 2.0 * jnp.pi / SAMPLES * phase_ids.astype(jnp.float32)
-    taper = 0.5 - 0.5 * jnp.cos(2.0 * jnp.pi / SAMPLES * (sample_ids.astype(jnp.float32) + 0.5))
-    weights = taper[:, None] / jnp.sqrt(jnp.float32(SAMPLES))
-    return jnp.concatenate([weights * jnp.cos(angles), -weights * jnp.sin(angles)], axis=1)
+    sample_ids = np.arange(SAMPLES)
+    bin_ids = FIRST_BIN + np.arange(FREQ_BINS)
+    angles = 2.0 * np.pi / SAMPLES * (sample_ids[:, None] * bin_ids[None, :] % SAMPLES)
+    taper = 0.5 - 0.5 * np.cos(2.0 * np.pi / SAMPLES * (sample_ids + 0.5))
+    weights = taper[:, None] / np.sqrt(SAMPLES)
+    table = np.concatenate([weights * np.cos(angles), -weights * np.sin(angles)], axis=1)
+    return jnp.asarray(table.astype(np.float32))
 
 
 def smoothing_table():
@@ -103,14 +103,14 @@
     windows = banded.shape[1]
     spectra_block = banded.reshape(local_rows, -1)
     inverse_count = 1.0 / (spectra_block.shape[1] // 2)
-    col_set = gather_blocks(gather_blocks(spectra_block, "cb"), "cz")
-    row_set = gather_blocks(spectra_block, "cx")
+    col_set = gather_blocks(spectra_block, "cb")
+    row_set = gather_blocks(gather_blocks(spectra_block, "cz"), "cx")
     operands = jnp.concatenate([col_set, swapped_parts(col_set, windows)], axis=0)
     product = jnp.einsum("ik,jk->ij", row_set, operands, precision=lax.Precision.HIGHEST)
     product = (product * inverse_count).astype(jnp.bfloat16)
-    product = product.reshape(group_x, local_rows, operands.shape[0])
-    mine = lax.all_to_all(product, "cx", split_axis=0, concat_axis=0, tiled=True)
-    mine = mine.reshape(group_x, local_rows, 2, col_set.shape[0])
+    product = product.reshape(group_x * group_z, local_rows, operands.shape[0])
+    mine = lax.all_to_all(product, ("cx", "cz"), split_axis=0, concat_axis=0, tiled=True)
+    mine = mine.reshape(group_x * group_z, local_rows, 2, col_set.shape[0])
     cross_spectra = mine.transpose(2, 1, 0, 3).reshape(2, local_rows, -1)
     return cross_spectra[None]
 

time: 127 us -> 115 us (0.906); the launches traced: 124 us -> 114 us
  blocking collectives: 92.7 us -> 82.4 us
  waiting for transfers between devices: 0.62 us -> 7.36 us
  local copies, waits for them, and re-layouts: 11.6 us -> 6.86 us
  other arithmetic: 5.78 us -> 3.45 us
    all_to_all x2, blocking collectives: 66.2 us -> 34.2 us  [gather_blocks(): lax.all_to_all(copies, axis, split_axis=0, concat_axis=0, tiled=True)]
    all_to_all x1, blocking collectives: 16.9 us -> 37.7 us  [body(): lax.all_to_all(product, ('cx', 'cz'), split_axis=0, concat_axis=0, tiled=...]
    all_to_all x1, waiting for transfers between devices: 0.62 us -> 7.35 us  [gather_blocks(): lax.all_to_all(copies, axis, split_axis=0, concat_axis=0, tiled=True)]
    mul x1 -> x0, other arithmetic: 2.09 us -> none  [fourier_table(): weights * jnp.cos(angles)]
    all_to_all x1, local copies, waits for them, and re-layouts: 2.17 us -> 0.41 us  [gather_blocks(): lax.all_to_all(copies, axis, split_axis=0, concat_axis=0, tiled=True)]
    another operation x1, local copies, waits for them, and re-layouts: 1.92 us -> 0.31 us  [swapped_parts(): parts = flat.reshape(flat.shape[:-1] + (windows, 2, -1))]
  transfers between devices with their start and end apart: 3 -> 3, of which waited for: 1 -> 1; matrix products, arithmetic and copies ran while one was open for 8% -> 4% of each run, Pallas kernels for 0% -> 0%
where the time goes in v10:
time: 115 us; the launch traced here: 114 us
  blocking collectives  82.4 us (72%)
  starting transfers between devices  9.3 us (8%)
  waiting for transfers between devices  7.36 us (6%)
  local copies, waits for them, and re-layouts  6.86 us (6%)
  matrix products  4.1 us (4%)
  other arithmetic  3.45 us (3%)
    all_to_all x1, blocking collectives, body(): lax.all_to_all(product, ('cx', 'cz'), split_axis=0, concat_axis=0, tiled=...  37.7 us
    all_to_all x2, blocking collectives, gather_blocks(): lax.all_to_all(copies, axis, split_axis=0, concat_axis=0, tiled=True)  34.2 us
    all_to_all x1, blocking collectives, body(): lax.all_to_all(whitened, 'win', split_axis=3, concat_axis=1, tiled=True)  10.5 us
    all_to_all x1, waiting for transfers between devices, gather_blocks(): lax.all_to_all(copies, axis, split_axis=0, concat_axis=0, tiled=True)  7.35 us
    ppermute x1, starting transfers between devices, with_halo(): before = lax.ppermute(last, CHAN, up)  4.02 us
    all_to_all x1, starting transfers between devices, gather_blocks(): lax.all_to_all(copies, axis, split_axis=0, concat_axis=0, tiled=True)  3.99 us
  transfers between devices with their start and end apart: 3, of which 1 were waited for; matrix products, arithmetic and copies ran while one was open for 4% of the time, Pallas kernels for 0%

profile of v10, /device:TPU:1, one launch (start us, length us, event | category | flops | bytes accessed | tf_op | source)
XLA Modules:
  0.0 113.7 jit_solution(6892677130768138338)
XLA Ops:
  0.0 0.8 fusion.23
  0.8 4.0 %collective-permute-start = (bf16[8,1,1024]{2,0,1:T(8,128)(2,1)S(1)}, bf16[8,1,1024]{2,0,1:T(8,128)(2,1)S(1)}, u32[]{:S(2)}, u32[]{:S(2)}) collective-permute-start(bf16[8,1,1024]{2,0,1:T(8,128)(2,1)S(1)} %get-tuple-element.9), channel_id=1, source_target_pairs={{0,4},{4,8},{8,12},{12,16},{16,20},{20,24},{24,28},{28,32},{32,36}... | collective-permute-start | bytes 49160 | tf_op jit(solution)/shard_map/ppermute | solution.py:27
  4.9 1.3 %collective-permute-start.1 = (bf16[8,1,1024]{2,0,1:T(8,128)(2,1)S(1)}, bf16[8,1,1024]{2,0,1:T(8,128)(2,1)S(1)}, u32[]{:S(2)}, u32[]{:S(2)}) collective-permute-start(bf16[8,1,1024]{2,0,1:T(8,128)(2,1)S(1)} %get-tuple-element.10), channel_id=1, source_target_pairs={{4,0},{8,4},{12,8},{16,12},{20,16},{24,20},{28,24},{32,28},{36,32}... | collective-permute-start | bytes 49160 | tf_op jit(solution)/shard_map/ppermute | solution.py:28
  6.2 0.8 pad_dynamic-slice_fusion
  7.0 0.9 select_reduce_fusion
  7.9 0.8 broadcast_compare_fusion
  8.7 0.8 convert_reduce_fusion.1
  9.7 1.2 %fusion.3 = f32[48,1024]{1,0:T(8,128)S(1)} fusion(bf16[48,1,1024]{2,0,1:T(8,128)(2,1)} %param.5, bf16[8,1,1024]{2,0,1:T(8,128)(2,1)S(1)} %collective-permute-done.1, bf16[8,1,1024]{2,0,1:T(8,128)(2,1)S(1)} %collective-permute-done, f32[48]{0:T(128)S(1)} %broadcast_maximum_fusion, f32[48]{0:T(128)S(1)} %get-tuple-element.12, ...), kind=kOutput, calls=%fused_computation.6 | convolution fusion | flops 6899712 | bytes 328960 | tf_op jit(solution)/shard_map/cr,rwt->cwt/dot_general | solution.py:88
  10.9 0.6 fusion.24
  12.1 10.5 %all_to_all.35 = f32[4,1,3072]{2,1,0:T(1,128)S(1)} all-to-all(f32[4,1,3072]{2,1,0:T(1,128)S(1)} %reshape.72), channel_id=1, replica_groups=mesh['cx'=4,'cz'=4,'cb'=8,'win'=4] {'win'}, dimensions={0} | all-to-all | bytes 98304 | tf_op jit(solution)/shard_map/all_to_all | solution.py:102
  22.6 0.5 broadcast.24
  23.1 0.8 reduce
  24.3 19.3 %all_to_all.36 = f32[4,48,256]{2,1,0:T(8,128)S(1)} all-to-all(f32[4,48,256]{2,1,0:T(8,128)S(1)} %broadcast_in_dim.27), channel_id=1, replica_groups=mesh['cx'=4,'cz'=4,'cb'=8,'win'=4] {'cz'}, dimensions={0} | all-to-all | bytes 393216 | tf_op jit(solution)/shard_map/all_to_all | solution.py:35
  43.7 14.8 %all_to_all.37 = f32[8,48,256]{2,1,0:T(8,128)S(1)} all-to-all(f32[8,48,256]{2,1,0:T(8,128)S(1)} %broadcast_in_dim.30), channel_id=1, replica_groups=mesh['cx'=4,'cz'=4,'cb'=8,'win'=4] {'cb'}, dimensions={0} | all-to-all | bytes 786432 | tf_op jit(solution)/shard_map/all_to_all | solution.py:35
  58.5 0.9 broadcast_in_dim.29
  59.5 4.0 %all-to-all-start.2 = ((f32[4,192,256]{2,1,0:T(8,128)}), f32[4,192,256]{2,1,0:T(8,128)S(1)}, u32[]{:S(2)}, u32[]{:S(2)}) async-start(f32[4,192,256]{2,1,0:T(8,128)} %broadcast_in_dim.29), calls=%async_computation.2 | async-start | bytes 1572864 | tf_op jit(solution)/shard_map/all_to_all | solution.py:35
  63.4 0.4 copy.31
  63.9 0.3 reshape_reshape.3
  64.4 7.4 %all-to-all-done.2 = f32[4,192,256]{2,1,0:T(8,128)S(1)} async-done(((f32[4,192,256]{2,1,0:T(8,128)}), f32[4,192,256]{2,1,0:T(8,128)S(1)}, u32[]{:S(2)}, u32[]{:S(2)}) %all-to-all-start.2) | async-done | bytes 786464 | tf_op jit(solution)/shard_map/all_to_all | solution.py:35
  71.8 2.1 %multiply_convert_fusion = bf16[768,768]{1,0:T(8,128)(2,1)S(1)} fusion(f32[768,256]{1,0:T(8,128)S(1)} %bitcast.41, f32[384,256]{1,0:T(8,128)S(1)} %copy.32, f32[384,256]{1,0:T(8,128)S(1)} %bitcast.40), kind=kOutput, calls=%fused_computation | convolution fusion | flops 1813315584 | bytes 2752512 | tf_op jit(solution)/shard_map/ik,jk->ij/dot_general | solution.py:109
  73.9 37.7 %all_to_all.38 = bf16[16,48,768]{2,1,0:T(8,128)(2,1)S(1)} all-to-all(bf16[16,48,768]{2,1,0:T(8,128)(2,1)S(1)} %bitcast.39), channel_id=1, replica_groups=mesh['cx'=4,'cz'=4,'cb'=8,'win'=4] {'cx','cz'}, dimensions={0} | all-to-all | bytes 2359296 | tf_op jit(solution)/shard_map/all_to_all | solution.py:112
  111.6 0.3 reshape.71
  111.9 0.4 copy.35
  112.3 1.4 %broadcast_in_dim_reshape.2 = bf16[1,2,48,6144]{3,2,1,0:T(8,128)(2,1)} reshape(bf16[2,48,16,384]{3,2,1,0:T(8,128)(2,1)S(1)} %bitcast.38) | data formatting | bytes 2359296 | tf_op jit(solution)/shard_map/broadcast_in_dim;reshape | solution.py:115
  (22 shorter events, 1.4 us)
Async XLA Ops:
  0.0 10.9 %copy-start = (f32[1024,256]{1,0:T(8,128)S(1)}, f32[1024,256]{1,0:T(8,128)}, u32[]{:S(2)}) copy-start(f32[1024,256]{1,0:T(8,128)} %constant.42.clone) | copy-start | bytes 3145732
  0.8 8.8 %collective-permute-start = (bf16[8,1,1024]{2,0,1:T(8,128)(2,1)S(1)}, bf16[8,1,1024]{2,0,1:T(8,128)(2,1)S(1)}, u32[]{:S(2)}, u32[]{:S(2)}) collective-permute-start(bf16[8,1,1024]{2,0,1:T(8,128)(2,1)S(1)} %get-tuple-element.9), channel_id=1, source_target_pairs={{0,4},{4,8},{8,12},{12,16},{16,20},{20,24},{24,28},{28,32},{32,36}... | collective-permute-start | bytes 49160 | tf_op jit(solution)/shard_map/ppermute | solution.py:27
  4.9 4.8 %collective-permute-start.1 = (bf16[8,1,1024]{2,0,1:T(8,128)(2,1)S(1)}, bf16[8,1,1024]{2,0,1:T(8,128)(2,1)S(1)}, u32[]{:S(2)}, u32[]{:S(2)}) collective-permute-start(bf16[8,1,1024]{2,0,1:T(8,128)(2,1)S(1)} %get-tuple-element.10), channel_id=1, source_target_pairs={{4,0},{8,4},{12,8},{16,12},{20,16},{24,20},{28,24},{32,28},{36,32}... | collective-permute-start | bytes 49160 | tf_op jit(solution)/shard_map/ppermute | solution.py:28
  59.5 12.3 %all-to-all-start.2 = ((f32[4,192,256]{2,1,0:T(8,128)}), f32[4,192,256]{2,1,0:T(8,128)S(1)}, u32[]{:S(2)}, u32[]{:S(2)}) async-start(f32[4,192,256]{2,1,0:T(8,128)} %broadcast_in_dim.29), calls=%async_computation.2 | async-start | bytes 1572864 | tf_op jit(solution)/shard_map/all_to_all | solution.py:35

commit v11 on v10

--- a/solution.py
+++ b/solution.py
@@ -34,6 +34,14 @@
     copies = jnp.broadcast_to(block[None], (size,) + block.shape)
     every = lax.all_to_all(copies, axis, split_axis=0, concat_axis=0, tiled=True)
     return every.reshape(-1, block.shape[1])
+
+def spread_band(per_band, axis):
+    size = lax.axis_size(axis)
+    bands, rows, width = per_band.shape
+    copies = jnp.broadcast_to(per_band[None], (size, bands, rows, width)).reshape(size * bands, rows, width)
+    every = lax.all_to_all(copies, (axis, "win"), split_axis=0, concat_axis=0, tiled=True)
+    every = every.reshape(size, bands, rows, width).transpose(0, 2, 1, 3)
+    return every.reshape(size * rows, bands * width)
 
 def fourier_table():
     sample_ids = np.arange(SAMPLES)
@@ -98,13 +106,13 @@
     )
     inverse_amp = lax.rsqrt(jnp.maximum(smoothed, FLOOR_POWER))
     whitened = spectra * jnp.concatenate([inverse_amp, inverse_amp], axis=-1)
-    whitened = whitened.reshape(local_rows, strain.shape[1], 2, FREQ_BINS)
-    banded = lax.all_to_all(whitened, "win", split_axis=3, concat_axis=1, tiled=True)
-    windows = banded.shape[1]
-    spectra_block = banded.reshape(local_rows, -1)
-    inverse_count = 1.0 / (spectra_block.shape[1] // 2)
-    col_set = gather_blocks(spectra_block, "cb")
-    row_set = gather_blocks(gather_blocks(spectra_block, "cz"), "cx")
+    bands = lax.axis_size("win")
+    whitened = whitened.reshape(local_rows, 2, bands, FREQ_BINS // bands).transpose(2, 0, 1, 3)
+    whitened = whitened.reshape(bands, local_rows, -1)
+    windows = bands
+    inverse_count = 1.0 / (windows * whitened.shape[2] // 2)
+    col_set = spread_band(whitened, "cb")
+    row_set = gather_blocks(spread_band(whitened, "cz"), "cx")
     operands = jnp.concatenate([col_set, swapped_parts(col_set, windows)], axis=0)
     product = jnp.einsum("ik,jk->ij", row_set, operands, precision=lax.Precision.HIGHEST)
     product = (product * inverse_count).astype(jnp.bfloat16)

time: 115 us -> 114 us (level)
  the two profiles are of different devices: /device:TPU:1 before, /device:TPU:72 now
where the time goes in v11:
time: 114 us; the launch traced here: 113 us
  blocking collectives  35.3 us (31%)
  starting transfers between devices  30.3 us (27%)
  waiting for transfers between devices  27.5 us (24%)
  local copies, waits for them, and re-layouts  10.1 us (9%)
  other arithmetic  5.45 us (5%)
  matrix products  4.1 us (4%)
    all_to_all x1, blocking collectives, body(): lax.all_to_all(product, ('cx', 'cz'), split_axis=0, concat_axis=0, tiled=...  35.3 us
    all_to_all x2, starting transfers between devices, spread_band(): lax.all_to_all(copies, (axis, 'win'), split_axis=0, concat_axis=0, tiled=...  20.2 us
    all_to_all x2, waiting for transfers between devices, spread_band(): lax.all_to_all(copies, (axis, 'win'), split_axis=0, concat_axis=0, tiled=...  19 us
    all_to_all x1, waiting for transfers between devices, gather_blocks(): lax.all_to_all(copies, axis, split_axis=0, concat_axis=0, tiled=True)  8.57 us
    all_to_all x1, starting transfers between devices, gather_blocks(): lax.all_to_all(copies, axis, split_axis=0, concat_axis=0, tiled=True)  4.27 us
    ppermute x1, starting transfers between devices, with_halo(): before = lax.ppermute(last, CHAN, up)  3.47 us
    all_to_all x2, other arithmetic, spread_band(): lax.all_to_all(copies, (axis, 'win'), split_axis=0, concat_axis=0, tiled=...  2.76 us
    unnamed x6, local copies, waits for them, and re-layouts  2.46 us
  transfers between devices with their start and end apart: 5, of which 3 were waited for; matrix products, arithmetic and copies ran while one was open for 9% of the time, Pallas kernels for 0%

profile of v11, /device:TPU:72, one launch (start us, length us, event | category | flops | bytes accessed | tf_op | source)
XLA Modules:
  0.0 113.0 jit_solution(7829440229755913385)
XLA Ops:
  0.0 0.8 fusion.23
  0.8 3.5 %collective-permute-start = (bf16[8,1,1024]{2,0,1:T(8,128)(2,1)S(1)}, bf16[8,1,1024]{2,0,1:T(8,128)(2,1)S(1)}, u32[]{:S(2)}, u32[]{:S(2)}) collective-permute-start(bf16[8,1,1024]{2,0,1:T(8,128)(2,1)S(1)} %get-tuple-element.9), channel_id=1, source_target_pairs={{0,4},{4,8},{8,12},{12,16},{16,20},{20,24},{24,28},{28,32},{32,36}... | collective-permute-start | bytes 49160 | tf_op jit(solution)/shard_map/ppermute | solution.py:27
  4.3 2.4 %collective-permute-start.1 = (bf16[8,1,1024]{2,0,1:T(8,128)(2,1)S(1)}, bf16[8,1,1024]{2,0,1:T(8,128)(2,1)S(1)}, u32[]{:S(2)}, u32[]{:S(2)}) collective-permute-start(bf16[8,1,1024]{2,0,1:T(8,128)(2,1)S(1)} %get-tuple-element.10), channel_id=1, source_target_pairs={{4,0},{8,4},{12,8},{16,12},{20,16},{24,20},{28,24},{32,28},{36,32}... | collective-permute-start | bytes 49160 | tf_op jit(solution)/shard_map/ppermute | solution.py:28
  6.7 0.8 pad_dynamic-slice_fusion
  7.5 0.9 select_reduce_fusion
  8.4 0.8 broadcast_compare_fusion
  9.3 0.8 convert_reduce_fusion.1
  10.2 1.2 %fusion.3 = f32[48,1024]{1,0:T(8,128)S(1)} fusion(bf16[48,1,1024]{2,0,1:T(8,128)(2,1)} %param.5, bf16[8,1,1024]{2,0,1:T(8,128)(2,1)S(1)} %collective-permute-done.1, bf16[8,1,1024]{2,0,1:T(8,128)(2,1)S(1)} %collective-permute-done, f32[48]{0:T(128)S(1)} %broadcast_maximum_fusion, f32[48]{0:T(128)S(1)} %get-tuple-element.12, ...), kind=kOutput, calls=%fused_computation.6 | convolution fusion | flops 6899712 | bytes 328960 | tf_op jit(solution)/shard_map/cr,rwt->cwt/dot_general | solution.py:96
  11.4 0.6 fusion.24
  12.5 0.9 reshape.87
  13.4 10.0 %all-to-all-start = ((f32[16,1,3072]{2,1,0:T(1,128)}), f32[16,1,3072]{2,1,0:T(1,128)S(1)}, u32[]{:S(2)}, u32[]{:S(2)}) async-start(f32[16,1,3072]{2,1,0:T(1,128)} %reshape.87), calls=%async_computation | async-start | bytes 393216 | tf_op jit(solution)/shard_map/all_to_all | solution.py:42
  23.5 1.2 %reshape.89 = f32[32,1,3072]{2,1,0:T(1,128)} reshape(f32[32,48,64]{2,1,0:T(8,128)S(1)} %bitcast.48) | data formatting | bytes 786432
  24.7 7.2 %all-to-all-done = f32[16,1,3072]{2,1,0:T(1,128)S(1)} async-done(((f32[16,1,3072]{2,1,0:T(1,128)}), f32[16,1,3072]{2,1,0:T(1,128)S(1)}, u32[]{:S(2)}, u32[]{:S(2)}) %all-to-all-start) | async-done | bytes 196640 | tf_op jit(solution)/shard_map/all_to_all | solution.py:42
  31.9 10.3 %all-to-all-start.2 = ((f32[32,1,3072]{2,1,0:T(1,128)}), f32[32,1,3072]{2,1,0:T(1,128)S(1)}, u32[]{:S(2)}, u32[]{:S(2)}) async-start(f32[32,1,3072]{2,1,0:T(1,128)} %reshape.89), calls=%async_computation.2 | async-start | bytes 786432 | tf_op jit(solution)/shard_map/all_to_all | solution.py:42
  42.2 0.6 broadcast.24
  42.8 1.1 %reduce = f32[16,3072]{1,0:T(8,128)S(1)} reduce(f32[16,1,3072]{2,1,0:T(1,128)S(1)} %all-to-all-done, f32[]{:T(128)} %broadcast.24), dimensions={1}, to_apply=%all_to_all.12.reduce_sub_computation | reduce | bytes 393220 | tf_op jit(solution)/shard_map/all_to_all | solution.py:42
  44.5 11.7 %all-to-all-done.2 = f32[32,1,3072]{2,1,0:T(1,128)S(1)} async-done(((f32[32,1,3072]{2,1,0:T(1,128)}), f32[32,1,3072]{2,1,0:T(1,128)S(1)}, u32[]{:S(2)}, u32[]{:S(2)}) %all-to-all-start.2) | async-done | bytes 393248 | tf_op jit(solution)/shard_map/all_to_all | solution.py:42
  56.2 0.9 broadcast_in_dim.29
  57.1 4.3 %all-to-all-start.1 = ((f32[4,192,256]{2,1,0:T(8,128)}), f32[4,192,256]{2,1,0:T(8,128)S(1)}, u32[]{:S(2)}, u32[]{:S(2)}) async-start(f32[4,192,256]{2,1,0:T(8,128)} %broadcast_in_dim.29), calls=%async_computation.1 | async-start | bytes 1572864 | tf_op jit(solution)/shard_map/all_to_all | solution.py:35
  61.4 1.6 %reduce.1 = f32[32,3072]{1,0:T(8,128)S(1)} reduce(f32[32,1,3072]{2,1,0:T(1,128)S(1)} %all-to-all-done.2, f32[]{:T(128)} %broadcast.24), dimensions={1}, to_apply=%all_to_all.14.reduce_sub_computation | reduce | bytes 786436 | tf_op jit(solution)/shard_map/all_to_all | solution.py:42
  65.0 8.6 %all-to-all-done.1 = f32[4,192,256]{2,1,0:T(8,128)S(1)} async-done(((f32[4,192,256]{2,1,0:T(8,128)}), f32[4,192,256]{2,1,0:T(8,128)S(1)}, u32[]{:S(2)}, u32[]{:S(2)}) %all-to-all-start.1) | async-done | bytes 786464 | tf_op jit(solution)/shard_map/all_to_all | solution.py:35
  73.6 2.1 %multiply_convert_fusion = bf16[768,768]{1,0:T(8,128)(2,1)S(1)} fusion(f32[768,256]{1,0:T(8,128)S(1)} %bitcast.49, f32[384,256]{1,0:T(8,128)S(1)} %copy.30, f32[384,256]{1,0:T(8,128)S(1)} %reshape.83), kind=kOutput, calls=%fused_computation | convolution fusion | flops 1813315584 | bytes 2752512 | tf_op jit(solution)/shard_map/ik,jk->ij/dot_general | solution.py:117
  75.7 35.3 %all_to_all.20 = bf16[16,48,768]{2,1,0:T(8,128)(2,1)S(1)} all-to-all(bf16[16,48,768]{2,1,0:T(8,128)(2,1)S(1)} %bitcast.47), channel_id=1, replica_groups=mesh['cx'=4,'cz'=4,'cb'=8,'win'=4] {'cx','cz'}, dimensions={0} | all-to-all | bytes 2359296 | tf_op jit(solution)/shard_map/all_to_all | solution.py:120
  111.6 1.4 %broadcast_in_dim_reshape.2 = bf16[1,2,48,6144]{3,2,1,0:T(8,128)(2,1)} reshape(bf16[2,48,16,384]{3,2,1,0:T(8,128)(2,1)S(1)} %bitcast.46) | data formatting | bytes 2359296 | tf_op jit(solution)/shard_map/broadcast_in_dim;reshape | solution.py:123
  (28 shorter events, 3.8 us)
Async XLA Ops:
  0.0 11.4 %copy-start = (f32[1024,256]{1,0:T(8,128)S(1)}, f32[1024,256]{1,0:T(8,128)}, u32[]{:S(2)}) copy-start(f32[1024,256]{1,0:T(8,128)} %constant.42.clone) | copy-start | bytes 3145732
  0.8 9.4 %collective-permute-start = (bf16[8,1,1024]{2,0,1:T(8,128)(2,1)S(1)}, bf16[8,1,1024]{2,0,1:T(8,128)(2,1)S(1)}, u32[]{:S(2)}, u32[]{:S(2)}) collective-permute-start(bf16[8,1,1024]{2,0,1:T(8,128)(2,1)S(1)} %get-tuple-element.9), channel_id=1, source_target_pairs={{0,4},{4,8},{8,12},{12,16},{16,20},{20,24},{24,28},{28,32},{32,36}... | collective-permute-start | bytes 49160 | tf_op jit(solution)/shard_map/ppermute | solution.py:27
  4.3 5.9 %collective-permute-start.1 = (bf16[8,1,1024]{2,0,1:T(8,128)(2,1)S(1)}, bf16[8,1,1024]{2,0,1:T(8,128)(2,1)S(1)}, u32[]{:S(2)}, u32[]{:S(2)}) collective-permute-start(bf16[8,1,1024]{2,0,1:T(8,128)(2,1)S(1)} %get-tuple-element.10), channel_id=1, source_target_pairs={{4,0},{8,4},{12,8},{16,12},{20,16},{24,20},{28,24},{32,28},{36,32}... | collective-permute-start | bytes 49160 | tf_op jit(solution)/shard_map/ppermute | solution.py:28
  13.4 18.5 %all-to-all-start = ((f32[16,1,3072]{2,1,0:T(1,128)}), f32[16,1,3072]{2,1,0:T(1,128)S(1)}, u32[]{:S(2)}, u32[]{:S(2)}) async-start(f32[16,1,3072]{2,1,0:T(1,128)} %reshape.87), calls=%async_computation | async-start | bytes 393216 | tf_op jit(solution)/shard_map/all_to_all | solution.py:42
  31.9 24.3 %all-to-all-start.2 = ((f32[32,1,3072]{2,1,0:T(1,128)}), f32[32,1,3072]{2,1,0:T(1,128)S(1)}, u32[]{:S(2)}, u32[]{:S(2)}) async-start(f32[32,1,3072]{2,1,0:T(1,128)} %reshape.89), calls=%async_computation.2 | async-start | bytes 786432 | tf_op jit(solution)/shard_map/all_to_all | solution.py:42
  57.1 16.4 %all-to-all-start.1 = ((f32[4,192,256]{2,1,0:T(8,128)}), f32[4,192,256]{2,1,0:T(8,128)S(1)}, u32[]{:S(2)}, u32[]{:S(2)}) async-start(f32[4,192,256]{2,1,0:T(8,128)} %broadcast_in_dim.29), calls=%async_computation.1 | async-start | bytes 1572864 | tf_op jit(solution)/shard_map/all_to_all | solution.py:35

commit v12 on v11

--- a/solution.py
+++ b/solution.py
@@ -35,11 +35,11 @@
     every = lax.all_to_all(copies, axis, split_axis=0, concat_axis=0, tiled=True)
     return every.reshape(-1, block.shape[1])
 
-def spread_band(per_band, axis):
-    size = lax.axis_size(axis)
+def spread_band(per_band, axes):
+    size = lax.axis_size(axes)
     bands, rows, width = per_band.shape
     copies = jnp.broadcast_to(per_band[None], (size, bands, rows, width)).reshape(size * bands, rows, width)
-    every = lax.all_to_all(copies, (axis, "win"), split_axis=0, concat_axis=0, tiled=True)
+    every = lax.all_to_all(copies, axes + ("win",), split_axis=0, concat_axis=0, tiled=True)
     every = every.reshape(size, bands, rows, width).transpose(0, 2, 1, 3)
     return every.reshape(size * rows, bands * width)
 
@@ -111,10 +111,10 @@
     whitened = whitened.reshape(bands, local_rows, -1)
     windows = bands
     inverse_count = 1.0 / (windows * whitened.shape[2] // 2)
-    col_set = spread_band(whitened, "cb")
-    row_set = gather_blocks(spread_band(whitened, "cz"), "cx")
+    col_set = spread_band(whitened, ("cb",))
+    row_set = spread_band(whitened, ("cx", "cz"))
     operands = jnp.concatenate([col_set, swapped_parts(col_set, windows)], axis=0)
-    product = jnp.einsum("ik,jk->ij", row_set, operands, precision=lax.Precision.HIGHEST)
+    product = jnp.einsum("ik,jk->ij", row_set, operands, precision=lax.Precision.HIGH)
     product = (product * inverse_count).astype(jnp.bfloat16)
     product = product.reshape(group_x * group_z, local_rows, operands.shape[0])
     mine = lax.all_to_all(product, ("cx", "cz"), split_axis=0, concat_axis=0, tiled=True)

time: 114 us -> 123 us (1.079)
  the two profiles are of different devices: /device:TPU:72 before, /device:TPU:64 now
where the time goes in v12:
time: 123 us; the launch traced here: 122 us
  blocking collectives  37.9 us (31%)
  starting transfers between devices  30.8 us (25%)
  waiting for transfers between devices  29.9 us (24%)
  local copies, waits for them, and re-layouts  13.3 us (11%)
  other arithmetic  6.72 us (5%)
  matrix products  3.15 us (3%)
    all_to_all x1, blocking collectives, body(): lax.all_to_all(product, ('cx', 'cz'), split_axis=0, concat_axis=0, tiled=...  37.9 us
    all_to_all x2, waiting for transfers between devices, spread_band(): lax.all_to_all(copies, axes + ('win',), split_axis=0, concat_axis=0, tile...  29.9 us
    all_to_all x2, starting transfers between devices, spread_band(): lax.all_to_all(copies, axes + ('win',), split_axis=0, concat_axis=0, tile...  25 us
    ppermute x1, starting transfers between devices, with_halo(): before = lax.ppermute(last, CHAN, up)  4.55 us
    all_to_all x2, other arithmetic, spread_band(): lax.all_to_all(copies, axes + ('win',), split_axis=0, concat_axis=0, tile...  4.05 us
    unnamed x10, local copies, waits for them, and re-layouts  3.94 us
  transfers between devices with their start and end apart: 4, of which 2 were waited for; matrix products, arithmetic and copies ran while one was open for 9% of the time, Pallas kernels for 0%

profile of v12, /device:TPU:64, one launch (start us, length us, event | category | flops | bytes accessed | tf_op | source)
XLA Modules:
  0.0 122.1 jit_solution(7756820519497710565)
XLA Ops:
  0.0 0.8 fusion.23
  0.8 1.3 %collective-permute-start.1 = (bf16[8,1,1024]{2,0,1:T(8,128)(2,1)S(1)}, bf16[8,1,1024]{2,0,1:T(8,128)(2,1)S(1)}, u32[]{:S(2)}, u32[]{:S(2)}) collective-permute-start(bf16[8,1,1024]{2,0,1:T(8,128)(2,1)S(1)} %get-tuple-element.10), channel_id=1, source_target_pairs={{4,0},{8,4},{12,8},{16,12},{20,16},{24,20},{28,24},{32,28},{36,32}... | collective-permute-start | bytes 49160 | tf_op jit(solution)/shard_map/ppermute | solution.py:28
  2.1 4.5 %collective-permute-start = (bf16[8,1,1024]{2,0,1:T(8,128)(2,1)S(1)}, bf16[8,1,1024]{2,0,1:T(8,128)(2,1)S(1)}, u32[]{:S(2)}, u32[]{:S(2)}) collective-permute-start(bf16[8,1,1024]{2,0,1:T(8,128)(2,1)S(1)} %get-tuple-element.9), channel_id=1, source_target_pairs={{0,4},{4,8},{8,12},{12,16},{16,20},{20,24},{24,28},{28,32},{32,36}... | collective-permute-start | bytes 49160 | tf_op jit(solution)/shard_map/ppermute | solution.py:27
  6.7 0.8 pad_dynamic-slice_fusion
  7.5 0.9 select_reduce_fusion
  8.4 0.8 broadcast_compare_fusion
  9.3 0.8 convert_reduce_fusion.1
  10.2 1.2 fusion.3
  11.4 0.6 fusion.24
  12.5 1.2 %reshape.88 = f32[32,1,3072]{2,1,0:T(1,128)} reshape(f32[32,48,64]{2,1,0:T(8,128)S(1)} %bitcast.49) | data formatting | bytes 786432
  13.7 9.4 %all-to-all-start.1 = ((f32[32,1,3072]{2,1,0:T(1,128)}), f32[32,1,3072]{2,1,0:T(1,128)S(1)}, u32[]{:S(2)}, u32[]{:S(2)}) async-start(f32[32,1,3072]{2,1,0:T(1,128)} %reshape.88), calls=%async_computation.1 | async-start | bytes 786432 | tf_op jit(solution)/shard_map/all_to_all | solution.py:42
  23.3 1.9 %reshape.86 = f32[64,1,3072]{2,1,0:T(1,128)} reshape(f32[64,48,64]{2,1,0:T(8,128)S(1)} %bitcast.45) | data formatting | bytes 1572864
  25.1 12.9 %all-to-all-done.1 = f32[32,1,3072]{2,1,0:T(1,128)S(1)} async-done(((f32[32,1,3072]{2,1,0:T(1,128)}), f32[32,1,3072]{2,1,0:T(1,128)S(1)}, u32[]{:S(2)}, u32[]{:S(2)}) %all-to-all-start.1) | async-done | bytes 393248 | tf_op jit(solution)/shard_map/all_to_all | solution.py:42
  38.0 15.6 %all-to-all-start = ((f32[64,1,3072]{2,1,0:T(1,128)}), f32[64,1,3072]{2,1,0:T(1,128)S(1)}, u32[]{:S(2)}, u32[]{:S(2)}) async-start(f32[64,1,3072]{2,1,0:T(1,128)} %reshape.86), calls=%async_computation | async-start | bytes 1572864 | tf_op jit(solution)/shard_map/all_to_all | solution.py:42
  54.2 1.6 %reduce.1 = f32[32,3072]{1,0:T(8,128)S(1)} reduce(f32[32,1,3072]{2,1,0:T(1,128)S(1)} %all-to-all-done.1, f32[]{:T(128)} %broadcast.24), dimensions={1}, to_apply=%all_to_all.10.reduce_sub_computation | reduce | bytes 786436 | tf_op jit(solution)/shard_map/all_to_all | solution.py:42
  57.1 0.9 copy.30
  58.0 1.2 reshape.82
  59.2 17.0 %all-to-all-done = f32[64,1,3072]{2,1,0:T(1,128)S(1)} async-done(((f32[64,1,3072]{2,1,0:T(1,128)}), f32[64,1,3072]{2,1,0:T(1,128)S(1)}, u32[]{:S(2)}, u32[]{:S(2)}) %all-to-all-start) | async-done | bytes 786464 | tf_op jit(solution)/shard_map/all_to_all | solution.py:42
  76.3 2.5 %reduce = f32[64,3072]{1,0:T(8,128)S(1)} reduce(f32[64,1,3072]{2,1,0:T(1,128)S(1)} %all-to-all-done, f32[]{:T(128)} %broadcast.24), dimensions={1}, to_apply=%all_to_all.9.reduce_sub_computation | reduce | bytes 1572868 | tf_op jit(solution)/shard_map/all_to_all | solution.py:42
  79.2 0.6 copy.26
  79.8 0.9 reshape.79
  80.9 1.1 multiply_convert_fusion
  82.1 37.9 %all_to_all.15 = bf16[16,48,768]{2,1,0:T(8,128)(2,1)S(1)} all-to-all(bf16[16,48,768]{2,1,0:T(8,128)(2,1)S(1)} %bitcast.48), channel_id=1, replica_groups=mesh['cx'=4,'cz'=4,'cb'=8,'win'=4] {'cx','cz'}, dimensions={0} | all-to-all | bytes 2359296 | tf_op jit(solution)/shard_map/all_to_all | solution.py:120
  120.7 1.4 %broadcast_in_dim_reshape.2 = bf16[1,2,48,6144]{3,2,1,0:T(8,128)(2,1)} reshape(bf16[2,48,16,384]{3,2,1,0:T(8,128)(2,1)S(1)} %bitcast.47) | data formatting | bytes 2359296 | tf_op jit(solution)/shard_map/broadcast_in_dim;reshape | solution.py:123
  (29 shorter events, 4.0 us)
Async XLA Ops:
  0.0 11.4 %copy-start.2 = (f32[1024,256]{1,0:T(8,128)S(1)}, f32[1024,256]{1,0:T(8,128)}, u32[]{:S(2)}) copy-start(f32[1024,256]{1,0:T(8,128)} %constant.42.clone) | copy-start | bytes 3145732
  0.8 9.3 %collective-permute-start.1 = (bf16[8,1,1024]{2,0,1:T(8,128)(2,1)S(1)}, bf16[8,1,1024]{2,0,1:T(8,128)(2,1)S(1)}, u32[]{:S(2)}, u32[]{:S(2)}) collective-permute-start(bf16[8,1,1024]{2,0,1:T(8,128)(2,1)S(1)} %get-tuple-element.10), channel_id=1, source_target_pairs={{4,0},{8,4},{12,8},{16,12},{20,16},{24,20},{28,24},{32,28},{36,32}... | collective-permute-start | bytes 49160 | tf_op jit(solution)/shard_map/ppermute | solution.py:28
  2.1 8.1 %collective-permute-start = (bf16[8,1,1024]{2,0,1:T(8,128)(2,1)S(1)}, bf16[8,1,1024]{2,0,1:T(8,128)(2,1)S(1)}, u32[]{:S(2)}, u32[]{:S(2)}) collective-permute-start(bf16[8,1,1024]{2,0,1:T(8,128)(2,1)S(1)} %get-tuple-element.9), channel_id=1, source_target_pairs={{0,4},{4,8},{8,12},{12,16},{16,20},{20,24},{24,28},{28,32},{32,36}... | collective-permute-start | bytes 49160 | tf_op jit(solution)/shard_map/ppermute | solution.py:27
  13.7 24.3 %all-to-all-start.1 = ((f32[32,1,3072]{2,1,0:T(1,128)}), f32[32,1,3072]{2,1,0:T(1,128)S(1)}, u32[]{:S(2)}, u32[]{:S(2)}) async-start(f32[32,1,3072]{2,1,0:T(1,128)} %reshape.88), calls=%async_computation.1 | async-start | bytes 786432 | tf_op jit(solution)/shard_map/all_to_all | solution.py:42
  38.0 38.2 %all-to-all-start = ((f32[64,1,3072]{2,1,0:T(1,128)}), f32[64,1,3072]{2,1,0:T(1,128)S(1)}, u32[]{:S(2)}, u32[]{:S(2)}) async-start(f32[64,1,3072]{2,1,0:T(1,128)} %reshape.86), calls=%async_computation | async-start | bytes 1572864 | tf_op jit(solution)/shard_map/all_to_all | solution.py:42
  79.8 1.0 copy-start
  79.8 1.1 copy-start.1

commit v13 on v11

--- a/solution.py
+++ b/solution.py
@@ -42,6 +42,18 @@
     every = lax.all_to_all(copies, (axis, "win"), split_axis=0, concat_axis=0, tiled=True)
     every = every.reshape(size, bands, rows, width).transpose(0, 2, 1, 3)
     return every.reshape(size * rows, bands * width)
+
+def gather_by_permutes(block, axis):
+    size = lax.axis_size(axis)
+    me = lax.axis_index(axis)
+    pieces = [block]
+    for shift in range(1, size):
+        pairs = [(src, (src - shift) % size) for src in range(size)]
+        pieces.append(lax.ppermute(block, axis, pairs))
+    rel = jnp.concatenate(pieces + pieces, axis=0)
+    rows = block.shape[0]
+    start = ((size - me) % size) * rows
+    return lax.dynamic_slice_in_dim(rel, start, size * rows, axis=0)
 
 def fourier_table():
     sample_ids = np.arange(SAMPLES)
@@ -112,7 +124,7 @@
     windows = bands
     inverse_count = 1.0 / (windows * whitened.shape[2] // 2)
     col_set = spread_band(whitened, "cb")
-    row_set = gather_blocks(spread_band(whitened, "cz"), "cx")
+    row_set = gather_by_permutes(spread_band(whitened, "cz"), "cx")
     operands = jnp.concatenate([col_set, swapped_parts(col_set, windows)], axis=0)
     product = jnp.einsum("ik,jk->ij", row_set, operands, precision=lax.Precision.HIGHEST)
     product = (product * inverse_count).astype(jnp.bfloat16)

time: 114 us -> 113 us (level)
  the two profiles are of different devices: /device:TPU:72 before, /device:TPU:64 now
where the time goes in v13:
time: 113 us
  blocking collectives  59.4 us (53%)
  starting transfers between devices  20.8 us (18%)
  local copies, waits for them, and re-layouts  13.9 us (12%)
  waiting for transfers between devices  7.81 us (7%)
  other arithmetic  5.27 us (5%)
  matrix products  5.23 us (5%)
    all_to_all x1, blocking collectives, body(): lax.all_to_all(product, ('cx', 'cz'), split_axis=0, concat_axis=0, tiled=...  36.7 us
    all_to_all x1, blocking collectives, spread_band(): lax.all_to_all(copies, (axis, 'win'), split_axis=0, concat_axis=0, tiled=...  22.8 us
    ppermute x3, starting transfers between devices, gather_by_permutes(): pieces.append(lax.ppermute(block, axis, pairs))  10.1 us
    ppermute x3, waiting for transfers between devices, gather_by_permutes(): pieces.append(lax.ppermute(block, axis, pairs))  6.97 us
    unnamed x13, local copies, waits for them, and re-layouts  6.6 us
    all_to_all x1, starting transfers between devices, spread_band(): lax.all_to_all(copies, (axis, 'win'), split_axis=0, concat_axis=0, tiled=...  5.89 us
    ppermute x1, starting transfers between devices, with_halo(): before = lax.ppermute(last, CHAN, up)  3.47 us
    dot_general x1, matrix products, body(): jnp.einsum('ik,jk->ij', row_set, operands, precision=lax.Precision.HIGHEST)  3.23 us
  transfers between devices with their start and end apart: 6, of which 3 were waited for; matrix products, arithmetic and copies ran while one was open for 9% of the time, Pallas kernels for 0%

profile of v13, /device:TPU:64, one launch (start us, length us, event | category | flops | bytes accessed | tf_op | source)
XLA Modules:
  0.0 112.7 jit_solution(7515045297659173928)
XLA Ops:
  0.0 0.8 fusion.25
  0.8 3.5 %collective-permute-start = (bf16[8,1,1024]{2,0,1:T(8,128)(2,1)S(1)}, bf16[8,1,1024]{2,0,1:T(8,128)(2,1)S(1)}, u32[]{:S(2)}, u32[]{:S(2)}) collective-permute-start(bf16[8,1,1024]{2,0,1:T(8,128)(2,1)S(1)} %get-tuple-element.9), channel_id=1, source_target_pairs={{0,4},{4,8},{8,12},{12,16},{16,20},{20,24},{24,28},{28,32},{32,36}... | collective-permute-start | bytes 49160 | tf_op jit(solution)/shard_map/ppermute | solution.py:27
  4.3 1.3 %collective-permute-start.1 = (bf16[8,1,1024]{2,0,1:T(8,128)(2,1)S(1)}, bf16[8,1,1024]{2,0,1:T(8,128)(2,1)S(1)}, u32[]{:S(2)}, u32[]{:S(2)}) collective-permute-start(bf16[8,1,1024]{2,0,1:T(8,128)(2,1)S(1)} %get-tuple-element.10), channel_id=1, source_target_pairs={{4,0},{8,4},{12,8},{16,12},{20,16},{24,20},{28,24},{32,28},{36,32}... | collective-permute-start | bytes 49160 | tf_op jit(solution)/shard_map/ppermute | solution.py:28
  5.6 0.8 pad_dynamic-slice_fusion
  6.5 0.9 select_reduce_fusion
  7.3 0.8 broadcast_compare_fusion
  8.2 0.8 convert_reduce_fusion.1
  9.1 0.8 collective-permute-done.1
  9.9 1.2 %fusion.3 = f32[48,1024]{1,0:T(8,128)S(1)} fusion(bf16[48,1,1024]{2,0,1:T(8,128)(2,1)} %param.5, bf16[8,1,1024]{2,0,1:T(8,128)(2,1)S(1)} %collective-permute-done.1, bf16[8,1,1024]{2,0,1:T(8,128)(2,1)S(1)} %collective-permute-done, f32[48]{0:T(128)S(1)} %broadcast_maximum_fusion, f32[48]{0:T(128)S(1)} %get-tuple-element.12, ...), kind=kOutput, calls=%fused_computation.6 | convolution fusion | flops 6899712 | bytes 328960 | tf_op jit(solution)/shard_map/cr,rwt->cwt/dot_general | solution.py:108
  12.5 22.8 %all_to_all.15 = f32[16,1,3072]{2,1,0:T(1,128)S(1)} all-to-all(f32[16,1,3072]{2,1,0:T(1,128)S(1)} %reshape.88), channel_id=1, replica_groups=mesh['cx'=4,'cz'=4,'cb'=8,'win'=4] {'cz','win'}, dimensions={0} | all-to-all | bytes 393216 | tf_op jit(solution)/shard_map/all_to_all | solution.py:42
  35.8 1.1 reduce.1
  37.4 4.6 %collective-permute-start.2 = (f32[192,256]{1,0:T(8,128)S(1)}, f32[192,256]{1,0:T(8,128)S(1)}, u32[]{:S(2)}, u32[]{:S(2)}) collective-permute-start(f32[192,256]{1,0:T(8,128)S(1)} %reshape.79), channel_id=1, source_target_pairs={{0,384},{128,0},{256,128},{384,256},{1,385},{129,1},{257,129},{385... | collective-permute-start | bytes 589832 | tf_op jit(solution)/shard_map/ppermute | solution.py:52
  42.1 1.2 %reshape.86 = f32[32,1,3072]{2,1,0:T(1,128)} reshape(f32[32,48,64]{2,1,0:T(8,128)S(1)} %bitcast.46) | data formatting | bytes 786432
  43.4 5.9 %all-to-all-start.1 = ((f32[32,1,3072]{2,1,0:T(1,128)}), f32[32,1,3072]{2,1,0:T(1,128)S(1)}, u32[]{:S(2)}, u32[]{:S(2)}) async-start(f32[32,1,3072]{2,1,0:T(1,128)} %reshape.86), calls=%async_computation.1 | async-start | bytes 786432 | tf_op jit(solution)/shard_map/all_to_all | solution.py:42
  49.3 2.7 %collective-permute-start.3 = (f32[192,256]{1,0:T(8,128)S(1)}, f32[192,256]{1,0:T(8,128)S(1)}, u32[]{:S(2)}, u32[]{:S(2)}) collective-permute-start(f32[192,256]{1,0:T(8,128)S(1)} %reshape.79), channel_id=1, source_target_pairs={{0,256},{128,384},{256,0},{384,128},{1,257},{129,385},{257,1},{385... | collective-permute-start | bytes 589832 | tf_op jit(solution)/shard_map/ppermute | solution.py:52
  52.0 2.8 %collective-permute-start.4 = (f32[192,256]{1,0:T(8,128)S(1)}, f32[192,256]{1,0:T(8,128)S(1)}, u32[]{:S(2)}, u32[]{:S(2)}) collective-permute-start(f32[192,256]{1,0:T(8,128)S(1)} %reshape.79), channel_id=1, source_target_pairs={{0,128},{128,256},{256,384},{384,0},{1,129},{129,257},{257,385},{3... | collective-permute-start | bytes 589832 | tf_op jit(solution)/shard_map/ppermute | solution.py:52
  55.5 0.7 constant_dynamic-update-slice_fusion.6
  56.2 4.2 %collective-permute-done.3 = f32[192,256]{1,0:T(8,128)S(1)} collective-permute-done((f32[192,256]{1,0:T(8,128)S(1)}, f32[192,256]{1,0:T(8,128)S(1)}, u32[]{:S(2)}, u32[]{:S(2)}) %collective-permute-start.3) | collective-permute-done | bytes 196640 | tf_op jit(solution)/shard_map/ppermute | solution.py:52
  61.1 2.7 %collective-permute-done.4 = f32[192,256]{1,0:T(8,128)S(1)} collective-permute-done((f32[192,256]{1,0:T(8,128)S(1)}, f32[192,256]{1,0:T(8,128)S(1)}, u32[]{:S(2)}, u32[]{:S(2)}) %collective-permute-start.4) | collective-permute-done | bytes 196640 | tf_op jit(solution)/shard_map/ppermute | solution.py:52
  66.6 0.7 constant_dynamic-update-slice_fusion
  67.3 1.5 %reduce = f32[32,3072]{1,0:T(8,128)S(1)} reduce(f32[32,1,3072]{2,1,0:T(1,128)S(1)} %all-to-all-done.1, f32[]{:T(128)} %broadcast.25), dimensions={1}, to_apply=%all_to_all.10.reduce_sub_computation | reduce | bytes 786436 | tf_op jit(solution)/shard_map/all_to_all | solution.py:42
  70.8 3.2 %multiply_convert_fusion = bf16[768,768]{1,0:T(8,128)(2,1)S(1)} fusion(f32[384,256]{1,0:T(8,128)S(1)} %copy.30, f32[384,256]{1,0:T(8,128)S(1)} %reshape.82, f32[1536,256]{1,0:T(8,128)} %constant_dynamic-update-slice_fusion, s32[]{:T(128)S(6)} %select_n.25), kind=kOutput, calls=%fused_computation | convolution fusion | flops 1813315584 | bytes 2752516 | tf_op jit(solution)/shard_map/ik,jk->ij/dot_general | solution.py:129
  74.0 36.7 %all_to_all.16 = bf16[16,48,768]{2,1,0:T(8,128)(2,1)S(1)} all-to-all(bf16[16,48,768]{2,1,0:T(8,128)(2,1)S(1)} %bitcast.44), channel_id=1, replica_groups=mesh['cx'=4,'cz'=4,'cb'=8,'win'=4] {'cx','cz'}, dimensions={0} | all-to-all | bytes 2359296 | tf_op jit(solution)/shard_map/all_to_all | solution.py:132
  111.4 1.4 %broadcast_in_dim_reshape.2 = bf16[1,2,48,6144]{3,2,1,0:T(8,128)(2,1)} reshape(bf16[2,48,16,384]{3,2,1,0:T(8,128)(2,1)S(1)} %bitcast.45) | data formatting | bytes 2359296 | tf_op jit(solution)/shard_map/broadcast_in_dim;reshape | solution.py:135
  (38 shorter events, 9.3 us)
Async XLA Ops:
  0.0 11.1 %copy-start = (f32[1024,256]{1,0:T(8,128)S(1)}, f32[1024,256]{1,0:T(8,128)}, u32[]{:S(2)}) copy-start(f32[1024,256]{1,0:T(8,128)} %constant.56.clone) | copy-start | bytes 3145732
  0.8 8.3 %collective-permute-start = (bf16[8,1,1024]{2,0,1:T(8,128)(2,1)S(1)}, bf16[8,1,1024]{2,0,1:T(8,128)(2,1)S(1)}, u32[]{:S(2)}, u32[]{:S(2)}) collective-permute-start(bf16[8,1,1024]{2,0,1:T(8,128)(2,1)S(1)} %get-tuple-element.9), channel_id=1, source_target_pairs={{0,4},{4,8},{8,12},{12,16},{16,20},{20,24},{24,28},{28,32},{32,36}... | collective-permute-start | bytes 49160 | tf_op jit(solution)/shard_map/ppermute | solution.py:27
  4.3 5.6 %collective-permute-start.1 = (bf16[8,1,1024]{2,0,1:T(8,128)(2,1)S(1)}, bf16[8,1,1024]{2,0,1:T(8,128)(2,1)S(1)}, u32[]{:S(2)}, u32[]{:S(2)}) collective-permute-start(bf16[8,1,1024]{2,0,1:T(8,128)(2,1)S(1)} %get-tuple-element.10), channel_id=1, source_target_pairs={{4,0},{8,4},{12,8},{16,12},{20,16},{24,20},{28,24},{32,28},{36,32}... | collective-permute-start | bytes 49160 | tf_op jit(solution)/shard_map/ppermute | solution.py:28
  37.4 18.1 %collective-permute-start.2 = (f32[192,256]{1,0:T(8,128)S(1)}, f32[192,256]{1,0:T(8,128)S(1)}, u32[]{:S(2)}, u32[]{:S(2)}) collective-permute-start(f32[192,256]{1,0:T(8,128)S(1)} %reshape.79), channel_id=1, source_target_pairs={{0,384},{128,0},{256,128},{384,256},{1,385},{129,1},{257,129},{385... | collective-permute-start | bytes 589832 | tf_op jit(solution)/shard_map/ppermute | solution.py:52
  43.4 23.9 %all-to-all-start.1 = ((f32[32,1,3072]{2,1,0:T(1,128)}), f32[32,1,3072]{2,1,0:T(1,128)S(1)}, u32[]{:S(2)}, u32[]{:S(2)}) async-start(f32[32,1,3072]{2,1,0:T(1,128)} %reshape.86), calls=%async_computation.1 | async-start | bytes 786432 | tf_op jit(solution)/shard_map/all_to_all | solution.py:42
  49.3 11.1 %collective-permute-start.3 = (f32[192,256]{1,0:T(8,128)S(1)}, f32[192,256]{1,0:T(8,128)S(1)}, u32[]{:S(2)}, u32[]{:S(2)}) collective-permute-start(f32[192,256]{1,0:T(8,128)S(1)} %reshape.79), channel_id=1, source_target_pairs={{0,256},{128,384},{256,0},{384,128},{1,257},{129,385},{257,1},{385... | collective-permute-start | bytes 589832 | tf_op jit(solution)/shard_map/ppermute | solution.py:52
  52.0 11.8 %collective-permute-start.4 = (f32[192,256]{1,0:T(8,128)S(1)}, f32[192,256]{1,0:T(8,128)S(1)}, u32[]{:S(2)}, u32[]{:S(2)}) collective-permute-start(f32[192,256]{1,0:T(8,128)S(1)} %reshape.79), channel_id=1, source_target_pairs={{0,128},{128,256},{256,384},{384,0},{1,129},{129,257},{257,385},{3... | collective-permute-start | bytes 589832 | tf_op jit(solution)/shard_map/ppermute | solution.py:52

commit v14 on v12

--- a/solution.py
+++ b/solution.py
@@ -111,14 +111,14 @@
     whitened = whitened.reshape(bands, local_rows, -1)
     windows = bands
     inverse_count = 1.0 / (windows * whitened.shape[2] // 2)
-    col_set = spread_band(whitened, ("cb",))
-    row_set = spread_band(whitened, ("cx", "cz"))
+    col_set = spread_band(whitened, ("cz", "cb"))
+    row_set = spread_band(whitened, ("cx",))
     operands = jnp.concatenate([col_set, swapped_parts(col_set, windows)], axis=0)
-    product = jnp.einsum("ik,jk->ij", row_set, operands, precision=lax.Precision.HIGH)
+    product = jnp.einsum("ik,jk->ij", row_set, operands, precision=lax.Precision.HIGHEST)
     product = (product * inverse_count).astype(jnp.bfloat16)
-    product = product.reshape(group_x * group_z, local_rows, operands.shape[0])
-    mine = lax.all_to_all(product, ("cx", "cz"), split_axis=0, concat_axis=0, tiled=True)
-    mine = mine.reshape(group_x * group_z, local_rows, 2, col_set.shape[0])
+    product = product.reshape(group_x, local_rows, operands.shape[0])
+    mine = lax.all_to_all(product, "cx", split_axis=0, concat_axis=0, tiled=True)
+    mine = mine.reshape(group_x, local_rows, 2, col_set.shape[0])
     cross_spectra = mine.transpose(2, 1, 0, 3).reshape(2, local_rows, -1)
     return cross_spectra[None]
 

time: 123 us -> 141 us (1.15)
  the two profiles are of different devices: /device:TPU:64 before, /device:TPU:1 now
where the time goes in v14:
time: 141 us; the launch traced here: 140 us
  waiting for transfers between devices  42.1 us (30%)
  starting transfers between devices  31.5 us (22%)
  local copies, waits for them, and re-layouts  30.3 us (21%)
  blocking collectives  17.4 us (12%)
  other arithmetic  11.2 us (8%)
  matrix products  7.17 us (5%)
    all_to_all x2, waiting for transfers between devices, spread_band(): lax.all_to_all(copies, axes + ('win',), split_axis=0, concat_axis=0, tile...  42.1 us
    all_to_all x2, starting transfers between devices, spread_band(): lax.all_to_all(copies, axes + ('win',), split_axis=0, concat_axis=0, tile...  26.2 us
    all_to_all x1, blocking collectives, body(): lax.all_to_all(product, 'cx', split_axis=0, concat_axis=0, tiled=True)  17.4 us
    transpose x3, local copies, waits for them, and re-layouts, spread_band(): every = every.reshape(size, bands, rows, width).transpose(0, 2, 1, 3)  7.61 us
    all_to_all x2, other arithmetic, spread_band(): lax.all_to_all(copies, axes + ('win',), split_axis=0, concat_axis=0, tile...  7.1 us
    unnamed x8, local copies, waits for them, and re-layouts  5.91 us
    dot_general x1, matrix products, body(): jnp.einsum('ik,jk->ij', row_set, operands, precision=lax.Precision.HIGHEST)  5.17 us
    another operation x1, local copies, waits for them, and re-layouts, swapped_parts(): parts = flat.reshape(flat.shape[:-1] + (windows, 2, -1))  4.45 us
  transfers between devices with their start and end apart: 4, of which 2 were waited for; matrix products, arithmetic and copies ran while one was open for 6% of the time, Pallas kernels for 0%

profile of v14, /device:TPU:1, one launch (start us, length us, event | category | flops | bytes accessed | tf_op | source)
XLA Modules:
  0.0 139.8 jit_solution(17315420448107646436)
XLA Ops:
  0.8 4.0 %collective-permute-start = (bf16[8,1,1024]{2,0,1:T(8,128)(2,1)S(1)}, bf16[8,1,1024]{2,0,1:T(8,128)(2,1)S(1)}, u32[]{:S(2)}, u32[]{:S(2)}) collective-permute-start(bf16[8,1,1024]{2,0,1:T(8,128)(2,1)S(1)} %get-tuple-element.9), channel_id=1, source_target_pairs={{0,4},{4,8},{8,12},{12,16},{16,20},{20,24},{24,28},{28,32},{32,36}... | collective-permute-start | bytes 49160 | tf_op jit(solution)/shard_map/ppermute | solution.py:27
  4.9 1.3 collective-permute-start.1
  7.0 0.9 select_reduce_fusion
  9.7 1.2 fusion.7
  12.0 0.9 reshape.86
  12.9 17.2 %all-to-all-start = ((f32[16,1,3072]{2,1,0:T(1,128)}), f32[16,1,3072]{2,1,0:T(1,128)S(1)}, u32[]{:S(2)}, u32[]{:S(2)}) async-start(f32[16,1,3072]{2,1,0:T(1,128)} %reshape.86), calls=%async_computation | async-start | bytes 393216 | tf_op jit(solution)/shard_map/all_to_all | solution.py:42
  30.4 2.9 %reshape.88 = f32[128,1,3072]{2,1,0:T(1,128)} reshape(f32[128,48,64]{2,1,0:T(8,128)S(1)} %bitcast.43) | data formatting | bytes 3145728
  33.3 3.4 %all-to-all-done = f32[16,1,3072]{2,1,0:T(1,128)S(1)} async-done(((f32[16,1,3072]{2,1,0:T(1,128)}), f32[16,1,3072]{2,1,0:T(1,128)S(1)}, u32[]{:S(2)}, u32[]{:S(2)}) %all-to-all-start) | async-done | bytes 196640 | tf_op jit(solution)/shard_map/all_to_all | solution.py:42
  36.7 9.0 %all-to-all-start.1 = ((f32[128,1,3072]{2,1,0:T(1,128)}), f32[128,1,3072]{2,1,0:T(1,128)S(1)}, u32[]{:S(2)}, u32[]{:S(2)}) async-start(f32[128,1,3072]{2,1,0:T(1,128)} %reshape.88), calls=%async_computation.1 | async-start | bytes 3145728 | tf_op jit(solution)/shard_map/all_to_all | solution.py:42
  46.2 1.1 reduce
  47.9 38.6 %all-to-all-done.1 = f32[128,1,3072]{2,1,0:T(1,128)S(1)} async-done(((f32[128,1,3072]{2,1,0:T(1,128)}), f32[128,1,3072]{2,1,0:T(1,128)S(1)}, u32[]{:S(2)}, u32[]{:S(2)}) %all-to-all-start.1) | async-done | bytes 1572896 | tf_op jit(solution)/shard_map/all_to_all | solution.py:42
  86.5 6.0 %reduce.1 = f32[128,3072]{1,0:T(8,128)} reduce(f32[128,1,3072]{2,1,0:T(1,128)S(1)} %all-to-all-done.1, f32[]{:T(128)} %broadcast.24), dimensions={1}, to_apply=%all_to_all.10.reduce_sub_computation | reduce | bytes 3145732 | tf_op jit(solution)/shard_map/all_to_all | solution.py:42
  92.5 2.0 %reshape.89 = f32[128,48,64]{2,1,0:T(8,128)S(1)} reshape(f32[128,3072]{1,0:T(8,128)} %reduce.1) | data formatting | bytes 3145728
  94.5 4.6 %copy.29 = f32[32,48,4,64]{1,0,3,2:T(8,128)} copy(f32[32,48,4,64]{3,1,2,0:T(8,128)S(1)} %bitcast.41) | data formatting | bytes 3145728 | tf_op jit(solution)/shard_map/transpose | solution.py:43
  99.1 2.9 %copy.28 = f32[32,48,4,64]{3,2,1,0:T(4,128)} copy(f32[32,48,4,64]{3,1,2,0:T(8,128)S(1)} %bitcast.42) | data formatting | bytes 3145728 | tf_op jit(solution)/shard_map/transpose | solution.py:43
  102.0 4.4 %reshape_reshape.3 = f32[1536,4,2,32]{0,3,2,1:T(8,128)S(1)} reshape(f32[32,48,4,64]{1,0,3,2:T(8,128)} %copy.29) | data formatting | bytes 3145728 | tf_op jit(solution)/shard_map/reshape;reshape | solution.py:63
  106.6 1.3 pad_maximum_fusion
  107.9 3.2 %copy.30 = f32[1536,256]{1,0:T(8,128)} copy(f32[1536,256]{0,1:T(8,128)} %bitcast.44) | data formatting | bytes 3145728 | tf_op jit(solution)/shard_map/reshape | solution.py:65
  111.1 2.6 %reshape.82 = f32[1536,256]{1,0:T(8,128)} reshape(f32[32,48,4,64]{3,2,1,0:T(4,128)S(1)} %copy-done) | data formatting | bytes 3145728 | tf_op jit(solution)/shard_map/reshape | solution.py:44
  113.7 5.2 %fusion = bf16[192,3072]{1,0:T(8,128)(2,1)S(1)} fusion(f32[192,256]{1,0:T(8,128)S(1)} %reshape.79, f32[1536,256]{1,0:T(8,128)} %copy.30, f32[1536,256]{1,0:T(8,128)} %reshape.82), kind=kOutput, calls=%fused_computation.1 | convolution fusion | flops 1813905408 | bytes 4521984 | tf_op jit(solution)/shard_map/ik,jk->ij/dot_general | solution.py:117
  118.9 17.4 %all_to_all.15 = bf16[4,48,3072]{2,1,0:T(8,128)(2,1)S(1)} all-to-all(bf16[4,48,3072]{2,1,0:T(8,128)(2,1)S(1)} %bitcast.46), channel_id=1, replica_groups=mesh['cx'=4,'cz'=4,'cb'=8,'win'=4] {'cx'}, dimensions={0} | all-to-all | bytes 2359296 | tf_op jit(solution)/shard_map/all_to_all | solution.py:120
  136.3 0.9 reshape.85
  137.2 0.9 copy.33
  138.1 1.7 %broadcast_in_dim_reshape.2 = bf16[1,2,48,6144]{3,2,1,0:T(8,128)(2,1)} reshape(bf16[2,48,4,1536]{3,2,1,0:T(4,128)(2,1)S(1)} %bitcast.45) | data formatting | bytes 2359296 | tf_op jit(solution)/shard_map/broadcast_in_dim;reshape | solution.py:123
  (27 shorter events, 6.0 us)
Async XLA Ops:
  0.0 10.9 %copy-start.1 = (f32[1024,256]{1,0:T(8,128)S(1)}, f32[1024,256]{1,0:T(8,128)}, u32[]{:S(2)}) copy-start(f32[1024,256]{1,0:T(8,128)} %constant.42.clone) | copy-start | bytes 3145732
  0.8 8.8 %collective-permute-start = (bf16[8,1,1024]{2,0,1:T(8,128)(2,1)S(1)}, bf16[8,1,1024]{2,0,1:T(8,128)(2,1)S(1)}, u32[]{:S(2)}, u32[]{:S(2)}) collective-permute-start(bf16[8,1,1024]{2,0,1:T(8,128)(2,1)S(1)} %get-tuple-element.9), channel_id=1, source_target_pairs={{0,4},{4,8},{8,12},{12,16},{16,20},{20,24},{24,28},{28,32},{32,36}... | collective-permute-start | bytes 49160 | tf_op jit(solution)/shard_map/ppermute | solution.py:27
  4.9 4.8 %collective-permute-start.1 = (bf16[8,1,1024]{2,0,1:T(8,128)(2,1)S(1)}, bf16[8,1,1024]{2,0,1:T(8,128)(2,1)S(1)}, u32[]{:S(2)}, u32[]{:S(2)}) collective-permute-start(bf16[8,1,1024]{2,0,1:T(8,128)(2,1)S(1)} %get-tuple-element.10), channel_id=1, source_target_pairs={{4,0},{8,4},{12,8},{16,12},{20,16},{24,20},{28,24},{32,28},{36,32}... | collective-permute-start | bytes 49160 | tf_op jit(solution)/shard_map/ppermute | solution.py:28
  12.9 23.9 %all-to-all-start = ((f32[16,1,3072]{2,1,0:T(1,128)}), f32[16,1,3072]{2,1,0:T(1,128)S(1)}, u32[]{:S(2)}, u32[]{:S(2)}) async-start(f32[16,1,3072]{2,1,0:T(1,128)} %reshape.86), calls=%async_computation | async-start | bytes 393216 | tf_op jit(solution)/shard_map/all_to_all | solution.py:42
  36.7 49.8 %all-to-all-start.1 = ((f32[128,1,3072]{2,1,0:T(1,128)}), f32[128,1,3072]{2,1,0:T(1,128)S(1)}, u32[]{:S(2)}, u32[]{:S(2)}) async-start(f32[128,1,3072]{2,1,0:T(1,128)} %reshape.88), calls=%async_computation.1 | async-start | bytes 3145728 | tf_op jit(solution)/shard_map/all_to_all | solution.py:42
  107.9 3.2 %copy-start = (f32[32,48,4,64]{3,2,1,0:T(4,128)S(1)}, f32[32,48,4,64]{3,2,1,0:T(4,128)}, u32[]{:S(2)}) copy-start(f32[32,48,4,64]{3,2,1,0:T(4,128)} %copy.28) | copy-start | bytes 4718596

commit v15 on v11

--- a/solution.py
+++ b/solution.py
@@ -112,14 +112,14 @@
     windows = bands
     inverse_count = 1.0 / (windows * whitened.shape[2] // 2)
     col_set = spread_band(whitened, "cb")
-    row_set = gather_blocks(spread_band(whitened, "cz"), "cx")
+    row_set = gather_blocks(spread_band(whitened, "cx"), "cz")
     operands = jnp.concatenate([col_set, swapped_parts(col_set, windows)], axis=0)
     product = jnp.einsum("ik,jk->ij", row_set, operands, precision=lax.Precision.HIGHEST)
     product = (product * inverse_count).astype(jnp.bfloat16)
-    product = product.reshape(group_x * group_z, local_rows, operands.shape[0])
-    mine = lax.all_to_all(product, ("cx", "cz"), split_axis=0, concat_axis=0, tiled=True)
-    mine = mine.reshape(group_x * group_z, local_rows, 2, col_set.shape[0])
-    cross_spectra = mine.transpose(2, 1, 0, 3).reshape(2, local_rows, -1)
+    product = product.reshape(group_z * group_x, local_rows, operands.shape[0])
+    mine = lax.all_to_all(product, ("cz", "cx"), split_axis=0, concat_axis=0, tiled=True)
+    mine = mine.reshape(group_z, group_x, local_rows, 2, col_set.shape[0])
+    cross_spectra = mine.transpose(3, 2, 1, 0, 4).reshape(2, local_rows, -1)
     return cross_spectra[None]
 
 

time: 114 us -> 120 us (1.053)
  the two profiles are of different devices: /device:TPU:72 before, /device:TPU:80 now
where the time goes in v15:
time: 120 us; the launch traced here: 119 us
  waiting for transfers between devices  34.7 us (29%)
  blocking collectives  33.6 us (28%)
  starting transfers between devices  30.3 us (25%)
  local copies, waits for them, and re-layouts  10.9 us (9%)
  other arithmetic  5.45 us (5%)
  matrix products  4.09 us (3%)
    all_to_all x1, blocking collectives, body(): lax.all_to_all(product, ('cz', 'cx'), split_axis=0, concat_axis=0, tiled=...  33.6 us
    all_to_all x2, starting transfers between devices, spread_band(): lax.all_to_all(copies, (axis, 'win'), split_axis=0, concat_axis=0, tiled=...  19.3 us
    all_to_all x1, waiting for transfers between devices, gather_blocks(): lax.all_to_all(copies, axis, split_axis=0, concat_axis=0, tiled=True)  19.1 us
    all_to_all x2, waiting for transfers between devices, spread_band(): lax.all_to_all(copies, (axis, 'win'), split_axis=0, concat_axis=0, tiled=...  15.1 us
    all_to_all x1, starting transfers between devices, gather_blocks(): lax.all_to_all(copies, axis, split_axis=0, concat_axis=0, tiled=True)  5.2 us
    ppermute x1, starting transfers between devices, with_halo(): before = lax.ppermute(last, CHAN, up)  3.47 us
    all_to_all x2, other arithmetic, spread_band(): lax.all_to_all(copies, (axis, 'win'), split_axis=0, concat_axis=0, tiled=...  2.76 us
    unnamed x6, local copies, waits for them, and re-layouts  2.46 us
  transfers between devices with their start and end apart: 5, of which 4 were waited for; matrix products, arithmetic and copies ran while one was open for 9% of the time, Pallas kernels for 0%

profile of v15, /device:TPU:80, one launch (start us, length us, event | category | flops | bytes accessed | tf_op | source)
XLA Modules:
  0.0 119.2 jit_solution(13789634991986140148)
XLA Ops:
  0.0 0.8 fusion.23
  0.8 3.5 %collective-permute-start = (bf16[8,1,1024]{2,0,1:T(8,128)(2,1)S(1)}, bf16[8,1,1024]{2,0,1:T(8,128)(2,1)S(1)}, u32[]{:S(2)}, u32[]{:S(2)}) collective-permute-start(bf16[8,1,1024]{2,0,1:T(8,128)(2,1)S(1)} %get-tuple-element.9), channel_id=1, source_target_pairs={{0,4},{4,8},{8,12},{12,16},{16,20},{20,24},{24,28},{28,32},{32,36}... | collective-permute-start | bytes 49160 | tf_op jit(solution)/shard_map/ppermute | solution.py:27
  4.3 2.4 %collective-permute-start.1 = (bf16[8,1,1024]{2,0,1:T(8,128)(2,1)S(1)}, bf16[8,1,1024]{2,0,1:T(8,128)(2,1)S(1)}, u32[]{:S(2)}, u32[]{:S(2)}) collective-permute-start(bf16[8,1,1024]{2,0,1:T(8,128)(2,1)S(1)} %get-tuple-element.10), channel_id=1, source_target_pairs={{4,0},{8,4},{12,8},{16,12},{20,16},{24,20},{28,24},{32,28},{36,32}... | collective-permute-start | bytes 49160 | tf_op jit(solution)/shard_map/ppermute | solution.py:28
  6.7 0.8 pad_dynamic-slice_fusion
  7.5 0.9 select_reduce_fusion
  8.4 0.8 broadcast_compare_fusion
  9.3 0.8 convert_reduce_fusion.1
  10.7 1.2 %fusion.3 = f32[48,1024]{1,0:T(8,128)S(1)} fusion(bf16[48,1,1024]{2,0,1:T(8,128)(2,1)} %param.5, bf16[8,1,1024]{2,0,1:T(8,128)(2,1)S(1)} %collective-permute-done.1, bf16[8,1,1024]{2,0,1:T(8,128)(2,1)S(1)} %collective-permute-done, f32[48]{0:T(128)S(1)} %broadcast_maximum_fusion, f32[48]{0:T(128)S(1)} %get-tuple-element.12, ...), kind=kOutput, calls=%fused_computation.6 | convolution fusion | flops 6899712 | bytes 328960 | tf_op jit(solution)/shard_map/cr,rwt->cwt/dot_general | solution.py:96
  11.9 0.6 fusion.24
  13.0 0.9 reshape.87
  13.9 5.8 %all-to-all-start = ((f32[16,1,3072]{2,1,0:T(1,128)}), f32[16,1,3072]{2,1,0:T(1,128)S(1)}, u32[]{:S(2)}, u32[]{:S(2)}) async-start(f32[16,1,3072]{2,1,0:T(1,128)} %reshape.87), calls=%async_computation | async-start | bytes 393216 | tf_op jit(solution)/shard_map/all_to_all | solution.py:42
  19.7 1.2 %reshape.89 = f32[32,1,3072]{2,1,0:T(1,128)} reshape(f32[32,48,64]{2,1,0:T(8,128)S(1)} %bitcast.46) | data formatting | bytes 786432
  21.0 4.5 %all-to-all-done = f32[16,1,3072]{2,1,0:T(1,128)S(1)} async-done(((f32[16,1,3072]{2,1,0:T(1,128)}), f32[16,1,3072]{2,1,0:T(1,128)S(1)}, u32[]{:S(2)}, u32[]{:S(2)}) %all-to-all-start) | async-done | bytes 196640 | tf_op jit(solution)/shard_map/all_to_all | solution.py:42
  25.5 13.5 %all-to-all-start.2 = ((f32[32,1,3072]{2,1,0:T(1,128)}), f32[32,1,3072]{2,1,0:T(1,128)S(1)}, u32[]{:S(2)}, u32[]{:S(2)}) async-start(f32[32,1,3072]{2,1,0:T(1,128)} %reshape.89), calls=%async_computation.2 | async-start | bytes 786432 | tf_op jit(solution)/shard_map/all_to_all | solution.py:42
  39.6 1.1 reduce
  41.3 10.5 %all-to-all-done.2 = f32[32,1,3072]{2,1,0:T(1,128)S(1)} async-done(((f32[32,1,3072]{2,1,0:T(1,128)}), f32[32,1,3072]{2,1,0:T(1,128)S(1)}, u32[]{:S(2)}, u32[]{:S(2)}) %all-to-all-start.2) | async-done | bytes 393248 | tf_op jit(solution)/shard_map/all_to_all | solution.py:42
  51.8 0.9 broadcast_in_dim.29
  52.8 5.2 %all-to-all-start.1 = ((f32[4,192,256]{2,1,0:T(8,128)}), f32[4,192,256]{2,1,0:T(8,128)S(1)}, u32[]{:S(2)}, u32[]{:S(2)}) async-start(f32[4,192,256]{2,1,0:T(8,128)} %broadcast_in_dim.29), calls=%async_computation.1 | async-start | bytes 1572864 | tf_op jit(solution)/shard_map/all_to_all | solution.py:35
  58.0 1.6 %reduce.1 = f32[32,3072]{1,0:T(8,128)S(1)} reduce(f32[32,1,3072]{2,1,0:T(1,128)S(1)} %all-to-all-done.2, f32[]{:T(128)} %broadcast.24), dimensions={1}, to_apply=%all_to_all.14.reduce_sub_computation | reduce | bytes 786436 | tf_op jit(solution)/shard_map/all_to_all | solution.py:42
  61.5 19.1 %all-to-all-done.1 = f32[4,192,256]{2,1,0:T(8,128)S(1)} async-done(((f32[4,192,256]{2,1,0:T(8,128)}), f32[4,192,256]{2,1,0:T(8,128)S(1)}, u32[]{:S(2)}, u32[]{:S(2)}) %all-to-all-start.1) | async-done | bytes 786464 | tf_op jit(solution)/shard_map/all_to_all | solution.py:35
  80.7 2.1 %multiply_convert_fusion = bf16[768,768]{1,0:T(8,128)(2,1)S(1)} fusion(f32[768,256]{1,0:T(8,128)S(1)} %bitcast.47, f32[384,256]{1,0:T(8,128)S(1)} %copy.30, f32[384,256]{1,0:T(8,128)S(1)} %reshape.83), kind=kOutput, calls=%fused_computation | convolution fusion | flops 1813315584 | bytes 2752512 | tf_op jit(solution)/shard_map/ik,jk->ij/dot_general | solution.py:117
  82.8 33.6 %all_to_all.20 = bf16[16,48,768]{2,1,0:T(8,128)(2,1)S(1)} all-to-all(bf16[16,48,768]{2,1,0:T(8,128)(2,1)S(1)} %bitcast.45), channel_id=1, replica_groups=mesh['cx'=4,'cz'=4,'cb'=8,'win'=4] {'cz','cx'}, dimensions={0} | all-to-all | bytes 2359296 | tf_op jit(solution)/shard_map/all_to_all | solution.py:120
  116.6 0.9 copy.33
  117.6 1.7 %broadcast_in_dim_reshape.2 = bf16[1,2,48,6144]{3,2,1,0:T(8,128)(2,1)} reshape(bf16[2,48,4,4,384]{4,3,2,1,0:T(4,128)(2,1)S(1)} %bitcast.44) | data formatting | bytes 2359296 | tf_op jit(solution)/shard_map/broadcast_in_dim;reshape | solution.py:123
  (28 shorter events, 4.5 us)
Async XLA Ops:
  0.0 11.9 %copy-start = (f32[1024,256]{1,0:T(8,128)S(1)}, f32[1024,256]{1,0:T(8,128)}, u32[]{:S(2)}) copy-start(f32[1024,256]{1,0:T(8,128)} %constant.42.clone) | copy-start | bytes 3145732
  0.8 9.4 %collective-permute-start = (bf16[8,1,1024]{2,0,1:T(8,128)(2,1)S(1)}, bf16[8,1,1024]{2,0,1:T(8,128)(2,1)S(1)}, u32[]{:S(2)}, u32[]{:S(2)}) collective-permute-start(bf16[8,1,1024]{2,0,1:T(8,128)(2,1)S(1)} %get-tuple-element.9), channel_id=1, source_target_pairs={{0,4},{4,8},{8,12},{12,16},{16,20},{20,24},{24,28},{28,32},{32,36}... | collective-permute-start | bytes 49160 | tf_op jit(solution)/shard_map/ppermute | solution.py:27
  4.3 6.4 %collective-permute-start.1 = (bf16[8,1,1024]{2,0,1:T(8,128)(2,1)S(1)}, bf16[8,1,1024]{2,0,1:T(8,128)(2,1)S(1)}, u32[]{:S(2)}, u32[]{:S(2)}) collective-permute-start(bf16[8,1,1024]{2,0,1:T(8,128)(2,1)S(1)} %get-tuple-element.10), channel_id=1, source_target_pairs={{4,0},{8,4},{12,8},{16,12},{20,16},{24,20},{28,24},{32,28},{36,32}... | collective-permute-start | bytes 49160 | tf_op jit(solution)/shard_map/ppermute | solution.py:28
  13.9 11.6 %all-to-all-start = ((f32[16,1,3072]{2,1,0:T(1,128)}), f32[16,1,3072]{2,1,0:T(1,128)S(1)}, u32[]{:S(2)}, u32[]{:S(2)}) async-start(f32[16,1,3072]{2,1,0:T(1,128)} %reshape.87), calls=%async_computation | async-start | bytes 393216 | tf_op jit(solution)/shard_map/all_to_all | solution.py:42
  25.5 26.3 %all-to-all-start.2 = ((f32[32,1,3072]{2,1,0:T(1,128)}), f32[32,1,3072]{2,1,0:T(1,128)S(1)}, u32[]{:S(2)}, u32[]{:S(2)}) async-start(f32[32,1,3072]{2,1,0:T(1,128)} %reshape.89), calls=%async_computation.2 | async-start | bytes 786432 | tf_op jit(solution)/shard_map/all_to_all | solution.py:42
  52.8 27.9 %all-to-all-start.1 = ((f32[4,192,256]{2,1,0:T(8,128)}), f32[4,192,256]{2,1,0:T(8,128)S(1)}, u32[]{:S(2)}, u32[]{:S(2)}) async-start(f32[4,192,256]{2,1,0:T(8,128)} %broadcast_in_dim.29), calls=%async_computation.1 | async-start | bytes 1572864 | tf_op jit(solution)/shard_map/all_to_all | solution.py:35

commit v16 on v14

--- a/solution.py
+++ b/solution.py
@@ -11,11 +11,12 @@
 MOST_REACH = 8
 ROW_GROUP = 8
 Z_GROUP = 4
+Y_NEAR = 4
 
 
 FLOOR_POWER = 0.01
 
-CHAN = ("cx", "cz", "cb")
+CHAN = ("cx", "cz", "cyh", "cyl")
 
 
 def with_halo(x, width):
@@ -67,10 +68,9 @@
 
 def body(strain, seg_ids, dead, radius):
     local_rows = strain.shape[0]
-    group_b = lax.axis_size("cb")
     group_x = lax.axis_size("cx")
-    group_z = lax.axis_size("cz")
-    device = (lax.axis_index("cx") * group_z + lax.axis_index("cz")) * group_b + lax.axis_index("cb")
+    group_l = lax.axis_size("cyl")
+    device = lax.axis_index(CHAN)
     seg_padded = jnp.pad(seg_ids, (MOST_REACH, MOST_REACH), constant_values=-1)
     near_segs = lax.dynamic_slice_in_dim(
         seg_padded, device * local_rows, local_rows + 2 * MOST_REACH
@@ -111,23 +111,24 @@
     whitened = whitened.reshape(bands, local_rows, -1)
     windows = bands
     inverse_count = 1.0 / (windows * whitened.shape[2] // 2)
-    col_set = spread_band(whitened, ("cz", "cb"))
-    row_set = spread_band(whitened, ("cx",))
+    col_set = spread_band(whitened, ("cz", "cyh"))
+    row_set = gather_blocks(spread_band(whitened, ("cyl",)), "cx")
     operands = jnp.concatenate([col_set, swapped_parts(col_set, windows)], axis=0)
     product = jnp.einsum("ik,jk->ij", row_set, operands, precision=lax.Precision.HIGHEST)
     product = (product * inverse_count).astype(jnp.bfloat16)
-    product = product.reshape(group_x, local_rows, operands.shape[0])
-    mine = lax.all_to_all(product, "cx", split_axis=0, concat_axis=0, tiled=True)
-    mine = mine.reshape(group_x, local_rows, 2, col_set.shape[0])
-    cross_spectra = mine.transpose(2, 1, 0, 3).reshape(2, local_rows, -1)
+    product = product.reshape(group_x * group_l, local_rows, operands.shape[0])
+    mine = lax.all_to_all(product, ("cx", "cyl"), split_axis=0, concat_axis=0, tiled=True)
+    mine = mine.reshape(group_x, group_l, local_rows, 2, -1, local_rows)
+    mine = mine.transpose(3, 2, 0, 4, 1, 5)
+    cross_spectra = mine.reshape(2, local_rows, -1)
     return cross_spectra[None]
 
 
 def solution(mesh):
     chan_size = mesh.shape["chan"]
     outer = chan_size // ROW_GROUP
-    grid = mesh.devices.reshape(outer // Z_GROUP, Z_GROUP, ROW_GROUP, mesh.shape["win"])
-    sub_mesh = Mesh(grid, ("cx", "cz", "cb", "win"))
+    grid = mesh.devices.reshape(outer // Z_GROUP, Z_GROUP, ROW_GROUP // Y_NEAR, Y_NEAR, mesh.shape["win"])
+    sub_mesh = Mesh(grid, ("cx", "cz", "cyh", "cyl", "win"))
     return jax.shard_map(
         body,
         mesh=sub_mesh,

time: 141 us -> 137 us (0.972)
  blocking collectives: 17.4 us -> 34.9 us
  waiting for transfers between devices: 42.1 us -> 29.8 us
  other arithmetic: 11.2 us -> 5.44 us
  local copies, waits for them, and re-layouts: 30.3 us -> 26.4 us
  starting transfers between devices: 31.5 us -> 34.2 us
  matrix products: 7.17 us -> 5.32 us
    all_to_all x2, waiting for transfers between devices: 42.1 us -> 22.2 us  [spread_band(): lax.all_to_all(copies, axes + ('win',), split_axis=0, concat_axis=0, tile...]
    all_to_all x1, blocking collectives: 17.4 us -> 34.9 us  [body(): lax.all_to_all(product, ('cx', 'cyl'), split_axis=0, concat_axis=0, tiled...]
    reshape x2, local copies, waits for them, and re-layouts: 1.8 us -> 10.4 us  [body(): mine = mine.reshape(group_x, group_l, local_rows, 2, -1, local_rows)]
    all_to_all x0 -> x1, waiting for transfers between devices: none -> 7.59 us  [gather_blocks(): lax.all_to_all(copies, axis, split_axis=0, concat_axis=0, tiled=True)]
    transpose x3, local copies, waits for them, and re-layouts: 7.61 us -> 0.85 us  [spread_band(): every = every.reshape(size, bands, rows, width).transpose(0, 2, 1, 3)]
    another operation x1, local copies, waits for them, and re-layouts: 1.68 us -> 7.33 us  [body(): return cross_spectra[None]]
    all_to_all x2, other arithmetic: 7.1 us -> 2.76 us  [spread_band(): lax.all_to_all(copies, axes + ('win',), split_axis=0, concat_axis=0, tile...]
    another operation x1, local copies, waits for them, and re-layouts: 4.45 us -> 0.31 us  [swapped_parts(): parts = flat.reshape(flat.shape[:-1] + (windows, 2, -1))]
  transfers between devices with their start and end apart: 4 -> 5, of which waited for: 2 -> 3; matrix products, arithmetic and copies ran while one was open for 6% -> 8% of each run, Pallas kernels for 0% -> 0%
where the time goes in v16:
time: 137 us; the launch traced here: 136 us
  blocking collectives  34.9 us (25%)
  starting transfers between devices  34.2 us (25%)
  waiting for transfers between devices  29.8 us (22%)
  local copies, waits for them, and re-layouts  26.4 us (19%)
  other arithmetic  5.44 us (4%)
  matrix products  5.32 us (4%)
    all_to_all x1, blocking collectives, body(): lax.all_to_all(product, ('cx', 'cyl'), split_axis=0, concat_axis=0, tiled...  34.9 us
    all_to_all x2, starting transfers between devices, spread_band(): lax.all_to_all(copies, axes + ('win',), split_axis=0, concat_axis=0, tile...  24.9 us
    all_to_all x2, waiting for transfers between devices, spread_band(): lax.all_to_all(copies, axes + ('win',), split_axis=0, concat_axis=0, tile...  22.2 us
    reshape x2, local copies, waits for them, and re-layouts, body(): mine = mine.reshape(group_x, group_l, local_rows, 2, -1, local_rows)  10.4 us
    all_to_all x1, waiting for transfers between devices, gather_blocks(): lax.all_to_all(copies, axis, split_axis=0, concat_axis=0, tiled=True)  7.59 us
    another operation x1, local copies, waits for them, and re-layouts, body(): return cross_spectra[None]  7.33 us
    ppermute x1, starting transfers between devices, with_halo(): before = lax.ppermute(last, CHAN, up)  4.02 us
    all_to_all x1, starting transfers between devices, gather_blocks(): lax.all_to_all(copies, axis, split_axis=0, concat_axis=0, tiled=True)  4.01 us
  transfers between devices with their start and end apart: 5, of which 3 were waited for; matrix products, arithmetic and copies ran while one was open for 8% of the time, Pallas kernels for 0%

profile of v16, /device:TPU:1, one launch (start us, length us, event | category | flops | bytes accessed | tf_op | source)
XLA Modules:
  0.0 136.3 jit_solution(8413904330508428842)
XLA Ops:
  0.7 4.0 %collective-permute-start = (bf16[8,1,1024]{2,0,1:T(8,128)(2,1)S(1)}, bf16[8,1,1024]{2,0,1:T(8,128)(2,1)S(1)}, u32[]{:S(2)}, u32[]{:S(2)}) collective-permute-start(bf16[8,1,1024]{2,0,1:T(8,128)(2,1)S(1)} %get-tuple-element.9), channel_id=1, source_target_pairs={{0,4},{4,8},{8,12},{12,16},{16,20},{20,24},{24,28},{28,32},{32,36}... | collective-permute-start | bytes 49160 | tf_op jit(solution)/shard_map/ppermute | solution.py:28
  4.8 1.3 collective-permute-start.1
  6.9 0.9 select_reduce_fusion
  7.8 0.8 broadcast_compare_fusion
  8.7 0.8 convert_reduce_fusion.1
  9.6 1.2 fusion.3
  10.8 1.8 %fusion.24 = f32[48,256]{1,0:T(8,128)S(1)} fusion(f32[48,1024]{1,0:T(8,128)S(1)} %fusion.3, f32[1024,256]{1,0:T(8,128)} %constant.49.clone), kind=kOutput, calls=%fused_computation.45 | convolution fusion | flops 150994944 | bytes 1294336 | tf_op jit(solution)/shard_map/cwt,tk->cwk/dot_general | solution.py:102
  13.1 0.9 reshape.87
  14.0 10.9 %all-to-all-start = ((f32[16,1,3072]{2,1,0:T(1,128)}), f32[16,1,3072]{2,1,0:T(1,128)S(1)}, u32[]{:S(2)}, u32[]{:S(2)}) async-start(f32[16,1,3072]{2,1,0:T(1,128)} %reshape.87), calls=%async_computation | async-start | bytes 393216 | tf_op jit(solution)/shard_map/all_to_all | solution.py:43
  24.9 1.2 reshape.89
  26.2 7.0 %all-to-all-done = f32[16,1,3072]{2,1,0:T(1,128)S(1)} async-done(((f32[16,1,3072]{2,1,0:T(1,128)}), f32[16,1,3072]{2,1,0:T(1,128)S(1)}, u32[]{:S(2)}, u32[]{:S(2)}) %all-to-all-start) | async-done | bytes 196640 | tf_op jit(solution)/shard_map/all_to_all | solution.py:43
  33.2 14.0 %all-to-all-start.2 = ((f32[32,1,3072]{2,1,0:T(1,128)}), f32[32,1,3072]{2,1,0:T(1,128)S(1)}, u32[]{:S(2)}, u32[]{:S(2)}) async-start(f32[32,1,3072]{2,1,0:T(1,128)} %reshape.89), calls=%async_computation.2 | async-start | bytes 786432 | tf_op jit(solution)/shard_map/all_to_all | solution.py:43
  47.8 1.1 reduce
  49.5 15.2 %all-to-all-done.2 = f32[32,1,3072]{2,1,0:T(1,128)S(1)} async-done(((f32[32,1,3072]{2,1,0:T(1,128)}), f32[32,1,3072]{2,1,0:T(1,128)S(1)}, u32[]{:S(2)}, u32[]{:S(2)}) %all-to-all-start.2) | async-done | bytes 393248 | tf_op jit(solution)/shard_map/all_to_all | solution.py:43
  64.7 0.9 broadcast_in_dim.29
  65.6 4.0 %all-to-all-start.1 = ((f32[4,192,256]{2,1,0:T(8,128)}), f32[4,192,256]{2,1,0:T(8,128)S(1)}, u32[]{:S(2)}, u32[]{:S(2)}) async-start(f32[4,192,256]{2,1,0:T(8,128)} %broadcast_in_dim.29), calls=%async_computation.1 | async-start | bytes 1572864 | tf_op jit(solution)/shard_map/all_to_all | solution.py:36
  69.6 1.6 %reduce.1 = f32[32,3072]{1,0:T(8,128)S(1)} reduce(f32[32,1,3072]{2,1,0:T(1,128)S(1)} %all-to-all-done.2, f32[]{:T(128)} %broadcast.24), dimensions={1}, to_apply=%all_to_all.14.reduce_sub_computation | reduce | bytes 786436 | tf_op jit(solution)/shard_map/all_to_all | solution.py:43
  72.2 1.2 reshape.83
  74.0 7.6 %all-to-all-done.1 = f32[4,192,256]{2,1,0:T(8,128)S(1)} async-done(((f32[4,192,256]{2,1,0:T(8,128)}), f32[4,192,256]{2,1,0:T(8,128)S(1)}, u32[]{:S(2)}, u32[]{:S(2)}) %all-to-all-start.1) | async-done | bytes 786464 | tf_op jit(solution)/shard_map/all_to_all | solution.py:36
  81.5 2.1 %multiply_convert_fusion = bf16[768,768]{1,0:T(8,128)(2,1)S(1)} fusion(f32[768,256]{1,0:T(8,128)S(1)} %bitcast.47, f32[384,256]{1,0:T(8,128)S(1)} %copy.30, f32[384,256]{1,0:T(8,128)S(1)} %copy-done), kind=kOutput, calls=%fused_computation.1 | convolution fusion | flops 1813315584 | bytes 2752512 | tf_op jit(solution)/shard_map/ik,jk->ij/dot_general | solution.py:117
  83.6 34.9 %all_to_all.20 = bf16[16,48,768]{2,1,0:T(8,128)(2,1)} all-to-all(bf16[16,48,768]{2,1,0:T(8,128)(2,1)S(1)} %bitcast.45), channel_id=1, replica_groups=mesh['cx'=4,'cz'=4,'cyh'=2,'cyl'=4,'win'=4] {'cx','cyl'}, dimensions={0} | all-to-all | bytes 2359296 | tf_op jit(solution)/shard_map/all_to_all | solution.py:120
  118.6 4.7 %reshape.86 = bf16[4,4,48,2,8,48]{5,4,3,2,1,0:T(8,128)(2,1)S(1)} reshape(bf16[16,48,768]{2,1,0:T(8,128)(2,1)} %all_to_all.20) | data formatting | bytes 2359296 | tf_op jit(solution)/shard_map/reshape | solution.py:121
  123.2 5.7 %copy.33 = bf16[4,4,48,2,8,48]{5,1,4,0,2,3:T(4,128)(2,1)} copy(bf16[4,4,48,2,8,48]{5,4,3,2,1,0:T(8,128)(2,1)S(1)} %reshape.86) | data formatting | bytes 2359296 | tf_op jit(solution)/shard_map/reshape | solution.py:121
  128.9 7.3 %broadcast_in_dim_reshape.2 = bf16[1,2,48,6144]{3,2,1,0:T(8,128)(2,1)} reshape(bf16[2,48,4,8,4,48]{5,4,3,2,1,0:T(4,128)(2,1)} %bitcast.42) | data formatting | bytes 2359296 | tf_op jit(solution)/shard_map/broadcast_in_dim;reshape | solution.py:124
  (28 shorter events, 4.8 us)
Async XLA Ops:
  0.7 8.8 %collective-permute-start = (bf16[8,1,1024]{2,0,1:T(8,128)(2,1)S(1)}, bf16[8,1,1024]{2,0,1:T(8,128)(2,1)S(1)}, u32[]{:S(2)}, u32[]{:S(2)}) collective-permute-start(bf16[8,1,1024]{2,0,1:T(8,128)(2,1)S(1)} %get-tuple-element.9), channel_id=1, source_target_pairs={{0,4},{4,8},{8,12},{12,16},{16,20},{20,24},{24,28},{28,32},{32,36}... | collective-permute-start | bytes 49160 | tf_op jit(solution)/shard_map/ppermute | solution.py:28
  4.8 4.8 %collective-permute-start.1 = (bf16[8,1,1024]{2,0,1:T(8,128)(2,1)S(1)}, bf16[8,1,1024]{2,0,1:T(8,128)(2,1)S(1)}, u32[]{:S(2)}, u32[]{:S(2)}) collective-permute-start(bf16[8,1,1024]{2,0,1:T(8,128)(2,1)S(1)} %get-tuple-element.10), channel_id=1, source_target_pairs={{4,0},{8,4},{12,8},{16,12},{20,16},{24,20},{28,24},{32,28},{36,32}... | collective-permute-start | bytes 49160 | tf_op jit(solution)/shard_map/ppermute | solution.py:29
  14.0 19.2 %all-to-all-start = ((f32[16,1,3072]{2,1,0:T(1,128)}), f32[16,1,3072]{2,1,0:T(1,128)S(1)}, u32[]{:S(2)}, u32[]{:S(2)}) async-start(f32[16,1,3072]{2,1,0:T(1,128)} %reshape.87), calls=%async_computation | async-start | bytes 393216 | tf_op jit(solution)/shard_map/all_to_all | solution.py:43
  33.2 31.5 %all-to-all-start.2 = ((f32[32,1,3072]{2,1,0:T(1,128)}), f32[32,1,3072]{2,1,0:T(1,128)S(1)}, u32[]{:S(2)}, u32[]{:S(2)}) async-start(f32[32,1,3072]{2,1,0:T(1,128)} %reshape.89), calls=%async_computation.2 | async-start | bytes 786432 | tf_op jit(solution)/shard_map/all_to_all | solution.py:43
  65.6 15.9 %all-to-all-start.1 = ((f32[4,192,256]{2,1,0:T(8,128)}), f32[4,192,256]{2,1,0:T(8,128)S(1)}, u32[]{:S(2)}, u32[]{:S(2)}) async-start(f32[4,192,256]{2,1,0:T(8,128)} %broadcast_in_dim.29), calls=%async_computation.1 | async-start | bytes 1572864 | tf_op jit(solution)/shard_map/all_to_all | solution.py:36
  73.4 8.2 %copy-start = (f32[384,256]{1,0:T(8,128)S(1)}, f32[384,256]{1,0:T(8,128)}, u32[]{:S(2)}) copy-start(f32[384,256]{1,0:T(8,128)} %reshape.83) | copy-start | bytes 1179652

commit v17 on v11

--- a/solution.py
+++ b/solution.py
@@ -75,10 +75,7 @@
     near_segs = lax.dynamic_slice_in_dim(
         seg_padded, device * local_rows, local_rows + 2 * MOST_REACH
     )
-    segment_ids = jnp.arange(dead.shape[0], dtype=jnp.int32)
-    dead_near = jnp.sum(
-        jnp.where(near_segs[:, None] == segment_ids[None, :], dead[None, :], 0), axis=1
-    )
+    dead_near = jnp.where(near_segs >= 0, dead[jnp.clip(near_segs, 0, dead.shape[0] - 1)], 0)
     alive_near = jnp.where(near_segs >= 0, 1 - dead_near, 0)
     own_segs = near_segs[MOST_REACH : MOST_REACH + local_rows]
     alive_own = alive_near[MOST_REACH : MOST_REACH + local_rows].astype(jnp.float32)
@@ -99,7 +96,7 @@
     filtered = alive_own[:, None, None] * (
         strain.astype(jnp.float32) - neighbor_sums / counts[:, None, None]
     )
-    spectra = jnp.einsum("cwt,tk->cwk", filtered, fourier, precision=lax.Precision.HIGHEST)
+    spectra = jnp.einsum("cwt,tk->cwk", filtered, fourier, precision=lax.Precision.HIGH)
     power_bins = spectra[..., :FREQ_BINS] ** 2 + spectra[..., FREQ_BINS:] ** 2
     smoothed = jnp.einsum(
         "cwk,kj->cwj", power_bins, smoothing_table(), precision=lax.Precision.HIGHEST
@@ -114,7 +111,7 @@
     col_set = spread_band(whitened, "cb")
     row_set = gather_blocks(spread_band(whitened, "cz"), "cx")
     operands = jnp.concatenate([col_set, swapped_parts(col_set, windows)], axis=0)
-    product = jnp.einsum("ik,jk->ij", row_set, operands, precision=lax.Precision.HIGHEST)
+    product = jnp.einsum("ik,jk->ij", row_set, operands, precision=lax.Precision.HIGH)
     product = (product * inverse_count).astype(jnp.bfloat16)
     product = product.reshape(group_x * group_z, local_rows, operands.shape[0])
     mine = lax.all_to_all(product, ("cx", "cz"), split_axis=0, concat_axis=0, tiled=True)

time: 114 us -> 112 us (0.982)
    unnamed x6 -> x8, local copies, waits for them, and re-layouts: 2.46 us -> 2.47 us
  transfers between devices with their start and end apart: 5 -> 5, of which waited for: 3 -> 4; matrix products, arithmetic and copies ran while one was open for 9% -> 9% of each run, Pallas kernels for 0% -> 0%
where the time goes in v17:
time: 112 us
  blocking collectives  35.3 us (32%)
  starting transfers between devices  30.3 us (27%)
  waiting for transfers between devices  28.3 us (25%)
  local copies, waits for them, and re-layouts  10.1 us (9%)
  other arithmetic  4.47 us (4%)
  matrix products  2.98 us (3%)
    all_to_all x1, blocking collectives, body(): lax.all_to_all(product, ('cx', 'cz'), split_axis=0, concat_axis=0, tiled=...  35.3 us
    all_to_all x2, starting transfers between devices, spread_band(): lax.all_to_all(copies, (axis, 'win'), split_axis=0, concat_axis=0, tiled=...  20.2 us
    all_to_all x2, waiting for transfers between devices, spread_band(): lax.all_to_all(copies, (axis, 'win'), split_axis=0, concat_axis=0, tiled=...  19.1 us
    all_to_all x1, waiting for transfers between devices, gather_blocks(): lax.all_to_all(copies, axis, split_axis=0, concat_axis=0, tiled=True)  8.63 us
    all_to_all x1, starting transfers between devices, gather_blocks(): lax.all_to_all(copies, axis, split_axis=0, concat_axis=0, tiled=True)  4.29 us
    ppermute x1, starting transfers between devices, with_halo(): before = lax.ppermute(last, CHAN, up)  3.47 us
    all_to_all x2, other arithmetic, spread_band(): lax.all_to_all(copies, (axis, 'win'), split_axis=0, concat_axis=0, tiled=...  2.63 us
    unnamed x8, local copies, waits for them, and re-layouts  2.47 us
  transfers between devices with their start and end apart: 5, of which 4 were waited for; matrix products, arithmetic and copies ran while one was open for 9% of the time, Pallas kernels for 0%

profile of v17, /device:TPU:72, one launch (start us, length us, event | category | flops | bytes accessed | tf_op | source)
XLA Modules:
  0.0 111.7 jit_solution(11796219460178456369)
XLA Ops:
  0.0 0.8 fusion.24
  0.8 3.5 %collective-permute-start = (bf16[8,1,1024]{2,0,1:T(8,128)(2,1)S(1)}, bf16[8,1,1024]{2,0,1:T(8,128)(2,1)S(1)}, u32[]{:S(2)}, u32[]{:S(2)}) collective-permute-start(bf16[8,1,1024]{2,0,1:T(8,128)(2,1)S(1)} %get-tuple-element.11), channel_id=1, source_target_pairs={{0,4},{4,8},{8,12},{12,16},{16,20},{20,24},{24,28},{28,32},{32,36}... | collective-permute-start | bytes 49160 | tf_op jit(solution)/shard_map/ppermute | solution.py:27
  4.3 2.4 %collective-permute-start.1 = (bf16[8,1,1024]{2,0,1:T(8,128)(2,1)S(1)}, bf16[8,1,1024]{2,0,1:T(8,128)(2,1)S(1)}, u32[]{:S(2)}, u32[]{:S(2)}) collective-permute-start(bf16[8,1,1024]{2,0,1:T(8,128)(2,1)S(1)} %get-tuple-element.12), channel_id=1, source_target_pairs={{4,0},{8,4},{12,8},{16,12},{20,16},{24,20},{28,24},{32,28},{36,32}... | collective-permute-start | bytes 49160 | tf_op jit(solution)/shard_map/ppermute | solution.py:28
  6.7 0.8 compare_select_fusion
  7.6 0.8 gather_fusion
  8.4 0.8 convert_reduce_fusion.1
  9.3 0.6 collective-permute-done.1
  9.9 1.2 %fusion.3 = f32[48,1024]{1,0:T(8,128)S(1)} fusion(bf16[48,1,1024]{2,0,1:T(8,128)(2,1)} %param.5, bf16[8,1,1024]{2,0,1:T(8,128)(2,1)S(1)} %collective-permute-done.1, bf16[8,1,1024]{2,0,1:T(8,128)(2,1)S(1)} %collective-permute-done, f32[48]{0:T(128)S(1)} %broadcast_maximum_fusion, f32[48]{0:T(128)S(1)} %get-tuple-element.14, s32[64]{0:T(128)S(1)} %get-tuple-element.8, ...), kind=kOutput, calls=%fused_computation.7 | convolution fusion | flops 6899712 | bytes 328960 | tf_op jit(solution)/shard_map/cr,rwt->cwt/dot_general | solution.py:93
  12.1 0.9 reshape.94
  13.0 10.0 %all-to-all-start = ((f32[16,1,3072]{2,1,0:T(1,128)}), f32[16,1,3072]{2,1,0:T(1,128)S(1)}, u32[]{:S(2)}, u32[]{:S(2)}) async-start(f32[16,1,3072]{2,1,0:T(1,128)} %reshape.94), calls=%async_computation | async-start | bytes 393216 | tf_op jit(solution)/shard_map/all_to_all | solution.py:42
  23.0 1.2 %reshape.96 = f32[32,1,3072]{2,1,0:T(1,128)} reshape(f32[32,48,64]{2,1,0:T(8,128)S(1)} %bitcast.48) | data formatting | bytes 786432
  24.2 7.2 %all-to-all-done = f32[16,1,3072]{2,1,0:T(1,128)S(1)} async-done(((f32[16,1,3072]{2,1,0:T(1,128)}), f32[16,1,3072]{2,1,0:T(1,128)S(1)}, u32[]{:S(2)}, u32[]{:S(2)}) %all-to-all-start) | async-done | bytes 196640 | tf_op jit(solution)/shard_map/all_to_all | solution.py:42
  31.5 10.2 %all-to-all-start.2 = ((f32[32,1,3072]{2,1,0:T(1,128)}), f32[32,1,3072]{2,1,0:T(1,128)S(1)}, u32[]{:S(2)}, u32[]{:S(2)}) async-start(f32[32,1,3072]{2,1,0:T(1,128)} %reshape.96), calls=%async_computation.2 | async-start | bytes 786432 | tf_op jit(solution)/shard_map/all_to_all | solution.py:42
  41.7 0.5 broadcast.34
  42.3 1.1 reduce
  43.9 11.8 %all-to-all-done.2 = f32[32,1,3072]{2,1,0:T(1,128)S(1)} async-done(((f32[32,1,3072]{2,1,0:T(1,128)}), f32[32,1,3072]{2,1,0:T(1,128)S(1)}, u32[]{:S(2)}, u32[]{:S(2)}) %all-to-all-start.2) | async-done | bytes 393248 | tf_op jit(solution)/shard_map/all_to_all | solution.py:42
  55.7 0.9 broadcast_in_dim.19
  56.7 4.3 %all-to-all-start.1 = ((f32[4,192,256]{2,1,0:T(8,128)}), f32[4,192,256]{2,1,0:T(8,128)S(1)}, u32[]{:S(2)}, u32[]{:S(2)}) async-start(f32[4,192,256]{2,1,0:T(8,128)} %broadcast_in_dim.19), calls=%async_computation.1 | async-start | bytes 1572864 | tf_op jit(solution)/shard_map/all_to_all | solution.py:35
  61.0 1.6 %reduce.1 = f32[32,3072]{1,0:T(8,128)S(1)} reduce(f32[32,1,3072]{2,1,0:T(1,128)S(1)} %all-to-all-done.2, f32[]{:T(128)} %broadcast.34), dimensions={1}, to_apply=%all_to_all.14.reduce_sub_computation | reduce | bytes 786436 | tf_op jit(solution)/shard_map/all_to_all | solution.py:42
  64.0 0.5 reshape.81
  64.5 8.6 %all-to-all-done.1 = f32[4,192,256]{2,1,0:T(8,128)S(1)} async-done(((f32[4,192,256]{2,1,0:T(8,128)}), f32[4,192,256]{2,1,0:T(8,128)S(1)}, u32[]{:S(2)}, u32[]{:S(2)}) %all-to-all-start.1) | async-done | bytes 786464 | tf_op jit(solution)/shard_map/all_to_all | solution.py:35
  73.1 1.2 %multiply_convert_fusion = bf16[768,768]{1,0:T(8,128)(2,1)S(1)} fusion(f32[768,256]{1,0:T(8,128)S(1)} %bitcast.49, f32[384,256]{1,0:T(8,128)S(1)} %copy.30, f32[384,256]{1,0:T(8,128)S(1)} %reshape.81), kind=kOutput, calls=%fused_computation.1 | convolution fusion | flops 907345920 | bytes 2752512 | tf_op jit(solution)/shard_map/ik,jk->ij/dot_general | solution.py:114
  74.3 35.3 %all_to_all.20 = bf16[16,48,768]{2,1,0:T(8,128)(2,1)S(1)} all-to-all(bf16[16,48,768]{2,1,0:T(8,128)(2,1)S(1)} %bitcast.47), channel_id=1, replica_groups=mesh['cx'=4,'cz'=4,'cb'=8,'win'=4] {'cx','cz'}, dimensions={0} | all-to-all | bytes 2359296 | tf_op jit(solution)/shard_map/all_to_all | solution.py:117
  110.3 1.4 %broadcast_in_dim_reshape.2 = bf16[1,2,48,6144]{3,2,1,0:T(8,128)(2,1)} reshape(bf16[2,48,16,384]{3,2,1,0:T(8,128)(2,1)S(1)} %bitcast.46) | data formatting | bytes 2359296 | tf_op jit(solution)/shard_map/broadcast_in_dim;reshape | solution.py:120
  (31 shorter events, 3.8 us)
Async XLA Ops:
  0.0 7.6 %copy-start = (s32[512]{0:T(512)S(1)}, s32[512]{0:T(512)}, u32[]{:S(2)}) copy-start(s32[512]{0:T(512)} %param.7) | copy-start | bytes 6148
  0.0 11.1 %copy-start.1 = (f32[1024,256]{1,0:T(8,128)S(1)}, f32[1024,256]{1,0:T(8,128)}, u32[]{:S(2)}) copy-start(f32[1024,256]{1,0:T(8,128)} %constant.46.clone) | copy-start | bytes 3145732
  0.8 8.5 %collective-permute-start = (bf16[8,1,1024]{2,0,1:T(8,128)(2,1)S(1)}, bf16[8,1,1024]{2,0,1:T(8,128)(2,1)S(1)}, u32[]{:S(2)}, u32[]{:S(2)}) collective-permute-start(bf16[8,1,1024]{2,0,1:T(8,128)(2,1)S(1)} %get-tuple-element.11), channel_id=1, source_target_pairs={{0,4},{4,8},{8,12},{12,16},{16,20},{20,24},{24,28},{28,32},{32,36}... | collective-permute-start | bytes 49160 | tf_op jit(solution)/shard_map/ppermute | solution.py:27
  4.3 5.6 %collective-permute-start.1 = (bf16[8,1,1024]{2,0,1:T(8,128)(2,1)S(1)}, bf16[8,1,1024]{2,0,1:T(8,128)(2,1)S(1)}, u32[]{:S(2)}, u32[]{:S(2)}) collective-permute-start(bf16[8,1,1024]{2,0,1:T(8,128)(2,1)S(1)} %get-tuple-element.12), channel_id=1, source_target_pairs={{4,0},{8,4},{12,8},{16,12},{20,16},{24,20},{28,24},{32,28},{36,32}... | collective-permute-start | bytes 49160 | tf_op jit(solution)/shard_map/ppermute | solution.py:28
  13.0 18.5 %all-to-all-start = ((f32[16,1,3072]{2,1,0:T(1,128)}), f32[16,1,3072]{2,1,0:T(1,128)S(1)}, u32[]{:S(2)}, u32[]{:S(2)}) async-start(f32[16,1,3072]{2,1,0:T(1,128)} %reshape.94), calls=%async_computation | async-start | bytes 393216 | tf_op jit(solution)/shard_map/all_to_all | solution.py:42
  31.5 24.3 %all-to-all-start.2 = ((f32[32,1,3072]{2,1,0:T(1,128)}), f32[32,1,3072]{2,1,0:T(1,128)S(1)}, u32[]{:S(2)}, u32[]{:S(2)}) async-start(f32[32,1,3072]{2,1,0:T(1,128)} %reshape.96), calls=%async_computation.2 | async-start | bytes 786432 | tf_op jit(solution)/shard_map/all_to_all | solution.py:42
  56.7 16.4 %all-to-all-start.1 = ((f32[4,192,256]{2,1,0:T(8,128)}), f32[4,192,256]{2,1,0:T(8,128)S(1)}, u32[]{:S(2)}, u32[]{:S(2)}) async-start(f32[4,192,256]{2,1,0:T(8,128)} %broadcast_in_dim.19), calls=%async_computation.1 | async-start | bytes 1572864 | tf_op jit(solution)/shard_map/all_to_all | solution.py:35

commit v18 on v17

--- a/solution.py
+++ b/solution.py
@@ -89,9 +89,18 @@
     linked_f = linked.astype(jnp.float32)
     counts = jnp.maximum(jnp.sum(linked_f, axis=1), 1.0)
     fourier = fourier_table()
-    extended = with_halo(strain, MOST_REACH)
-    neighbor_sums = jnp.einsum(
-        "cr,rwt->cwt", linked.astype(jnp.bfloat16), extended, preferred_element_type=jnp.float32
+    link_weights = linked.astype(jnp.bfloat16)
+    own_sums = jnp.einsum(
+        "cr,rwt->cwt", link_weights[:, MOST_REACH:MOST_REACH + local_rows], strain,
+        preferred_element_type=jnp.float32,
+    )
+    halo = with_halo(strain, MOST_REACH)
+    ends = jnp.concatenate([halo[:MOST_REACH], halo[MOST_REACH + local_rows:]], axis=0)
+    end_weights = jnp.concatenate(
+        [link_weights[:, :MOST_REACH], link_weights[:, MOST_REACH + local_rows:]], axis=1
+    )
+    neighbor_sums = own_sums + jnp.einsum(
+        "cr,rwt->cwt", end_weights, ends, preferred_element_type=jnp.float32
     )
     filtered = alive_own[:, None, None] * (
         strain.astype(jnp.float32) - neighbor_sums / counts[:, None, None]

time: 112 us -> 113 us (level)
  transfers between devices with their start and end apart: 5 -> 5, of which waited for: 4 -> 3; matrix products, arithmetic and copies ran while one was open for 9% -> 9% of each run, Pallas kernels for 0% -> 0%
where the time goes in v18:
time: 113 us; the launch traced here: 112 us
  blocking collectives  35.3 us (31%)
  starting transfers between devices  30.4 us (27%)
  waiting for transfers between devices  27.7 us (25%)
  local copies, waits for them, and re-layouts  10.1 us (9%)
  other arithmetic  4.41 us (4%)
  matrix products  4 us (4%)
    all_to_all x1, blocking collectives, body(): lax.all_to_all(product, ('cx', 'cz'), split_axis=0, concat_axis=0, tiled=...  35.3 us
    all_to_all x2, starting transfers between devices, spread_band(): lax.all_to_all(copies, (axis, 'win'), split_axis=0, concat_axis=0, tiled=...  20.2 us
    all_to_all x2, waiting for transfers between devices, spread_band(): lax.all_to_all(copies, (axis, 'win'), split_axis=0, concat_axis=0, tiled=...  19.1 us
    all_to_all x1, waiting for transfers between devices, gather_blocks(): lax.all_to_all(copies, axis, split_axis=0, concat_axis=0, tiled=True)  8.62 us
    all_to_all x1, starting transfers between devices, gather_blocks(): lax.all_to_all(copies, axis, split_axis=0, concat_axis=0, tiled=True)  4.28 us
    ppermute x1, starting transfers between devices, with_halo(): before = lax.ppermute(last, CHAN, up)  3.47 us
    all_to_all x2, other arithmetic, spread_band(): lax.all_to_all(copies, (axis, 'win'), split_axis=0, concat_axis=0, tiled=...  2.65 us
    unnamed x8, local copies, waits for them, and re-layouts  2.47 us
  transfers between devices with their start and end apart: 5, of which 3 were waited for; matrix products, arithmetic and copies ran while one was open for 9% of the time, Pallas kernels for 0%

profile of v18, /device:TPU:72, one launch (start us, length us, event | category | flops | bytes accessed | tf_op | source)
XLA Modules:
  0.0 112.1 jit_solution(6740843589853577770)
XLA Ops:
  0.0 0.8 fusion.30
  0.8 3.5 %collective-permute-start = (bf16[8,1,1024]{2,0,1:T(8,128)(2,1)S(1)}, bf16[8,1,1024]{2,0,1:T(8,128)(2,1)S(1)}, u32[]{:S(2)}, u32[]{:S(2)}) collective-permute-start(bf16[8,1,1024]{2,0,1:T(8,128)(2,1)S(1)} %get-tuple-element.13), channel_id=1, source_target_pairs={{0,4},{4,8},{8,12},{12,16},{16,20},{20,24},{24,28},{28,32},{32,36}... | collective-permute-start | bytes 49160 | tf_op jit(solution)/shard_map/ppermute | solution.py:27
  4.3 2.4 %collective-permute-start.1 = (bf16[8,1,1024]{2,0,1:T(8,128)(2,1)S(1)}, bf16[8,1,1024]{2,0,1:T(8,128)(2,1)S(1)}, u32[]{:S(2)}, u32[]{:S(2)}) collective-permute-start(bf16[8,1,1024]{2,0,1:T(8,128)(2,1)S(1)} %get-tuple-element.14), channel_id=1, source_target_pairs={{4,0},{8,4},{12,8},{16,12},{20,16},{24,20},{28,24},{32,28},{36,32}... | collective-permute-start | bytes 49160 | tf_op jit(solution)/shard_map/ppermute | solution.py:28
  6.7 0.8 compare_select_fusion
  7.6 0.8 gather_fusion
  8.4 0.7 fusion.28
  9.1 1.1 fusion.9
  10.4 1.1 fusion.4
  12.4 0.9 reshape.100
  13.3 10.0 %all-to-all-start = ((f32[16,1,3072]{2,1,0:T(1,128)}), f32[16,1,3072]{2,1,0:T(1,128)S(1)}, u32[]{:S(2)}, u32[]{:S(2)}) async-start(f32[16,1,3072]{2,1,0:T(1,128)} %reshape.100), calls=%async_computation | async-start | bytes 393216 | tf_op jit(solution)/shard_map/all_to_all | solution.py:42
  23.4 1.2 %reshape.102 = f32[32,1,3072]{2,1,0:T(1,128)} reshape(f32[32,48,64]{2,1,0:T(8,128)S(1)} %bitcast.51) | data formatting | bytes 786432
  24.6 7.2 %all-to-all-done = f32[16,1,3072]{2,1,0:T(1,128)S(1)} async-done(((f32[16,1,3072]{2,1,0:T(1,128)}), f32[16,1,3072]{2,1,0:T(1,128)S(1)}, u32[]{:S(2)}, u32[]{:S(2)}) %all-to-all-start) | async-done | bytes 196640 | tf_op jit(solution)/shard_map/all_to_all | solution.py:42
  31.9 10.3 %all-to-all-start.2 = ((f32[32,1,3072]{2,1,0:T(1,128)}), f32[32,1,3072]{2,1,0:T(1,128)S(1)}, u32[]{:S(2)}, u32[]{:S(2)}) async-start(f32[32,1,3072]{2,1,0:T(1,128)} %reshape.102), calls=%async_computation.2 | async-start | bytes 786432 | tf_op jit(solution)/shard_map/all_to_all | solution.py:42
  42.1 0.5 broadcast.34
  42.6 1.1 reduce
  44.3 11.9 %all-to-all-done.2 = f32[32,1,3072]{2,1,0:T(1,128)S(1)} async-done(((f32[32,1,3072]{2,1,0:T(1,128)}), f32[32,1,3072]{2,1,0:T(1,128)S(1)}, u32[]{:S(2)}, u32[]{:S(2)}) %all-to-all-start.2) | async-done | bytes 393248 | tf_op jit(solution)/shard_map/all_to_all | solution.py:42
  56.1 0.9 broadcast_in_dim.19
  57.1 4.3 %all-to-all-start.1 = ((f32[4,192,256]{2,1,0:T(8,128)}), f32[4,192,256]{2,1,0:T(8,128)S(1)}, u32[]{:S(2)}, u32[]{:S(2)}) async-start(f32[4,192,256]{2,1,0:T(8,128)} %broadcast_in_dim.19), calls=%async_computation.1 | async-start | bytes 1572864 | tf_op jit(solution)/shard_map/all_to_all | solution.py:35
  61.4 1.6 %reduce.1 = f32[32,3072]{1,0:T(8,128)S(1)} reduce(f32[32,1,3072]{2,1,0:T(1,128)S(1)} %all-to-all-done.2, f32[]{:T(128)} %broadcast.34), dimensions={1}, to_apply=%all_to_all.14.reduce_sub_computation | reduce | bytes 786436 | tf_op jit(solution)/shard_map/all_to_all | solution.py:42
  64.4 0.5 reshape.87
  64.9 8.6 %all-to-all-done.1 = f32[4,192,256]{2,1,0:T(8,128)S(1)} async-done(((f32[4,192,256]{2,1,0:T(8,128)}), f32[4,192,256]{2,1,0:T(8,128)S(1)}, u32[]{:S(2)}, u32[]{:S(2)}) %all-to-all-start.1) | async-done | bytes 786464 | tf_op jit(solution)/shard_map/all_to_all | solution.py:35
  73.5 1.2 %multiply_convert_fusion = bf16[768,768]{1,0:T(8,128)(2,1)S(1)} fusion(f32[768,256]{1,0:T(8,128)S(1)} %bitcast.52, f32[384,256]{1,0:T(8,128)S(1)} %copy.39, f32[384,256]{1,0:T(8,128)S(1)} %reshape.87), kind=kOutput, calls=%fused_computation.1 | convolution fusion | flops 907345920 | bytes 2752512 | tf_op jit(solution)/shard_map/ik,jk->ij/dot_general | solution.py:123
  74.7 35.3 %all_to_all.20 = bf16[16,48,768]{2,1,0:T(8,128)(2,1)S(1)} all-to-all(bf16[16,48,768]{2,1,0:T(8,128)(2,1)S(1)} %bitcast.50), channel_id=1, replica_groups=mesh['cx'=4,'cz'=4,'cb'=8,'win'=4] {'cx','cz'}, dimensions={0} | all-to-all | bytes 2359296 | tf_op jit(solution)/shard_map/all_to_all | solution.py:126
  110.7 1.4 %broadcast_in_dim_reshape.2 = bf16[1,2,48,6144]{3,2,1,0:T(8,128)(2,1)} reshape(bf16[2,48,16,384]{3,2,1,0:T(8,128)(2,1)S(1)} %bitcast.49) | data formatting | bytes 2359296 | tf_op jit(solution)/shard_map/broadcast_in_dim;reshape | solution.py:129
  (35 shorter events, 3.8 us)
Async XLA Ops:
  0.0 7.6 %copy-start = (s32[512]{0:T(512)S(1)}, s32[512]{0:T(512)}, u32[]{:S(2)}) copy-start(s32[512]{0:T(512)} %param.7) | copy-start | bytes 6148
  0.0 11.5 %copy-start.1 = (f32[1024,256]{1,0:T(8,128)S(1)}, f32[1024,256]{1,0:T(8,128)}, u32[]{:S(2)}) copy-start(f32[1024,256]{1,0:T(8,128)} %constant.46.clone) | copy-start | bytes 3145732
  0.8 9.6 %collective-permute-start = (bf16[8,1,1024]{2,0,1:T(8,128)(2,1)S(1)}, bf16[8,1,1024]{2,0,1:T(8,128)(2,1)S(1)}, u32[]{:S(2)}, u32[]{:S(2)}) collective-permute-start(bf16[8,1,1024]{2,0,1:T(8,128)(2,1)S(1)} %get-tuple-element.13), channel_id=1, source_target_pairs={{0,4},{4,8},{8,12},{12,16},{16,20},{20,24},{24,28},{28,32},{32,36}... | collective-permute-start | bytes 49160 | tf_op jit(solution)/shard_map/ppermute | solution.py:27
  4.3 6.1 %collective-permute-start.1 = (bf16[8,1,1024]{2,0,1:T(8,128)(2,1)S(1)}, bf16[8,1,1024]{2,0,1:T(8,128)(2,1)S(1)}, u32[]{:S(2)}, u32[]{:S(2)}) collective-permute-start(bf16[8,1,1024]{2,0,1:T(8,128)(2,1)S(1)} %get-tuple-element.14), channel_id=1, source_target_pairs={{4,0},{8,4},{12,8},{16,12},{20,16},{24,20},{28,24},{32,28},{36,32}... | collective-permute-start | bytes 49160 | tf_op jit(solution)/shard_map/ppermute | solution.py:28
  13.3 18.5 %all-to-all-start = ((f32[16,1,3072]{2,1,0:T(1,128)}), f32[16,1,3072]{2,1,0:T(1,128)S(1)}, u32[]{:S(2)}, u32[]{:S(2)}) async-start(f32[16,1,3072]{2,1,0:T(1,128)} %reshape.100), calls=%async_computation | async-start | bytes 393216 | tf_op jit(solution)/shard_map/all_to_all | solution.py:42
  31.9 24.3 %all-to-all-start.2 = ((f32[32,1,3072]{2,1,0:T(1,128)}), f32[32,1,3072]{2,1,0:T(1,128)S(1)}, u32[]{:S(2)}, u32[]{:S(2)}) async-start(f32[32,1,3072]{2,1,0:T(1,128)} %reshape.102), calls=%async_computation.2 | async-start | bytes 786432 | tf_op jit(solution)/shard_map/all_to_all | solution.py:42
  57.1 16.4 %all-to-all-start.1 = ((f32[4,192,256]{2,1,0:T(8,128)}), f32[4,192,256]{2,1,0:T(8,128)S(1)}, u32[]{:S(2)}, u32[]{:S(2)}) async-start(f32[4,192,256]{2,1,0:T(8,128)} %broadcast_in_dim.19), calls=%async_computation.1 | async-start | bytes 1572864 | tf_op jit(solution)/shard_map/all_to_all | solution.py:35

commit v19 on v17

--- a/solution.py
+++ b/solution.py
@@ -113,10 +113,9 @@
     operands = jnp.concatenate([col_set, swapped_parts(col_set, windows)], axis=0)
     product = jnp.einsum("ik,jk->ij", row_set, operands, precision=lax.Precision.HIGH)
     product = (product * inverse_count).astype(jnp.bfloat16)
-    product = product.reshape(group_x * group_z, local_rows, operands.shape[0])
+    product = product.reshape(group_x * group_z, local_rows, 2, col_set.shape[0]).transpose(0, 2, 1, 3)
     mine = lax.all_to_all(product, ("cx", "cz"), split_axis=0, concat_axis=0, tiled=True)
-    mine = mine.reshape(group_x * group_z, local_rows, 2, col_set.shape[0])
-    cross_spectra = mine.transpose(2, 1, 0, 3).reshape(2, local_rows, -1)
+    cross_spectra = mine.transpose(1, 2, 0, 3).reshape(2, local_rows, -1)
     return cross_spectra[None]
 
 

time: 112 us -> 112 us (level)
  no operation moved by 1% of the time
where the time goes in v19:
time: 112 us
  blocking collectives  35.3 us (32%)
  starting transfers between devices  30.3 us (27%)
  waiting for transfers between devices  28.3 us (25%)
  local copies, waits for them, and re-layouts  10.1 us (9%)
  other arithmetic  4.47 us (4%)
  matrix products  2.98 us (3%)
    all_to_all x1, blocking collectives, body(): lax.all_to_all(product, ('cx', 'cz'), split_axis=0, concat_axis=0, tiled=...  35.3 us
    all_to_all x2, starting transfers between devices, spread_band(): lax.all_to_all(copies, (axis, 'win'), split_axis=0, concat_axis=0, tiled=...  20.2 us
    all_to_all x2, waiting for transfers between devices, spread_band(): lax.all_to_all(copies, (axis, 'win'), split_axis=0, concat_axis=0, tiled=...  19.1 us
    all_to_all x1, waiting for transfers between devices, gather_blocks(): lax.all_to_all(copies, axis, split_axis=0, concat_axis=0, tiled=True)  8.63 us
    all_to_all x1, starting transfers between devices, gather_blocks(): lax.all_to_all(copies, axis, split_axis=0, concat_axis=0, tiled=True)  4.29 us
    ppermute x1, starting transfers between devices, with_halo(): before = lax.ppermute(last, CHAN, up)  3.47 us
    all_to_all x2, other arithmetic, spread_band(): lax.all_to_all(copies, (axis, 'win'), split_axis=0, concat_axis=0, tiled=...  2.63 us
    unnamed x8, local copies, waits for them, and re-layouts  2.47 us
  transfers between devices with their start and end apart: 5, of which 4 were waited for; matrix products, arithmetic and copies ran while one was open for 9% of the time, Pallas kernels for 0%

profile of v19, /device:TPU:72, one launch (start us, length us, event | category | flops | bytes accessed | tf_op | source)
XLA Modules:
  0.0 111.7 jit_solution(15179460196007191341)
XLA Ops:
  0.0 0.8 fusion.24
  0.8 3.5 %collective-permute-start = (bf16[8,1,1024]{2,0,1:T(8,128)(2,1)S(1)}, bf16[8,1,1024]{2,0,1:T(8,128)(2,1)S(1)}, u32[]{:S(2)}, u32[]{:S(2)}) collective-permute-start(bf16[8,1,1024]{2,0,1:T(8,128)(2,1)S(1)} %get-tuple-element.11), channel_id=1, source_target_pairs={{0,4},{4,8},{8,12},{12,16},{16,20},{20,24},{24,28},{28,32},{32,36}... | collective-permute-start | bytes 49160 | tf_op jit(solution)/shard_map/ppermute | solution.py:27
  4.3 2.4 %collective-permute-start.1 = (bf16[8,1,1024]{2,0,1:T(8,128)(2,1)S(1)}, bf16[8,1,1024]{2,0,1:T(8,128)(2,1)S(1)}, u32[]{:S(2)}, u32[]{:S(2)}) collective-permute-start(bf16[8,1,1024]{2,0,1:T(8,128)(2,1)S(1)} %get-tuple-element.12), channel_id=1, source_target_pairs={{4,0},{8,4},{12,8},{16,12},{20,16},{24,20},{28,24},{32,28},{36,32}... | collective-permute-start | bytes 49160 | tf_op jit(solution)/shard_map/ppermute | solution.py:28
  6.7 0.8 compare_select_fusion
  7.6 0.8 gather_fusion
  8.4 0.8 convert_reduce_fusion.1
  9.3 0.6 collective-permute-done.1
  9.9 1.2 %fusion.3 = f32[48,1024]{1,0:T(8,128)S(1)} fusion(bf16[48,1,1024]{2,0,1:T(8,128)(2,1)} %param.5, bf16[8,1,1024]{2,0,1:T(8,128)(2,1)S(1)} %collective-permute-done.1, bf16[8,1,1024]{2,0,1:T(8,128)(2,1)S(1)} %collective-permute-done, f32[48]{0:T(128)S(1)} %broadcast_maximum_fusion, f32[48]{0:T(128)S(1)} %get-tuple-element.14, s32[64]{0:T(128)S(1)} %get-tuple-element.8, ...), kind=kOutput, calls=%fused_computation.6 | convolution fusion | flops 6899712 | bytes 328960 | tf_op jit(solution)/shard_map/cr,rwt->cwt/dot_general | solution.py:93
  12.1 0.9 reshape.90
  13.0 10.0 %all-to-all-start = ((f32[16,1,3072]{2,1,0:T(1,128)}), f32[16,1,3072]{2,1,0:T(1,128)S(1)}, u32[]{:S(2)}, u32[]{:S(2)}) async-start(f32[16,1,3072]{2,1,0:T(1,128)} %reshape.90), calls=%async_computation | async-start | bytes 393216 | tf_op jit(solution)/shard_map/all_to_all | solution.py:42
  23.0 1.2 %reshape.92 = f32[32,1,3072]{2,1,0:T(1,128)} reshape(f32[32,48,64]{2,1,0:T(8,128)S(1)} %bitcast.46) | data formatting | bytes 786432
  24.2 7.2 %all-to-all-done = f32[16,1,3072]{2,1,0:T(1,128)S(1)} async-done(((f32[16,1,3072]{2,1,0:T(1,128)}), f32[16,1,3072]{2,1,0:T(1,128)S(1)}, u32[]{:S(2)}, u32[]{:S(2)}) %all-to-all-start) | async-done | bytes 196640 | tf_op jit(solution)/shard_map/all_to_all | solution.py:42
  31.5 10.2 %all-to-all-start.2 = ((f32[32,1,3072]{2,1,0:T(1,128)}), f32[32,1,3072]{2,1,0:T(1,128)S(1)}, u32[]{:S(2)}, u32[]{:S(2)}) async-start(f32[32,1,3072]{2,1,0:T(1,128)} %reshape.92), calls=%async_computation.2 | async-start | bytes 786432 | tf_op jit(solution)/shard_map/all_to_all | solution.py:42
  41.7 0.5 broadcast.34
  42.3 1.1 reduce
  43.9 11.8 %all-to-all-done.2 = f32[32,1,3072]{2,1,0:T(1,128)S(1)} async-done(((f32[32,1,3072]{2,1,0:T(1,128)}), f32[32,1,3072]{2,1,0:T(1,128)S(1)}, u32[]{:S(2)}, u32[]{:S(2)}) %all-to-all-start.2) | async-done | bytes 393248 | tf_op jit(solution)/shard_map/all_to_all | solution.py:42
  55.7 0.9 broadcast_in_dim.19
  56.7 4.3 %all-to-all-start.1 = ((f32[4,192,256]{2,1,0:T(8,128)}), f32[4,192,256]{2,1,0:T(8,128)S(1)}, u32[]{:S(2)}, u32[]{:S(2)}) async-start(f32[4,192,256]{2,1,0:T(8,128)} %broadcast_in_dim.19), calls=%async_computation.1 | async-start | bytes 1572864 | tf_op jit(solution)/shard_map/all_to_all | solution.py:35
  61.0 1.6 %reduce.1 = f32[32,3072]{1,0:T(8,128)S(1)} reduce(f32[32,1,3072]{2,1,0:T(1,128)S(1)} %all-to-all-done.2, f32[]{:T(128)} %broadcast.34), dimensions={1}, to_apply=%all_to_all.14.reduce_sub_computation | reduce | bytes 786436 | tf_op jit(solution)/shard_map/all_to_all | solution.py:42
  64.0 0.5 reshape.78
  64.5 8.6 %all-to-all-done.1 = f32[4,192,256]{2,1,0:T(8,128)S(1)} async-done(((f32[4,192,256]{2,1,0:T(8,128)}), f32[4,192,256]{2,1,0:T(8,128)S(1)}, u32[]{:S(2)}, u32[]{:S(2)}) %all-to-all-start.1) | async-done | bytes 786464 | tf_op jit(solution)/shard_map/all_to_all | solution.py:35
  73.1 1.2 %multiply_convert_fusion = bf16[768,768]{1,0:T(8,128)(2,1)S(1)} fusion(f32[768,256]{1,0:T(8,128)S(1)} %bitcast.47, f32[384,256]{1,0:T(8,128)S(1)} %copy.30, f32[384,256]{1,0:T(8,128)S(1)} %reshape.78), kind=kOutput, calls=%fused_computation.1 | convolution fusion | flops 907345920 | bytes 2752512 | tf_op jit(solution)/shard_map/ik,jk->ij/dot_general | solution.py:114
  74.6 35.3 %all_to_all.20 = bf16[16,2,48,384]{3,1,2,0:T(2,128)(2,1)S(1)} all-to-all(bf16[16,2,48,384]{3,1,2,0:T(2,128)(2,1)S(1)} %bitcast.44), channel_id=1, replica_groups=mesh['cx'=4,'cz'=4,'cb'=8,'win'=4] {'cx','cz'}, dimensions={0} | all-to-all | bytes 2359296 | tf_op jit(solution)/shard_map/all_to_all | solution.py:117
  110.3 1.4 %broadcast_in_dim_reshape.2 = bf16[1,2,48,6144]{3,2,1,0:T(8,128)(2,1)} reshape(bf16[2,48,16,384]{3,2,1,0:T(8,128)(2,1)S(1)} %copy.31) | data formatting | bytes 2359296 | tf_op jit(solution)/shard_map/broadcast_in_dim;reshape | solution.py:119
  (31 shorter events, 3.8 us)
Async XLA Ops:
  0.0 7.6 %copy-start = (s32[512]{0:T(512)S(1)}, s32[512]{0:T(512)}, u32[]{:S(2)}) copy-start(s32[512]{0:T(512)} %param.7) | copy-start | bytes 6148
  0.0 11.1 %copy-start.1 = (f32[1024,256]{1,0:T(8,128)S(1)}, f32[1024,256]{1,0:T(8,128)}, u32[]{:S(2)}) copy-start(f32[1024,256]{1,0:T(8,128)} %constant.46.clone) | copy-start | bytes 3145732
  0.8 8.5 %collective-permute-start = (bf16[8,1,1024]{2,0,1:T(8,128)(2,1)S(1)}, bf16[8,1,1024]{2,0,1:T(8,128)(2,1)S(1)}, u32[]{:S(2)}, u32[]{:S(2)}) collective-permute-start(bf16[8,1,1024]{2,0,1:T(8,128)(2,1)S(1)} %get-tuple-element.11), channel_id=1, source_target_pairs={{0,4},{4,8},{8,12},{12,16},{16,20},{20,24},{24,28},{28,32},{32,36}... | collective-permute-start | bytes 49160 | tf_op jit(solution)/shard_map/ppermute | solution.py:27
  4.3 5.6 %collective-permute-start.1 = (bf16[8,1,1024]{2,0,1:T(8,128)(2,1)S(1)}, bf16[8,1,1024]{2,0,1:T(8,128)(2,1)S(1)}, u32[]{:S(2)}, u32[]{:S(2)}) collective-permute-start(bf16[8,1,1024]{2,0,1:T(8,128)(2,1)S(1)} %get-tuple-element.12), channel_id=1, source_target_pairs={{4,0},{8,4},{12,8},{16,12},{20,16},{24,20},{28,24},{32,28},{36,32}... | collective-permute-start | bytes 49160 | tf_op jit(solution)/shard_map/ppermute | solution.py:28
  13.0 18.5 %all-to-all-start = ((f32[16,1,3072]{2,1,0:T(1,128)}), f32[16,1,3072]{2,1,0:T(1,128)S(1)}, u32[]{:S(2)}, u32[]{:S(2)}) async-start(f32[16,1,3072]{2,1,0:T(1,128)} %reshape.90), calls=%async_computation | async-start | bytes 393216 | tf_op jit(solution)/shard_map/all_to_all | solution.py:42
  31.5 24.3 %all-to-all-start.2 = ((f32[32,1,3072]{2,1,0:T(1,128)}), f32[32,1,3072]{2,1,0:T(1,128)S(1)}, u32[]{:S(2)}, u32[]{:S(2)}) async-start(f32[32,1,3072]{2,1,0:T(1,128)} %reshape.92), calls=%async_computation.2 | async-start | bytes 786432 | tf_op jit(solution)/shard_map/all_to_all | solution.py:42
  56.7 16.4 %all-to-all-start.1 = ((f32[4,192,256]{2,1,0:T(8,128)}), f32[4,192,256]{2,1,0:T(8,128)S(1)}, u32[]{:S(2)}, u32[]{:S(2)}) async-start(f32[4,192,256]{2,1,0:T(8,128)} %broadcast_in_dim.19), calls=%async_computation.1 | async-start | bytes 1572864 | tf_op jit(solution)/shard_map/all_to_all | solution.py:35

commit v20 on v17

--- a/solution.py
+++ b/solution.py
@@ -35,10 +35,11 @@
     every = lax.all_to_all(copies, axis, split_axis=0, concat_axis=0, tiled=True)
     return every.reshape(-1, block.shape[1])
 
-def spread_band(per_band, axis):
+def spread_band(per_band, axis, rows):
     size = lax.axis_size(axis)
-    bands, rows, width = per_band.shape
-    copies = jnp.broadcast_to(per_band[None], (size, bands, rows, width)).reshape(size * bands, rows, width)
+    bands, flat = per_band.shape
+    width = flat // rows
+    copies = jnp.broadcast_to(per_band[None], (size, bands, flat)).reshape(size * bands, flat)
     every = lax.all_to_all(copies, (axis, "win"), split_axis=0, concat_axis=0, tiled=True)
     every = every.reshape(size, bands, rows, width).transpose(0, 2, 1, 3)
     return every.reshape(size * rows, bands * width)
@@ -105,11 +106,11 @@
     whitened = spectra * jnp.concatenate([inverse_amp, inverse_amp], axis=-1)
     bands = lax.axis_size("win")
     whitened = whitened.reshape(local_rows, 2, bands, FREQ_BINS // bands).transpose(2, 0, 1, 3)
-    whitened = whitened.reshape(bands, local_rows, -1)
+    whitened = whitened.reshape(bands, -1)
     windows = bands
-    inverse_count = 1.0 / (windows * whitened.shape[2] // 2)
-    col_set = spread_band(whitened, "cb")
-    row_set = gather_blocks(spread_band(whitened, "cz"), "cx")
+    inverse_count = 1.0 / (windows * (FREQ_BINS // bands))
+    col_set = spread_band(whitened, "cb", local_rows)
+    row_set = gather_blocks(spread_band(whitened, "cz", local_rows), "cx")
     operands = jnp.concatenate([col_set, swapped_parts(col_set, windows)], axis=0)
     product = jnp.einsum("ik,jk->ij", row_set, operands, precision=lax.Precision.HIGH)
     product = (product * inverse_count).astype(jnp.bfloat16)

time: 112 us -> 113 us (level)
  waiting for transfers between devices: 28.3 us -> 30 us
  other arithmetic: 4.47 us -> 3.26 us
    unnamed x8 -> x4, local copies, waits for them, and re-layouts: 2.47 us -> 0.01 us
    all_to_all x1 -> x2, local copies, waits for them, and re-layouts: 0.54 us -> 2.22 us  [spread_band(): lax.all_to_all(copies, (axis, 'win'), split_axis=0, concat_axis=0, tiled=...]
    all_to_all x2, other arithmetic: 2.63 us -> 1.42 us  [spread_band(): lax.all_to_all(copies, (axis, 'win'), split_axis=0, concat_axis=0, tiled=...]
  transfers between devices with their start and end apart: 5 -> 5, of which waited for: 4 -> 4; matrix products, arithmetic and copies ran while one was open for 9% -> 6% of each run, Pallas kernels for 0% -> 0%
where the time goes in v20:
time: 113 us; the launch traced here: 112 us
  blocking collectives  35.3 us (31%)
  starting transfers between devices  30.3 us (27%)
  waiting for transfers between devices  30 us (27%)
  local copies, waits for them, and re-layouts  9.9 us (9%)
  other arithmetic  3.26 us (3%)
  matrix products  2.98 us (3%)
    all_to_all x1, blocking collectives, body(): lax.all_to_all(product, ('cx', 'cz'), split_axis=0, concat_axis=0, tiled=...  35.3 us
    all_to_all x2, starting transfers between devices, spread_band(): lax.all_to_all(copies, (axis, 'win'), split_axis=0, concat_axis=0, tiled=...  20.2 us
    all_to_all x2, waiting for transfers between devices, spread_band(): lax.all_to_all(copies, (axis, 'win'), split_axis=0, concat_axis=0, tiled=...  20.2 us
    all_to_all x1, waiting for transfers between devices, gather_blocks(): lax.all_to_all(copies, axis, split_axis=0, concat_axis=0, tiled=True)  9.24 us
    all_to_all x1, starting transfers between devices, gather_blocks(): lax.all_to_all(copies, axis, split_axis=0, concat_axis=0, tiled=True)  4.29 us
    ppermute x1, starting transfers between devices, with_halo(): before = lax.ppermute(last, CHAN, up)  3.47 us
    ppermute x1, starting transfers between devices, with_halo(): after = lax.ppermute(initial, CHAN, down)  2.35 us
  transfers between devices with their start and end apart: 5, of which 4 were waited for; matrix products, arithmetic and copies ran while one was open for 6% of the time, Pallas kernels for 0%

profile of v20, /device:TPU:72, one launch (start us, length us, event | category | flops | bytes accessed | tf_op | source)
XLA Modules:
  0.0 112.0 jit_solution(14278367858256436036)
XLA Ops:
  0.0 0.8 fusion.24
  0.8 3.5 %collective-permute-start = (bf16[8,1,1024]{2,0,1:T(8,128)(2,1)S(1)}, bf16[8,1,1024]{2,0,1:T(8,128)(2,1)S(1)}, u32[]{:S(2)}, u32[]{:S(2)}) collective-permute-start(bf16[8,1,1024]{2,0,1:T(8,128)(2,1)S(1)} %get-tuple-element.11), channel_id=1, source_target_pairs={{0,4},{4,8},{8,12},{12,16},{16,20},{20,24},{24,28},{28,32},{32,36}... | collective-permute-start | bytes 49160 | tf_op jit(solution)/shard_map/ppermute | solution.py:27
  4.3 2.4 %collective-permute-start.1 = (bf16[8,1,1024]{2,0,1:T(8,128)(2,1)S(1)}, bf16[8,1,1024]{2,0,1:T(8,128)(2,1)S(1)}, u32[]{:S(2)}, u32[]{:S(2)}) collective-permute-start(bf16[8,1,1024]{2,0,1:T(8,128)(2,1)S(1)} %get-tuple-element.12), channel_id=1, source_target_pairs={{4,0},{8,4},{12,8},{16,12},{20,16},{24,20},{28,24},{32,28},{36,32}... | collective-permute-start | bytes 49160 | tf_op jit(solution)/shard_map/ppermute | solution.py:28
  6.7 0.8 compare_select_fusion
  7.6 0.8 gather_fusion
  8.4 0.8 convert_reduce_fusion.1
  9.3 0.6 collective-permute-done.1
  9.9 1.2 %fusion.3 = f32[48,1024]{1,0:T(8,128)S(1)} fusion(bf16[48,1,1024]{2,0,1:T(8,128)(2,1)} %param.5, bf16[8,1,1024]{2,0,1:T(8,128)(2,1)S(1)} %collective-permute-done.1, bf16[8,1,1024]{2,0,1:T(8,128)(2,1)S(1)} %collective-permute-done, f32[48]{0:T(128)S(1)} %broadcast_maximum_fusion, f32[48]{0:T(128)S(1)} %get-tuple-element.14, s32[64]{0:T(128)S(1)} %get-tuple-element.8, ...), kind=kOutput, calls=%fused_computation.7 | convolution fusion | flops 6899712 | bytes 328960 | tf_op jit(solution)/shard_map/cr,rwt->cwt/dot_general | solution.py:94
  11.2 0.4 fusion.25
  12.3 0.9 all_to_all.18
  13.3 10.0 %all-to-all-start = ((f32[16,1,3072]{2,1,0:T(1,128)}), f32[16,1,3072]{2,1,0:T(1,128)S(1)}, u32[]{:S(2)}, u32[]{:S(2)}) async-start(f32[16,1,3072]{2,1,0:T(1,128)} %all_to_all.18), calls=%async_computation | async-start | bytes 393216 | tf_op jit(solution)/shard_map/all_to_all | solution.py:43
  23.3 1.3 %all_to_all.21 = f32[32,1,3072]{2,1,0:T(1,128)} reshape(f32[8,4,3072]{2,1,0:T(4,128)S(1)} %broadcast_in_dim.20) | data formatting | bytes 786432 | tf_op jit(solution)/shard_map/all_to_all | solution.py:43
  24.6 7.2 %all-to-all-done = f32[16,1,3072]{2,1,0:T(1,128)S(1)} async-done(((f32[16,1,3072]{2,1,0:T(1,128)}), f32[16,1,3072]{2,1,0:T(1,128)S(1)}, u32[]{:S(2)}, u32[]{:S(2)}) %all-to-all-start) | async-done | bytes 196640 | tf_op jit(solution)/shard_map/all_to_all | solution.py:43
  31.8 10.2 %all-to-all-start.2 = ((f32[32,1,3072]{2,1,0:T(1,128)}), f32[32,1,3072]{2,1,0:T(1,128)S(1)}, u32[]{:S(2)}, u32[]{:S(2)}) async-start(f32[32,1,3072]{2,1,0:T(1,128)} %all_to_all.21), calls=%async_computation.2 | async-start | bytes 786432 | tf_op jit(solution)/shard_map/all_to_all | solution.py:43
  42.0 0.5 reduce
  43.1 13.0 %all-to-all-done.2 = f32[32,1,3072]{2,1,0:T(1,128)S(1)} async-done(((f32[32,1,3072]{2,1,0:T(1,128)}), f32[32,1,3072]{2,1,0:T(1,128)S(1)}, u32[]{:S(2)}, u32[]{:S(2)}) %all-to-all-start.2) | async-done | bytes 393248 | tf_op jit(solution)/shard_map/all_to_all | solution.py:43
  56.0 0.9 broadcast_in_dim.19
  57.0 4.3 %all-to-all-start.1 = ((f32[4,192,256]{2,1,0:T(8,128)}), f32[4,192,256]{2,1,0:T(8,128)S(1)}, u32[]{:S(2)}, u32[]{:S(2)}) async-start(f32[4,192,256]{2,1,0:T(8,128)} %broadcast_in_dim.19), calls=%async_computation.1 | async-start | bytes 1572864 | tf_op jit(solution)/shard_map/all_to_all | solution.py:35
  61.3 0.9 reduce.1
  63.7 0.5 reshape.83
  64.2 9.2 %all-to-all-done.1 = f32[4,192,256]{2,1,0:T(8,128)S(1)} async-done(((f32[4,192,256]{2,1,0:T(8,128)}), f32[4,192,256]{2,1,0:T(8,128)S(1)}, u32[]{:S(2)}, u32[]{:S(2)}) %all-to-all-start.1) | async-done | bytes 786464 | tf_op jit(solution)/shard_map/all_to_all | solution.py:35
  73.4 1.2 %multiply_convert_fusion = bf16[768,768]{1,0:T(8,128)(2,1)S(1)} fusion(f32[768,256]{1,0:T(8,128)S(1)} %bitcast.41, f32[384,256]{1,0:T(8,128)S(1)} %copy.31, f32[384,256]{1,0:T(8,128)S(1)} %reshape.83), kind=kOutput, calls=%fused_computation.1 | convolution fusion | flops 907345920 | bytes 2752512 | tf_op jit(solution)/shard_map/ik,jk->ij/dot_general | solution.py:115
  74.6 35.3 %all_to_all.28 = bf16[16,48,768]{2,1,0:T(8,128)(2,1)S(1)} all-to-all(bf16[16,48,768]{2,1,0:T(8,128)(2,1)S(1)} %bitcast.40), channel_id=1, replica_groups=mesh['cx'=4,'cz'=4,'cb'=8,'win'=4] {'cx','cz'}, dimensions={0} | all-to-all | bytes 2359296 | tf_op jit(solution)/shard_map/all_to_all | solution.py:118
  110.6 1.4 %broadcast_in_dim_reshape.2 = bf16[1,2,48,6144]{3,2,1,0:T(8,128)(2,1)} reshape(bf16[2,48,16,384]{3,2,1,0:T(8,128)(2,1)S(1)} %bitcast.39) | data formatting | bytes 2359296 | tf_op jit(solution)/shard_map/broadcast_in_dim;reshape | solution.py:121
  (30 shorter events, 3.6 us)
Async XLA Ops:
  0.0 7.6 %copy-start = (s32[512]{0:T(512)S(1)}, s32[512]{0:T(512)}, u32[]{:S(2)}) copy-start(s32[512]{0:T(512)} %param.7) | copy-start | bytes 6148
  0.0 11.1 %copy-start.1 = (f32[1024,256]{1,0:T(8,128)S(1)}, f32[1024,256]{1,0:T(8,128)}, u32[]{:S(2)}) copy-start(f32[1024,256]{1,0:T(8,128)} %constant.46.clone) | copy-start | bytes 3145732
  0.8 8.5 %collective-permute-start = (bf16[8,1,1024]{2,0,1:T(8,128)(2,1)S(1)}, bf16[8,1,1024]{2,0,1:T(8,128)(2,1)S(1)}, u32[]{:S(2)}, u32[]{:S(2)}) collective-permute-start(bf16[8,1,1024]{2,0,1:T(8,128)(2,1)S(1)} %get-tuple-element.11), channel_id=1, source_target_pairs={{0,4},{4,8},{8,12},{12,16},{16,20},{20,24},{24,28},{28,32},{32,36}... | collective-permute-start | bytes 49160 | tf_op jit(solution)/shard_map/ppermute | solution.py:27
  4.3 5.6 %collective-permute-start.1 = (bf16[8,1,1024]{2,0,1:T(8,128)(2,1)S(1)}, bf16[8,1,1024]{2,0,1:T(8,128)(2,1)S(1)}, u32[]{:S(2)}, u32[]{:S(2)}) collective-permute-start(bf16[8,1,1024]{2,0,1:T(8,128)(2,1)S(1)} %get-tuple-element.12), channel_id=1, source_target_pairs={{4,0},{8,4},{12,8},{16,12},{20,16},{24,20},{28,24},{32,28},{36,32}... | collective-permute-start | bytes 49160 | tf_op jit(solution)/shard_map/ppermute | solution.py:28
  13.3 18.5 %all-to-all-start = ((f32[16,1,3072]{2,1,0:T(1,128)}), f32[16,1,3072]{2,1,0:T(1,128)S(1)}, u32[]{:S(2)}, u32[]{:S(2)}) async-start(f32[16,1,3072]{2,1,0:T(1,128)} %all_to_all.18), calls=%async_computation | async-start | bytes 393216 | tf_op jit(solution)/shard_map/all_to_all | solution.py:43
  31.8 24.3 %all-to-all-start.2 = ((f32[32,1,3072]{2,1,0:T(1,128)}), f32[32,1,3072]{2,1,0:T(1,128)S(1)}, u32[]{:S(2)}, u32[]{:S(2)}) async-start(f32[32,1,3072]{2,1,0:T(1,128)} %all_to_all.21), calls=%async_computation.2 | async-start | bytes 786432 | tf_op jit(solution)/shard_map/all_to_all | solution.py:43
  57.0 16.4 %all-to-all-start.1 = ((f32[4,192,256]{2,1,0:T(8,128)}), f32[4,192,256]{2,1,0:T(8,128)S(1)}, u32[]{:S(2)}, u32[]{:S(2)}) async-start(f32[4,192,256]{2,1,0:T(8,128)} %broadcast_in_dim.19), calls=%async_computation.1 | async-start | bytes 1572864 | tf_op jit(solution)/shard_map/all_to_all | solution.py:35

commit v21 on v17

--- a/solution.py
+++ b/solution.py
@@ -109,6 +109,7 @@
     windows = bands
     inverse_count = 1.0 / (windows * whitened.shape[2] // 2)
     col_set = spread_band(whitened, "cb")
+    col_set, whitened = lax.optimization_barrier((col_set, whitened))
     row_set = gather_blocks(spread_band(whitened, "cz"), "cx")
     operands = jnp.concatenate([col_set, swapped_parts(col_set, windows)], axis=0)
     product = jnp.einsum("ik,jk->ij", row_set, operands, precision=lax.Precision.HIGH)

time: 112 us -> 119 us (1.062)
  the two profiles are of different devices: /device:TPU:72 before, /device:TPU:1 now
where the time goes in v21:
time: 119 us
  blocking collectives  80.8 us (68%)
  waiting for transfers between devices  12.6 us (11%)
  starting transfers between devices  9.32 us (8%)
  local copies, waits for them, and re-layouts  8.18 us (7%)
  other arithmetic  4.53 us (4%)
  matrix products  2.98 us (3%)
    all_to_all x2, blocking collectives, spread_band(): lax.all_to_all(copies, (axis, 'win'), split_axis=0, concat_axis=0, tiled=...  47.2 us
    all_to_all x1, blocking collectives, body(): lax.all_to_all(product, ('cx', 'cz'), split_axis=0, concat_axis=0, tiled=...  33.6 us
    all_to_all x1, waiting for transfers between devices, gather_blocks(): lax.all_to_all(copies, axis, split_axis=0, concat_axis=0, tiled=True)  12 us
    ppermute x1, starting transfers between devices, with_halo(): before = lax.ppermute(last, CHAN, up)  4.02 us
    all_to_all x1, starting transfers between devices, gather_blocks(): lax.all_to_all(copies, axis, split_axis=0, concat_axis=0, tiled=True)  4.01 us
    all_to_all x2, other arithmetic, spread_band(): lax.all_to_all(copies, (axis, 'win'), split_axis=0, concat_axis=0, tiled=...  2.7 us
  transfers between devices with their start and end apart: 3, of which 2 were waited for; matrix products, arithmetic and copies ran while one was open for 3% of the time, Pallas kernels for 0%

profile of v21, /device:TPU:1, one launch (start us, length us, event | category | flops | bytes accessed | tf_op | source)
XLA Modules:
  0.0 118.6 jit_solution(6325288696245709)
XLA Ops:
  0.0 0.8 fusion.24
  0.8 4.0 %collective-permute-start = (bf16[8,1,1024]{2,0,1:T(8,128)(2,1)S(1)}, bf16[8,1,1024]{2,0,1:T(8,128)(2,1)S(1)}, u32[]{:S(2)}, u32[]{:S(2)}) collective-permute-start(bf16[8,1,1024]{2,0,1:T(8,128)(2,1)S(1)} %get-tuple-element.15), channel_id=1, source_target_pairs={{0,4},{4,8},{8,12},{12,16},{16,20},{20,24},{24,28},{28,32},{32,36}... | collective-permute-start | bytes 49160 | tf_op jit(solution)/shard_map/ppermute | solution.py:27
  4.9 1.3 %collective-permute-start.1 = (bf16[8,1,1024]{2,0,1:T(8,128)(2,1)S(1)}, bf16[8,1,1024]{2,0,1:T(8,128)(2,1)S(1)}, u32[]{:S(2)}, u32[]{:S(2)}) collective-permute-start(bf16[8,1,1024]{2,0,1:T(8,128)(2,1)S(1)} %get-tuple-element.16), channel_id=1, source_target_pairs={{4,0},{8,4},{12,8},{16,12},{20,16},{24,20},{28,24},{32,28},{36,32}... | collective-permute-start | bytes 49160 | tf_op jit(solution)/shard_map/ppermute | solution.py:28
  6.2 0.8 compare_select_fusion
  7.0 0.8 gather_fusion
  7.9 0.8 convert_reduce_fusion.1
  8.8 0.5 collective-permute-done.1
  9.3 1.2 %fusion.3 = f32[48,1024]{1,0:T(8,128)S(1)} fusion(bf16[48,1,1024]{2,0,1:T(8,128)(2,1)} %param.5, bf16[8,1,1024]{2,0,1:T(8,128)(2,1)S(1)} %collective-permute-done.1, bf16[8,1,1024]{2,0,1:T(8,128)(2,1)S(1)} %collective-permute-done, f32[48]{0:T(128)S(1)} %broadcast_maximum_fusion, f32[48]{0:T(128)S(1)} %get-tuple-element.18, s32[64]{0:T(128)S(1)} %get-tuple-element.12, ...), kind=kOutput, calls=%fused_computation.7 | convolution fusion | flops 6899712 | bytes 328960 | tf_op jit(solution)/shard_map/cr,rwt->cwt/dot_general | solution.py:93
  10.6 0.4 fusion.25
  11.5 0.5 reshape.100
  12.0 27.2 %all_to_all.20 = f32[32,1,3072]{2,1,0:T(1,128)S(1)} all-to-all(f32[32,1,3072]{2,1,0:T(1,128)S(1)} %reshape.100), channel_id=1, replica_groups=mesh['cx'=4,'cz'=4,'cb'=8,'win'=4] {'cb','win'}, dimensions={0} | all-to-all | bytes 786432 | tf_op jit(solution)/shard_map/all_to_all | solution.py:42
  39.2 0.5 broadcast.35
  39.7 1.6 %reduce = f32[32,3072]{1,0:T(8,128)S(1)} reduce(f32[32,1,3072]{2,1,0:T(1,128)S(1)} %all_to_all.20, f32[]{:T(128)} %broadcast.35), dimensions={1}, to_apply=%all_to_all.12.reduce_sub_computation | reduce | bytes 786436 | tf_op jit(solution)/shard_map/all_to_all | solution.py:42
  41.5 0.3 copy.26
  41.8 0.5 reshape.83
  42.6 20.0 %all_to_all.21 = f32[16,1,3072]{2,1,0:T(1,128)S(1)} all-to-all(f32[16,1,3072]{2,1,0:T(1,128)S(1)} %reshape.102), channel_id=1, replica_groups=mesh['cx'=4,'cz'=4,'cb'=8,'win'=4] {'cz','win'}, dimensions={0} | all-to-all | bytes 393216 | tf_op jit(solution)/shard_map/all_to_all | solution.py:42
  62.6 1.1 reduce.1
  64.3 0.9 broadcast_in_dim.20
  65.2 4.0 %all-to-all-start.2 = ((f32[4,192,256]{2,1,0:T(8,128)}), f32[4,192,256]{2,1,0:T(8,128)S(1)}, u32[]{:S(2)}, u32[]{:S(2)}) async-start(f32[4,192,256]{2,1,0:T(8,128)} %broadcast_in_dim.20), calls=%async_computation.2 | async-start | bytes 1572864 | tf_op jit(solution)/shard_map/all_to_all | solution.py:35
  69.7 12.0 %all-to-all-done.2 = f32[4,192,256]{2,1,0:T(8,128)S(1)} async-done(((f32[4,192,256]{2,1,0:T(8,128)}), f32[4,192,256]{2,1,0:T(8,128)S(1)}, u32[]{:S(2)}, u32[]{:S(2)}) %all-to-all-start.2) | async-done | bytes 786464 | tf_op jit(solution)/shard_map/all_to_all | solution.py:35
  81.7 1.2 multiply_convert_fusion
  82.9 33.6 %all_to_all.22 = bf16[16,48,768]{2,1,0:T(8,128)(2,1)S(1)} all-to-all(bf16[16,48,768]{2,1,0:T(8,128)(2,1)S(1)} %bitcast.42), channel_id=1, replica_groups=mesh['cx'=4,'cz'=4,'cb'=8,'win'=4] {'cx','cz'}, dimensions={0} | all-to-all | bytes 2359296 | tf_op jit(solution)/shard_map/all_to_all | solution.py:118
  116.8 0.4 copy.33
  117.2 1.4 %broadcast_in_dim_reshape.2 = bf16[1,2,48,6144]{3,2,1,0:T(8,128)(2,1)} reshape(bf16[2,48,16,384]{3,2,1,0:T(8,128)(2,1)S(1)} %bitcast.41) | data formatting | bytes 2359296 | tf_op jit(solution)/shard_map/broadcast_in_dim;reshape | solution.py:121
  (29 shorter events, 2.4 us)
Async XLA Ops:
  0.0 7.0 %copy-start = (s32[512]{0:T(512)S(1)}, s32[512]{0:T(512)}, u32[]{:S(2)}) copy-start(s32[512]{0:T(512)} %param.7) | copy-start | bytes 6148
  0.0 10.5 %copy-start.1 = (f32[1024,256]{1,0:T(8,128)S(1)}, f32[1024,256]{1,0:T(8,128)}, u32[]{:S(2)}) copy-start(f32[1024,256]{1,0:T(8,128)} %constant.46.clone) | copy-start | bytes 3145732
  0.8 8.0 %collective-permute-start = (bf16[8,1,1024]{2,0,1:T(8,128)(2,1)S(1)}, bf16[8,1,1024]{2,0,1:T(8,128)(2,1)S(1)}, u32[]{:S(2)}, u32[]{:S(2)}) collective-permute-start(bf16[8,1,1024]{2,0,1:T(8,128)(2,1)S(1)} %get-tuple-element.15), channel_id=1, source_target_pairs={{0,4},{4,8},{8,12},{12,16},{16,20},{20,24},{24,28},{28,32},{32,36}... | collective-permute-start | bytes 49160 | tf_op jit(solution)/shard_map/ppermute | solution.py:27
  4.9 4.5 %collective-permute-start.1 = (bf16[8,1,1024]{2,0,1:T(8,128)(2,1)S(1)}, bf16[8,1,1024]{2,0,1:T(8,128)(2,1)S(1)}, u32[]{:S(2)}, u32[]{:S(2)}) collective-permute-start(bf16[8,1,1024]{2,0,1:T(8,128)(2,1)S(1)} %get-tuple-element.16), channel_id=1, source_target_pairs={{4,0},{8,4},{12,8},{16,12},{20,16},{24,20},{28,24},{32,28},{36,32}... | collective-permute-start | bytes 49160 | tf_op jit(solution)/shard_map/ppermute | solution.py:28
  65.2 16.5 %all-to-all-start.2 = ((f32[4,192,256]{2,1,0:T(8,128)}), f32[4,192,256]{2,1,0:T(8,128)S(1)}, u32[]{:S(2)}, u32[]{:S(2)}) async-start(f32[4,192,256]{2,1,0:T(8,128)} %broadcast_in_dim.20), calls=%async_computation.2 | async-start | bytes 1572864 | tf_op jit(solution)/shard_map/all_to_all | solution.py:35

commit v22 on v13

--- a/solution.py
+++ b/solution.py
@@ -87,10 +87,7 @@
     near_segs = lax.dynamic_slice_in_dim(
         seg_padded, device * local_rows, local_rows + 2 * MOST_REACH
     )
-    segment_ids = jnp.arange(dead.shape[0], dtype=jnp.int32)
-    dead_near = jnp.sum(
-        jnp.where(near_segs[:, None] == segment_ids[None, :], dead[None, :], 0), axis=1
-    )
+    dead_near = jnp.where(near_segs >= 0, dead[jnp.clip(near_segs, 0, dead.shape[0] - 1)], 0)
     alive_near = jnp.where(near_segs >= 0, 1 - dead_near, 0)
     own_segs = near_segs[MOST_REACH : MOST_REACH + local_rows]
     alive_own = alive_near[MOST_REACH : MOST_REACH + local_rows].astype(jnp.float32)
@@ -111,7 +108,7 @@
     filtered = alive_own[:, None, None] * (
         strain.astype(jnp.float32) - neighbor_sums / counts[:, None, None]
     )
-    spectra = jnp.einsum("cwt,tk->cwk", filtered, fourier, precision=lax.Precision.HIGHEST)
+    spectra = jnp.einsum("cwt,tk->cwk", filtered, fourier, precision=lax.Precision.HIGH)
     power_bins = spectra[..., :FREQ_BINS] ** 2 + spectra[..., FREQ_BINS:] ** 2
     smoothed = jnp.einsum(
         "cwk,kj->cwj", power_bins, smoothing_table(), precision=lax.Precision.HIGHEST
@@ -126,7 +123,7 @@
     col_set = spread_band(whitened, "cb")
     row_set = gather_by_permutes(spread_band(whitened, "cz"), "cx")
     operands = jnp.concatenate([col_set, swapped_parts(col_set, windows)], axis=0)
-    product = jnp.einsum("ik,jk->ij", row_set, operands, precision=lax.Precision.HIGHEST)
+    product = jnp.einsum("ik,jk->ij", row_set, operands, precision=lax.Precision.HIGH)
     product = (product * inverse_count).astype(jnp.bfloat16)
     product = product.reshape(group_x * group_z, local_rows, operands.shape[0])
     mine = lax.all_to_all(product, ("cx", "cz"), split_axis=0, concat_axis=0, tiled=True)

time: 113 us -> 112 us (level)
    unnamed x13 -> x15, local copies, waits for them, and re-layouts: 6.6 us -> 6.65 us
  transfers between devices with their start and end apart: 6 -> 6, of which waited for: 3 -> 3; matrix products, arithmetic and copies ran while one was open for 9% -> 8% of each run, Pallas kernels for 0% -> 0%
where the time goes in v22:
time: 112 us
  blocking collectives  58.9 us (53%)
  starting transfers between devices  21.4 us (19%)
  local copies, waits for them, and re-layouts  14.1 us (13%)
  waiting for transfers between devices  8.38 us (7%)
  other arithmetic  4.51 us (4%)
  matrix products  4.12 us (4%)
    all_to_all x1, blocking collectives, body(): lax.all_to_all(product, ('cx', 'cz'), split_axis=0, concat_axis=0, tiled=...  37 us
    all_to_all x1, blocking collectives, spread_band(): lax.all_to_all(copies, (axis, 'win'), split_axis=0, concat_axis=0, tiled=...  21.9 us
    ppermute x3, starting transfers between devices, gather_by_permutes(): pieces.append(lax.ppermute(block, axis, pairs))  10.4 us
    ppermute x3, waiting for transfers between devices, gather_by_permutes(): pieces.append(lax.ppermute(block, axis, pairs))  6.71 us
    unnamed x15, local copies, waits for them, and re-layouts  6.65 us
    all_to_all x1, starting transfers between devices, spread_band(): lax.all_to_all(copies, (axis, 'win'), split_axis=0, concat_axis=0, tiled=...  6.21 us
    ppermute x1, starting transfers between devices, with_halo(): before = lax.ppermute(last, CHAN, up)  3.47 us
    all_to_all x2, other arithmetic, spread_band(): lax.all_to_all(copies, (axis, 'win'), split_axis=0, concat_axis=0, tiled=...  2.68 us
  transfers between devices with their start and end apart: 6, of which 3 were waited for; matrix products, arithmetic and copies ran while one was open for 8% of the time, Pallas kernels for 0%

profile of v22, /device:TPU:64, one launch (start us, length us, event | category | flops | bytes accessed | tf_op | source)
XLA Modules:
  0.0 111.6 jit_solution(3909972038880853252)
XLA Ops:
  0.0 0.8 fusion.26
  0.8 3.5 %collective-permute-start = (bf16[8,1,1024]{2,0,1:T(8,128)(2,1)S(1)}, bf16[8,1,1024]{2,0,1:T(8,128)(2,1)S(1)}, u32[]{:S(2)}, u32[]{:S(2)}) collective-permute-start(bf16[8,1,1024]{2,0,1:T(8,128)(2,1)S(1)} %get-tuple-element.11), channel_id=1, source_target_pairs={{0,4},{4,8},{8,12},{12,16},{16,20},{20,24},{24,28},{28,32},{32,36}... | collective-permute-start | bytes 49160 | tf_op jit(solution)/shard_map/ppermute | solution.py:27
  4.3 1.3 %collective-permute-start.1 = (bf16[8,1,1024]{2,0,1:T(8,128)(2,1)S(1)}, bf16[8,1,1024]{2,0,1:T(8,128)(2,1)S(1)}, u32[]{:S(2)}, u32[]{:S(2)}) collective-permute-start(bf16[8,1,1024]{2,0,1:T(8,128)(2,1)S(1)} %get-tuple-element.12), channel_id=1, source_target_pairs={{4,0},{8,4},{12,8},{16,12},{20,16},{24,20},{28,24},{32,28},{36,32}... | collective-permute-start | bytes 49160 | tf_op jit(solution)/shard_map/ppermute | solution.py:28
  5.6 0.8 compare_select_fusion
  6.5 0.8 gather_fusion
  7.4 0.8 convert_reduce_fusion.1
  8.3 1.7 %collective-permute-done.1 = bf16[8,1,1024]{2,0,1:T(8,128)(2,1)S(1)} collective-permute-done((bf16[8,1,1024]{2,0,1:T(8,128)(2,1)S(1)}, bf16[8,1,1024]{2,0,1:T(8,128)(2,1)S(1)}, u32[]{:S(2)}, u32[]{:S(2)}) %collective-permute-start.1) | collective-permute-done | bytes 16416 | tf_op jit(solution)/shard_map/ppermute | solution.py:28
  9.9 1.2 %fusion.3 = f32[48,1024]{1,0:T(8,128)S(1)} fusion(bf16[48,1,1024]{2,0,1:T(8,128)(2,1)} %param.5, bf16[8,1,1024]{2,0,1:T(8,128)(2,1)S(1)} %collective-permute-done.1, bf16[8,1,1024]{2,0,1:T(8,128)(2,1)S(1)} %collective-permute-done, f32[48]{0:T(128)S(1)} %broadcast_maximum_fusion, f32[48]{0:T(128)S(1)} %get-tuple-element.14, s32[64]{0:T(128)S(1)} %get-tuple-element.8, ...), kind=kOutput, calls=%fused_computation.7 | convolution fusion | flops 6899712 | bytes 328960 | tf_op jit(solution)/shard_map/cr,rwt->cwt/dot_general | solution.py:105
  12.3 21.9 %all_to_all.15 = f32[16,1,3072]{2,1,0:T(1,128)S(1)} all-to-all(f32[16,1,3072]{2,1,0:T(1,128)S(1)} %reshape.95), channel_id=1, replica_groups=mesh['cx'=4,'cz'=4,'cb'=8,'win'=4] {'cz','win'}, dimensions={0} | all-to-all | bytes 393216 | tf_op jit(solution)/shard_map/all_to_all | solution.py:42
  34.8 1.1 reduce.1
  36.5 4.6 %collective-permute-start.2 = (f32[192,256]{1,0:T(8,128)S(1)}, f32[192,256]{1,0:T(8,128)S(1)}, u32[]{:S(2)}, u32[]{:S(2)}) collective-permute-start(f32[192,256]{1,0:T(8,128)S(1)} %reshape.77), channel_id=1, source_target_pairs={{0,384},{128,0},{256,128},{384,256},{1,385},{129,1},{257,129},{385... | collective-permute-start | bytes 589832 | tf_op jit(solution)/shard_map/ppermute | solution.py:52
  41.2 1.2 %reshape.93 = f32[32,1,3072]{2,1,0:T(1,128)} reshape(f32[32,48,64]{2,1,0:T(8,128)S(1)} %bitcast.46) | data formatting | bytes 786432
  42.4 6.2 %all-to-all-start.1 = ((f32[32,1,3072]{2,1,0:T(1,128)}), f32[32,1,3072]{2,1,0:T(1,128)S(1)}, u32[]{:S(2)}, u32[]{:S(2)}) async-start(f32[32,1,3072]{2,1,0:T(1,128)} %reshape.93), calls=%async_computation.1 | async-start | bytes 786432 | tf_op jit(solution)/shard_map/all_to_all | solution.py:42
  48.6 3.0 %collective-permute-start.3 = (f32[192,256]{1,0:T(8,128)S(1)}, f32[192,256]{1,0:T(8,128)S(1)}, u32[]{:S(2)}, u32[]{:S(2)}) collective-permute-start(f32[192,256]{1,0:T(8,128)S(1)} %reshape.77), channel_id=1, source_target_pairs={{0,256},{128,384},{256,0},{384,128},{1,257},{129,385},{257,1},{385... | collective-permute-start | bytes 589832 | tf_op jit(solution)/shard_map/ppermute | solution.py:52
  51.6 2.8 %collective-permute-start.4 = (f32[192,256]{1,0:T(8,128)S(1)}, f32[192,256]{1,0:T(8,128)S(1)}, u32[]{:S(2)}, u32[]{:S(2)}) collective-permute-start(f32[192,256]{1,0:T(8,128)S(1)} %reshape.77), channel_id=1, source_target_pairs={{0,128},{128,256},{256,384},{384,0},{1,129},{129,257},{257,385},{3... | collective-permute-start | bytes 589832 | tf_op jit(solution)/shard_map/ppermute | solution.py:52
  55.1 0.7 constant_dynamic-update-slice_fusion.6
  55.8 4.0 %collective-permute-done.3 = f32[192,256]{1,0:T(8,128)S(1)} collective-permute-done((f32[192,256]{1,0:T(8,128)S(1)}, f32[192,256]{1,0:T(8,128)S(1)}, u32[]{:S(2)}, u32[]{:S(2)}) %collective-permute-start.3) | collective-permute-done | bytes 196640 | tf_op jit(solution)/shard_map/ppermute | solution.py:52
  60.5 2.7 %collective-permute-done.4 = f32[192,256]{1,0:T(8,128)S(1)} collective-permute-done((f32[192,256]{1,0:T(8,128)S(1)}, f32[192,256]{1,0:T(8,128)S(1)}, u32[]{:S(2)}, u32[]{:S(2)}) %collective-permute-start.4) | collective-permute-done | bytes 196640 | tf_op jit(solution)/shard_map/ppermute | solution.py:52
  63.9 0.7 constant_dynamic-update-slice_fusion.3
  65.3 0.7 constant_dynamic-update-slice_fusion.1
  66.7 1.6 %reduce = f32[32,3072]{1,0:T(8,128)S(1)} reduce(f32[32,1,3072]{2,1,0:T(1,128)S(1)} %all-to-all-done.1, f32[]{:T(128)} %broadcast.35), dimensions={1}, to_apply=%all_to_all.10.reduce_sub_computation | reduce | bytes 786436 | tf_op jit(solution)/shard_map/all_to_all | solution.py:42
  70.2 2.3 %multiply_convert_fusion = bf16[768,768]{1,0:T(8,128)(2,1)S(1)} fusion(f32[384,256]{1,0:T(8,128)S(1)} %copy.30, f32[384,256]{1,0:T(8,128)S(1)} %reshape.80, f32[1536,256]{1,0:T(8,128)} %constant_dynamic-update-slice_fusion, s32[]{:T(128)S(6)} %select_n.28), kind=kOutput, calls=%fused_computation.1 | convolution fusion | flops 907345920 | bytes 2752516 | tf_op jit(solution)/shard_map/ik,jk->ij/dot_general | solution.py:126
  72.5 37.0 %all_to_all.16 = bf16[16,48,768]{2,1,0:T(8,128)(2,1)S(1)} all-to-all(bf16[16,48,768]{2,1,0:T(8,128)(2,1)S(1)} %bitcast.44), channel_id=1, replica_groups=mesh['cx'=4,'cz'=4,'cb'=8,'win'=4] {'cx','cz'}, dimensions={0} | all-to-all | bytes 2359296 | tf_op jit(solution)/shard_map/all_to_all | solution.py:129
  110.2 1.4 %broadcast_in_dim_reshape.2 = bf16[1,2,48,6144]{3,2,1,0:T(8,128)(2,1)} reshape(bf16[2,48,16,384]{3,2,1,0:T(8,128)(2,1)S(1)} %bitcast.45) | data formatting | bytes 2359296 | tf_op jit(solution)/shard_map/broadcast_in_dim;reshape | solution.py:132
  (41 shorter events, 8.5 us)
Async XLA Ops:
  0.0 6.5 %copy-start = (s32[512]{0:T(512)S(1)}, s32[512]{0:T(512)}, u32[]{:S(2)}) copy-start(s32[512]{0:T(512)} %param.7) | copy-start | bytes 6148
  0.0 11.1 %copy-start.1 = (f32[1024,256]{1,0:T(8,128)S(1)}, f32[1024,256]{1,0:T(8,128)}, u32[]{:S(2)}) copy-start(f32[1024,256]{1,0:T(8,128)} %constant.60.clone) | copy-start | bytes 3145732
  0.8 7.4 %collective-permute-start = (bf16[8,1,1024]{2,0,1:T(8,128)(2,1)S(1)}, bf16[8,1,1024]{2,0,1:T(8,128)(2,1)S(1)}, u32[]{:S(2)}, u32[]{:S(2)}) collective-permute-start(bf16[8,1,1024]{2,0,1:T(8,128)(2,1)S(1)} %get-tuple-element.11), channel_id=1, source_target_pairs={{0,4},{4,8},{8,12},{12,16},{16,20},{20,24},{24,28},{28,32},{32,36}... | collective-permute-start | bytes 49160 | tf_op jit(solution)/shard_map/ppermute | solution.py:27
  4.3 5.6 %collective-permute-start.1 = (bf16[8,1,1024]{2,0,1:T(8,128)(2,1)S(1)}, bf16[8,1,1024]{2,0,1:T(8,128)(2,1)S(1)}, u32[]{:S(2)}, u32[]{:S(2)}) collective-permute-start(bf16[8,1,1024]{2,0,1:T(8,128)(2,1)S(1)} %get-tuple-element.12), channel_id=1, source_target_pairs={{4,0},{8,4},{12,8},{16,12},{20,16},{24,20},{28,24},{32,28},{36,32}... | collective-permute-start | bytes 49160 | tf_op jit(solution)/shard_map/ppermute | solution.py:28
  36.5 18.7 %collective-permute-start.2 = (f32[192,256]{1,0:T(8,128)S(1)}, f32[192,256]{1,0:T(8,128)S(1)}, u32[]{:S(2)}, u32[]{:S(2)}) collective-permute-start(f32[192,256]{1,0:T(8,128)S(1)} %reshape.77), channel_id=1, source_target_pairs={{0,384},{128,0},{256,128},{384,256},{1,385},{129,1},{257,129},{385... | collective-permute-start | bytes 589832 | tf_op jit(solution)/shard_map/ppermute | solution.py:52
  42.4 24.3 %all-to-all-start.1 = ((f32[32,1,3072]{2,1,0:T(1,128)}), f32[32,1,3072]{2,1,0:T(1,128)S(1)}, u32[]{:S(2)}, u32[]{:S(2)}) async-start(f32[32,1,3072]{2,1,0:T(1,128)} %reshape.93), calls=%async_computation.1 | async-start | bytes 786432 | tf_op jit(solution)/shard_map/all_to_all | solution.py:42
  48.6 11.1 %collective-permute-start.3 = (f32[192,256]{1,0:T(8,128)S(1)}, f32[192,256]{1,0:T(8,128)S(1)}, u32[]{:S(2)}, u32[]{:S(2)}) collective-permute-start(f32[192,256]{1,0:T(8,128)S(1)} %reshape.77), channel_id=1, source_target_pairs={{0,256},{128,384},{256,0},{384,128},{1,257},{129,385},{257,1},{385... | collective-permute-start | bytes 589832 | tf_op jit(solution)/shard_map/ppermute | solution.py:52
  51.6 11.6 %collective-permute-start.4 = (f32[192,256]{1,0:T(8,128)S(1)}, f32[192,256]{1,0:T(8,128)S(1)}, u32[]{:S(2)}, u32[]{:S(2)}) collective-permute-start(f32[192,256]{1,0:T(8,128)S(1)} %reshape.77), channel_id=1, source_target_pairs={{0,128},{128,256},{256,384},{384,0},{1,129},{129,257},{257,385},{3... | collective-permute-start | bytes 589832 | tf_op jit(solution)/shard_map/ppermute | solution.py:52
